TPU v7x, 128 devices: a whole 4x4x4 slice. The times are simulated.
128 devices in a mesh: tsink: 8 (over x, z_lo), mom: 16 (over y, z_hi, core).
Axes of the slice: x: 4, y: 4, z: 4 (z_hi: 2, z_lo: 2; z = z_hi * 2 + z_lo), core: 2. Of those that a mesh axis runs over, the one named last changes fastest.
Arguments:
- perambulators: bfloat16 [8, 4, 1024, 1024], P('tsink'), may hold values from -0.1875 to 0.1875
- elementals: bfloat16 [8, 16, 1024, 1024], P('tsink', 'mom'), may hold values from -6 to 6
- src_times: int32 [4], replicated, may hold values from 0 to 7, as said below
- diagrams: int32 [128, 2], replicated, may hold values from 0 to 15
Outputs:
- meson_blocks: bfloat16 [8, 16, 1024, 1024], P('tsink', 'mom')
- correlators: float32 [128, 8], P('mom', 'tsink')
Inputs may be any that keep to these rules, and one draw needn't show every extreme that they name: `src_times`: distinct time slices; the first and the last time slice are always among them.
All inputs are finite; a program needn't handle non-finite values.
Results may differ from a plain program's by a relative error of at most 0.0055.
Values may be sent and summed in bfloat16 or wider, within the bound.
No kernel may reach another device: no remote copies, remote signals or barrier semaphores. Data moves between devices by JAX's collectives and lax.ppermute only.
A program may use at most 192 MiB of HBM per device.

v0:
```python
import numpy as np
import jax
import jax.numpy as jnp
from jax import lax
from jax.sharding import PartitionSpec as P

NSRC = 4


def shifted(block, offset, n_t):
    pairs = [(t, (t + offset) % n_t) for t in range(n_t)]
    return lax.ppermute(block, "tsink", pairs)


def swapped(block, n_t):
    return lax.ppermute(block, "tsink", [(t, t ^ 1) for t in range(n_t)])


def source_pieces(own_elemental, src_times):
    n_t = lax.axis_size("tsink")
    order = own_elemental.shape[0]
    rows = order // n_t
    half = rows // 2
    quarter = half // 2
    pieces = own_elemental.reshape(n_t, rows, order)
    received = lax.all_to_all(pieces, "tsink", 0, 0)
    own = received[src_times]
    t = lax.axis_index("tsink")
    step = 2
    partner = swapped(own, n_t)
    from_left = shifted(own, step, n_t)
    from_right = shifted(own, -step, n_t)
    to_right = shifted(jnp.stack([from_left[:, :half], partner[:, :half]]), step, n_t)
    to_left = shifted(jnp.stack([from_right[:, half:], partner[:, :half]]), -step, n_t)
    far = jnp.concatenate([to_right[0], to_left[0]], axis=1)
    partner_b = swapped(jnp.stack([from_left[:, half:], from_right[:, half:]]), n_t)
    partner_left_a = to_right[1]
    partner_right_a = to_left[1]
    partner_far_a = jnp.concatenate(
        [
            shifted(partner_left_a[:, :quarter], step, n_t),
            shifted(partner_right_a[:, quarter:], -step, n_t),
        ],
        axis=1,
    )
    partner_far_b = swapped(far[:, half:], n_t)
    return [
        (t, own),
        (t ^ 1, partner),
        ((t - step) % n_t, from_left),
        ((t + step) % n_t, from_right),
        ((t + 2 * step) % n_t, far),
        ((t - step) % n_t ^ 1, jnp.concatenate([partner_left_a, partner_b[0]], axis=1)),
        ((t + step) % n_t ^ 1, jnp.concatenate([partner_right_a, partner_b[1]], axis=1)),
        ((t + 2 * step) % n_t ^ 1, jnp.concatenate([partner_far_a, partner_far_b], axis=1)),
    ]


def body(perambulators, elementals, src_times, diagrams):
    propagators = perambulators[0]
    own_elemental = elementals[0, 0]
    block_order = propagators.shape[1]
    pieces = source_pieces(own_elemental, src_times)
    rows = pieces[0][1].shape[1]
    halves = jnp.zeros((NSRC, block_order, block_order), jnp.bfloat16)
    for origin, piece in pieces:
        block = jnp.einsum(
            "sik,sjk->sij", piece, propagators, preferred_element_type=jnp.float32
        ).astype(jnp.bfloat16)
        halves = lax.dynamic_update_slice_in_dim(halves, block, origin * rows, 1)
    summed = jnp.zeros((block_order, block_order), jnp.float32)
    for source in range(NSRC):
        summed = summed + jnp.dot(
            propagators[source], halves[source], preferred_element_type=jnp.float32
        )
    meson = summed.astype(jnp.bfloat16)

    n_m = lax.axis_size("mom")
    width = 128
    n_b = block_order // width
    grid = meson.reshape(n_b, width, n_b, width).transpose(0, 2, 1, 3).reshape(n_b * n_b, width, width)
    pairs = [(row, col) for col in range(n_b) for row in range(col + 1)]
    upper = grid[np.array([row * n_b + col for row, col in pairs])]
    upper_t = jnp.swapaxes(grid[np.array([col * n_b + row for row, col in pairs])], 1, 2)
    row_index = lax.broadcasted_iota(jnp.int32, (width, width), 0)
    col_index = lax.broadcasted_iota(jnp.int32, (width, width), 1)
    triangle = jnp.where(row_index < col_index, 1.0, jnp.where(row_index == col_index, 0.5, 0.0))
    on_diagonal = np.array([row == col for row, col in pairs])[:, None, None]
    weight = jnp.where(on_diagonal, triangle[None], 1.0).astype(jnp.bfloat16)
    upper = (upper * weight).reshape(-1, width)
    upper_t = upper_t.reshape(-1, width)
    share = upper.shape[0] // n_m
    slices = jnp.concatenate(
        [upper.reshape(n_m, share, width), upper_t.reshape(n_m, share, width)], axis=1
    )
    received = lax.all_to_all(slices, "mom", 0, 0)
    own_rows = received[:, :share].reshape(n_m, share * width)
    own_cols = received[:, share:].reshape(n_m, share * width)
    partial = lax.dot_general(
        own_rows, own_cols, (((1,), (1,)), ((), ())), preferred_element_type=jnp.float32
    )
    partial = partial + partial.T
    per_diagram = partial[diagrams[:, 0], diagrams[:, 1]]
    spread = lax.all_to_all(per_diagram.reshape(n_m, -1), "mom", 0, 0)
    correlators = (jnp.sum(spread, axis=0) / block_order)[:, None]
    return (meson[None, None], correlators)


def solution(mesh):
    in_specs = (P("tsink", None, None, None), P("tsink", "mom", None, None), P(), P())
    out_specs = (P("tsink", "mom", None, None), P("mom", "tsink"))
    return jax.shard_map(body, mesh=mesh, in_specs=in_specs, out_specs=out_specs, check_vma=False)
```

profile of v0, /device:TPU:1, one launch (start us, length us, event | category | flops | bytes accessed | tf_op | source)
XLA Modules:
  0.0 196.4 jit_solution(8918771213711876063)
XLA Ops:
  0.7 6.3 %all-to-all-start = ((bf16[8,128,1024]{2,1,0:T(8,128)(2,1)}), bf16[8,128,1024]{2,1,0:T(8,128)(2,1)S(1)}, u32[]{:S(2)}, u32[]{:S(2)}) async-start(bf16[8,128,1024]{2,1,0:T(8,128)(2,1)} %bitcast.135), calls=%async_computation | async-start | bytes 4194304 | tf_op jit(solution)/shard_map/all_to_all | solution.py:26
  7.0 30.6 %all-to-all-done = bf16[8,128,1024]{2,1,0:T(8,128)(2,1)S(1)} async-done(((bf16[8,128,1024]{2,1,0:T(8,128)(2,1)}), bf16[8,128,1024]{2,1,0:T(8,128)(2,1)S(1)}, u32[]{:S(2)}, u32[]{:S(2)}) %all-to-all-start) | async-done | bytes 2097184 | tf_op jit(solution)/shard_map/all_to_all | solution.py:26
  37.6 0.6 gather_fusion
  38.6 1.4 collective-permute-start.1
  40.2 1.1 broadcast_in_dim.59
  41.3 2.2 %copy-done = bf16[1,4,1024,1024]{3,2,1,0:T(8,128)(2,1)S(1)} copy-done((bf16[1,4,1024,1024]{3,2,1,0:T(8,128)(2,1)S(1)}, bf16[1,4,1024,1024]{3,2,1,0:T(8,128)(2,1)}, u32[]{:S(2)}) %copy-start) | copy-done | bytes 8388632
  43.5 3.0 %fusion.73 = bf16[4,1024,1024]{2,1,0:T(8,128)(2,1)S(1)} fusion(bf16[4,1024,1024]{2,1,0:T(8,128)(2,1)S(1)} %broadcast_in_dim.59, s32[]{:T(128)S(6)} %select_n.84, bf16[4,128,1024]{2,1,0:T(8,128)(2,1)S(1)} %gather_fusion, bf16[1,4,1024,1024]{3,2,1,0:T(8,128)(2,1)S(1)} %copy-done), kind=kOutput, calls=%fused_computation.54 | convolution fusion | flops 1074266112 | bytes 10485764 | tf_op jit(solution)/shard_map/sik,sjk->sij/dot_general | solution.py:67
  46.5 15.0 %collective-permute-done.2 = bf16[4,128,1024]{2,1,0:T(8,128)(2,1)S(1)} collective-permute-done((bf16[4,128,1024]{2,1,0:T(8,128)(2,1)S(1)}, bf16[4,128,1024]{2,1,0:T(8,128)(2,1)S(1)}, u32[]{:S(2)}, u32[]{:S(2)}) %collective-permute-start.2) | collective-permute-done | bytes 1048608 | tf_op jit(solution)/shard_map/ppermute | solution.py:12
  61.5 1.6 collective-permute-done.1
  63.2 0.2 pad_maximum_fusion.3
  63.5 1.3 collective-permute-start.4
  64.7 0.2 collective-permute-start.3
  65.0 3.0 %fusion.70 = bf16[4,1024,1024]{2,1,0:T(8,128)(2,1)S(1)} fusion(bf16[4,1024,1024]{2,1,0:T(8,128)(2,1)S(1)} %fusion.73, s32[]{:T(128)S(6)} %select_n.85, bf16[4,128,1024]{2,1,0:T(8,128)(2,1)S(1)} %collective-permute-done, bf16[1,4,1024,1024]{3,2,1,0:T(8,128)(2,1)S(1)} %copy-done), kind=kOutput, calls=%fused_computation.53 | convolution fusion | flops 1074266112 | bytes 10485764 | tf_op jit(solution)/shard_map/sik,sjk->sij/dot_general | solution.py:67
  68.0 2.9 %fusion.67 = bf16[4,1024,1024]{2,1,0:T(8,128)(2,1)S(1)} fusion(bf16[4,1024,1024]{2,1,0:T(8,128)(2,1)S(1)} %fusion.70, s32[]{:T(128)S(6)} %select_n.87, bf16[4,128,1024]{2,1,0:T(8,128)(2,1)S(1)} %collective-permute-done.1, bf16[1,4,1024,1024]{3,2,1,0:T(8,128)(2,1)S(1)} %copy-done), kind=kOutput, calls=%fused_computation.52 | convolution fusion | flops 1074266112 | bytes 10485764 | tf_op jit(solution)/shard_map/sik,sjk->sij/dot_general | solution.py:67
  70.9 3.0 %fusion.64 = bf16[4,1024,1024]{2,1,0:T(8,128)(2,1)S(1)} fusion(bf16[4,1024,1024]{2,1,0:T(8,128)(2,1)S(1)} %fusion.67, s32[]{:T(128)S(6)} %select_n.89, bf16[4,128,1024]{2,1,0:T(8,128)(2,1)S(1)} %collective-permute-done.2, bf16[1,4,1024,1024]{3,2,1,0:T(8,128)(2,1)S(1)} %copy-done), kind=kOutput, calls=%fused_computation.51 | convolution fusion | flops 1074266112 | bytes 10485764 | tf_op jit(solution)/shard_map/sik,sjk->sij/dot_general | solution.py:67
  73.9 13.9 %collective-permute-done.3 = bf16[2,4,64,1024]{3,2,1,0:T(8,128)(2,1)} collective-permute-done((bf16[2,4,64,1024]{3,2,1,0:T(8,128)(2,1)S(1)}, bf16[2,4,64,1024]{3,2,1,0:T(8,128)(2,1)}, u32[]{:S(2)}, u32[]{:S(2)}) %collective-permute-start.3) | collective-permute-done | bytes 1048608 | tf_op jit(solution)/shard_map/ppermute | solution.py:12
  87.8 1.3 slice_bitcast_fusion.14
  89.1 0.3 collective-permute-start.6
  89.4 1.3 slice_bitcast_fusion.11
  90.7 2.7 %collective-permute-start.7 = (bf16[4,32,1024]{2,1,0:T(8,128)(2,1)S(1)}, bf16[4,32,1024]{2,1,0:T(8,128)(2,1)S(1)}, u32[]{:S(2)}, u32[]{:S(2)}) collective-permute-start(bf16[4,32,1024]{2,1,0:T(8,128)(2,1)S(1)} %slice.121), channel_id=1, source_target_pairs={{0,96},{16,112},{32,0},{48,16},{64,32},{80,48},{96,64},{112,80},{1... | collective-permute-start | bytes 786440 | tf_op jit(solution)/shard_map/ppermute | solution.py:12
  93.4 2.9 %fusion.61 = bf16[4,1024,1024]{2,1,0:T(8,128)(2,1)S(1)} fusion(bf16[4,1024,1024]{2,1,0:T(8,128)(2,1)S(1)} %fusion.64, s32[]{:T(128)S(6)} %select_n.91, bf16[1,4,1024,1024]{3,2,1,0:T(8,128)(2,1)S(1)} %copy-done, bf16[4,64,1024]{2,1,0:T(8,128)(2,1)S(1)} %get-tuple-element.11, bf16[4,64,1024]{2,1,0:T(8,128)(2,1)S(1)} %get-tuple-element.15), kind=kOutput, calls=%fused_computation.50 | convolution fusion | flops 1076363264 | bytes 10485764 | tf_op jit(solution)/shard_map/sik,sjk->sij/dot_general | solution.py:67
  96.4 2.9 %fusion.58 = bf16[4,1024,1024]{2,1,0:T(8,128)(2,1)S(1)} fusion(bf16[4,1024,1024]{2,1,0:T(8,128)(2,1)S(1)} %fusion.61, s32[]{:T(128)S(6)} %select_n.92, bf16[1,4,1024,1024]{3,2,1,0:T(8,128)(2,1)S(1)} %copy-done, bf16[4,64,1024]{2,1,0:T(8,128)(2,1)S(1)} %get-tuple-element.13, bf16[4,64,1024]{2,1,0:T(8,128)(2,1)S(1)} %get-tuple-element.14), kind=kOutput, calls=%fused_computation.49 | convolution fusion | flops 1076363264 | bytes 10485764 | tf_op jit(solution)/shard_map/sik,sjk->sij/dot_general | solution.py:67
  99.4 2.9 %fusion.55 = bf16[4,1024,1024]{2,1,0:T(8,128)(2,1)S(1)} fusion(bf16[4,1024,1024]{2,1,0:T(8,128)(2,1)S(1)} %fusion.58, s32[]{:T(128)S(6)} %select_n.93, bf16[1,4,1024,1024]{3,2,1,0:T(8,128)(2,1)S(1)} %copy-done, bf16[4,64,1024]{2,1,0:T(8,128)(2,1)S(1)} %get-tuple-element.12, bf16[4,64,1024]{2,1,0:T(8,128)(2,1)S(1)} %get-tuple-element.10), kind=kOutput, calls=%fused_computation.48 | convolution fusion | flops 1076363264 | bytes 10485764 | tf_op jit(solution)/shard_map/sik,sjk->sij/dot_general | solution.py:67
  102.3 0.2 collective-permute-done.8
  102.5 2.9 %fusion.52 = bf16[4,1024,1024]{2,1,0:T(8,128)(2,1)S(1)} fusion(bf16[4,1024,1024]{2,1,0:T(8,128)(2,1)S(1)} %fusion.55, s32[]{:T(128)S(6)} %select_n.94, bf16[1,4,1024,1024]{3,2,1,0:T(8,128)(2,1)S(1)} %copy-done, bf16[4,64,1024]{2,1,0:T(8,128)(2,1)S(1)} %collective-permute-done.8, bf16[4,32,1024]{2,1,0:T(8,128)(2,1)S(1)} %collective-permute-done.7, ...), kind=kOutput, calls=%fused_computation.47 | convolution fusion | flops 1077411840 | bytes 10485764 | tf_op jit(solution)/shard_map/sik,sjk->sij/dot_general | solution.py:67
  105.4 2.4 %fusion.16 = f32[1024,1024]{1,0:T(8,128)S(1)} fusion(bf16[4,1024,1024]{2,1,0:T(8,128)(2,1)S(1)} %fusion.52, bf16[1,4,1024,1024]{3,2,1,0:T(8,128)(2,1)S(1)} %copy-done), kind=kOutput, calls=%fused_computation.24 | convolution fusion | flops 2147483648 | bytes 8388608 | tf_op jit(solution)/shard_map/dot_general | solution.py:73
  107.8 4.6 %fusion.17 = f32[1024,1024]{1,0:T(8,128)} fusion(bf16[4,1024,1024]{2,1,0:T(8,128)(2,1)S(1)} %fusion.52, bf16[1,4,1024,1024]{3,2,1,0:T(8,128)(2,1)S(1)} %copy-done), kind=kOutput, calls=%fused_computation.26 | convolution fusion | flops 2147483648 | bytes 8388608 | tf_op jit(solution)/shard_map/dot_general | solution.py:73
  112.4 4.4 %fusion.18 = f32[1024,1024]{1,0:T(8,128)} fusion(bf16[4,1024,1024]{2,1,0:T(8,128)(2,1)S(1)} %fusion.52, bf16[1,4,1024,1024]{3,2,1,0:T(8,128)(2,1)S(1)} %copy-done), kind=kOutput, calls=%fused_computation.28 | convolution fusion | flops 2147483648 | bytes 8388608 | tf_op jit(solution)/shard_map/dot_general | solution.py:73
  116.8 6.2 %add_convert_fusion = bf16[1024,1024]{1,0:T(8,128)(2,1)S(1)} fusion(f32[1024,1024]{1,0:T(8,128)S(1)} %fusion.16, f32[1024,1024]{1,0:T(8,128)} %fusion.17, f32[1024,1024]{1,0:T(8,128)} %fusion.18, bf16[1,4,1024,1024]{3,2,1,0:T(8,128)(2,1)S(1)} %copy-done, bf16[4,1024,1024]{2,1,0:T(8,128)(2,1)S(1)} %fusion.52), kind=kOutput, calls=%fused_computation.20 | convolution fusion | flops 2151677952 | bytes 18874368 | tf_op jit(solution)/shard_map/dot_general | solution.py:73
  123.0 2.0 %copy.30 = bf16[128,8,8,128]{3,2,1,0:T(8,128)(2,1)} copy(bf16[128,8,8,128]{3,1,2,0:T(8,128)(2,1)S(1)} %bitcast.128) | data formatting | bytes 4194304
  125.1 3.3 %copy.21 = bf16[8,128,8,128]{3,1,2,0:T(8,128)(2,1)S(1)} copy(bf16[8,128,8,128]{1,0,3,2:T(8,128)(2,1)} %bitcast.130) | data formatting | bytes 4194304 | tf_op jit(solution)/shard_map/reshape | solution.py:81
  128.3 1.8 gather_fusion.1
  130.2 0.8 gather_fusion.2
  130.9 1.4 copy.22
  132.4 0.3 broadcast_in_dim.70
  132.7 0.9 fusion.78
  133.5 0.1 copy-done.4
  133.6 1.7 pad_maximum_fusion
  135.3 12.9 %all-to-all-start.1 = ((bf16[16,576,128]{2,1,0:T(8,128)(2,1)}), bf16[16,576,128]{2,1,0:T(8,128)(2,1)S(1)}, u32[]{:S(2)}, u32[]{:S(2)}) async-start(bf16[16,576,128]{2,1,0:T(8,128)(2,1)} %pad_maximum_fusion), calls=%async_computation.1 | async-start | bytes 4718592 | tf_op jit(solution)/shard_map/all_to_all | solution.py:96
  148.2 31.1 %all-to-all-done.1 = bf16[16,576,128]{2,1,0:T(8,128)(2,1)S(1)} async-done(((bf16[16,576,128]{2,1,0:T(8,128)(2,1)}), bf16[16,576,128]{2,1,0:T(8,128)(2,1)S(1)}, u32[]{:S(2)}, u32[]{:S(2)}) %all-to-all-start.1) | async-done | bytes 2359328 | tf_op jit(solution)/shard_map/all_to_all | solution.py:96
  179.3 0.2 fusion.111
  179.5 0.7 fusion.82
  180.3 1.3 gather_fusion.3
  181.6 0.7 all_to_all.14
  182.3 6.5 %all-to-all-start.2 = ((f32[16,1,8]{2,1,0:T(1,128)}), f32[16,1,8]{2,1,0:T(1,128)S(1)}, u32[]{:S(2)}, u32[]{:S(2)}) async-start(f32[16,1,8]{2,1,0:T(1,128)} %bitcast.32), calls=%async_computation.2 | async-start | bytes 16384 | tf_op jit(solution)/shard_map/all_to_all | solution.py:104
  188.8 2.6 %copy.27 = bf16[1,1,1024,1024]{3,2,1,0:T(8,128)(2,1)} copy(bf16[1,1,1024,1024]{2,3,1,0:T(8,128)(2,1)S(1)} %bitcast.129) | data formatting | bytes 4194304
  191.4 4.5 %all-to-all-done.2 = f32[16,1,8]{2,1,0:T(1,128)S(1)} async-done(((f32[16,1,8]{2,1,0:T(1,128)}), f32[16,1,8]{2,1,0:T(1,128)S(1)}, u32[]{:S(2)}, u32[]{:S(2)}) %all-to-all-start.2) | async-done | bytes 544 | tf_op jit(solution)/shard_map/all_to_all | solution.py:104
  195.9 0.5 multiply_bitcast_fusion
  (44 shorter events, 0.8 us)
Async XLA Ops:
  0.6 6.4 %copy-start.9 = (s32[4]{0:T(128)S(1)}, s32[4]{0:T(128)}, u32[]{:S(2)}) copy-start(s32[4]{0:T(128)} %param.11) | copy-start | bytes 52
  0.6 37.8 %copy-start.7 = (pred[36]{0:T(512)(128)(4,1)S(1)}, pred[36]{0:T(512)(128)(4,1)}, u32[]{:S(2)}) copy-start(pred[36]{0:T(512)(128)(4,1)} %constant.79) | copy-start | bytes 112
  0.7 38.0 %copy-start.6 = (s32[36]{0:T(128)S(1)}, s32[36]{0:T(128)}, u32[]{:S(2)}) copy-start(s32[36]{0:T(128)} %constant.94) | copy-start | bytes 436
  0.7 39.4 %copy-start.5 = (s32[36]{0:T(128)S(1)}, s32[36]{0:T(128)}, u32[]{:S(2)}) copy-start(s32[36]{0:T(128)} %constant.95) | copy-start | bytes 436
  0.7 37.0 %all-to-all-start = ((bf16[8,128,1024]{2,1,0:T(8,128)(2,1)}), bf16[8,128,1024]{2,1,0:T(8,128)(2,1)S(1)}, u32[]{:S(2)}, u32[]{:S(2)}) async-start(bf16[8,128,1024]{2,1,0:T(8,128)(2,1)} %bitcast.135), calls=%async_computation | async-start | bytes 4194304 | tf_op jit(solution)/shard_map/all_to_all | solution.py:26
  38.2 23.2 %collective-permute-start.2 = (bf16[4,128,1024]{2,1,0:T(8,128)(2,1)S(1)}, bf16[4,128,1024]{2,1,0:T(8,128)(2,1)S(1)}, u32[]{:S(2)}, u32[]{:S(2)}) collective-permute-start(bf16[4,128,1024]{2,1,0:T(8,128)(2,1)S(1)} %gather_fusion), channel_id=1, source_target_pairs={{0,96},{16,112},{32,0},{48,16},{64,32},{80,48},{96,64},{112,80},{1... | collective-permute-start | bytes 3145736 | tf_op jit(solution)/shard_map/ppermute | solution.py:12
  38.6 24.4 %collective-permute-start.1 = (bf16[4,128,1024]{2,1,0:T(8,128)(2,1)S(1)}, bf16[4,128,1024]{2,1,0:T(8,128)(2,1)S(1)}, u32[]{:S(2)}, u32[]{:S(2)}) collective-permute-start(bf16[4,128,1024]{2,1,0:T(8,128)(2,1)S(1)} %gather_fusion), channel_id=1, source_target_pairs={{0,32},{16,48},{32,64},{48,80},{64,96},{80,112},{96,0},{112,16},{1... | collective-permute-start | bytes 3145736 | tf_op jit(solution)/shard_map/ppermute | solution.py:12
  40.1 3.4 %copy-start = (bf16[1,4,1024,1024]{3,2,1,0:T(8,128)(2,1)S(1)}, bf16[1,4,1024,1024]{3,2,1,0:T(8,128)(2,1)}, u32[]{:S(2)}) copy-start(bf16[1,4,1024,1024]{3,2,1,0:T(8,128)(2,1)} %param.9) | copy-start | bytes 25165828
  40.1 23.0 %collective-permute-start = (bf16[4,128,1024]{2,1,0:T(8,128)(2,1)S(1)}, bf16[4,128,1024]{2,1,0:T(8,128)(2,1)S(1)}, u32[]{:S(2)}, u32[]{:S(2)}) collective-permute-start(bf16[4,128,1024]{2,1,0:T(8,128)(2,1)S(1)} %gather_fusion), channel_id=1, source_target_pairs={{0,16},{16,0},{32,48},{48,32},{64,80},{80,64},{96,112},{112,96},{1... | collective-permute-start | bytes 3145736 | tf_op jit(solution)/shard_map/ppermute | solution.py:16
  63.5 25.9 %collective-permute-start.4 = (bf16[2,4,64,1024]{3,2,1,0:T(8,128)(2,1)S(1)}, bf16[2,4,64,1024]{3,2,1,0:T(8,128)(2,1)}, u32[]{:S(2)}, u32[]{:S(2)}) collective-permute-start(bf16[2,4,64,1024]{3,2,1,0:T(8,128)(2,1)S(1)} %get-tuple-element.19), channel_id=1, source_target_pairs={{0,96},{16,112},{32,0},{48,16},{64,32},{80,48},{96,64},{112,80},{1... | collective-permute-start | bytes 3145736 | tf_op jit(solution)/shard_map/ppermute | solution.py:12
  64.7 23.1 %collective-permute-start.3 = (bf16[2,4,64,1024]{3,2,1,0:T(8,128)(2,1)S(1)}, bf16[2,4,64,1024]{3,2,1,0:T(8,128)(2,1)}, u32[]{:S(2)}, u32[]{:S(2)}) collective-permute-start(bf16[2,4,64,1024]{3,2,1,0:T(8,128)(2,1)S(1)} %get-tuple-element.20), channel_id=1, source_target_pairs={{0,32},{16,48},{32,64},{48,80},{64,96},{80,112},{96,0},{112,16},{1... | collective-permute-start | bytes 3145736 | tf_op jit(solution)/shard_map/ppermute | solution.py:12
  65.0 31.4 %collective-permute-start.5 = (bf16[2,4,64,1024]{3,2,1,0:T(8,128)(2,1)S(1)}, bf16[2,4,64,1024]{3,2,1,0:T(8,128)(2,1)S(1)}, u32[]{:S(2)}, u32[]{:S(2)}) collective-permute-start(bf16[2,4,64,1024]{3,2,1,0:T(8,128)(2,1)S(1)} %get-tuple-element.18), channel_id=1, source_target_pairs={{0,16},{16,0},{32,48},{48,32},{64,80},{80,64},{96,112},{112,96},{1... | collective-permute-start | bytes 3145736 | tf_op jit(solution)/shard_map/ppermute | solution.py:16
  89.1 13.2 %collective-permute-start.6 = (bf16[4,32,1024]{2,1,0:T(8,128)(2,1)S(1)}, bf16[4,32,1024]{2,1,0:T(8,128)(2,1)S(1)}, u32[]{:S(2)}, u32[]{:S(2)}) collective-permute-start(bf16[4,32,1024]{2,1,0:T(8,128)(2,1)S(1)} %slice.120), channel_id=1, source_target_pairs={{0,32},{16,48},{32,64},{48,80},{64,96},{80,112},{96,0},{112,16},{1... | collective-permute-start | bytes 786440 | tf_op jit(solution)/shard_map/ppermute | solution.py:12
  90.7 11.6 %collective-permute-start.7 = (bf16[4,32,1024]{2,1,0:T(8,128)(2,1)S(1)}, bf16[4,32,1024]{2,1,0:T(8,128)(2,1)S(1)}, u32[]{:S(2)}, u32[]{:S(2)}) collective-permute-start(bf16[4,32,1024]{2,1,0:T(8,128)(2,1)S(1)} %slice.121), channel_id=1, source_target_pairs={{0,96},{16,112},{32,0},{48,16},{64,32},{80,48},{96,64},{112,80},{1... | collective-permute-start | bytes 786440 | tf_op jit(solution)/shard_map/ppermute | solution.py:12
  93.4 9.1 %collective-permute-start.8 = (bf16[4,64,1024]{2,1,0:T(8,128)(2,1)S(1)}, bf16[4,64,1024]{2,1,0:T(8,128)(2,1)S(1)}, u32[]{:S(2)}, u32[]{:S(2)}) collective-permute-start(bf16[4,64,1024]{2,1,0:T(8,128)(2,1)S(1)} %get-tuple-element.11), channel_id=1, source_target_pairs={{0,16},{16,0},{32,48},{48,32},{64,80},{80,64},{96,112},{112,96},{1... | collective-permute-start | bytes 1572872 | tf_op jit(solution)/shard_map/ppermute | solution.py:16
  123.0 2.0 %copy-start.1 = (bf16[1024,1024]{1,0:T(8,128)(2,1)}, bf16[1024,1024]{1,0:T(8,128)(2,1)S(1)}, u32[]{:S(2)}) copy-start(bf16[1024,1024]{1,0:T(8,128)(2,1)S(1)} %add_convert_fusion) | copy-start | bytes 6291460
  130.9 1.7 copy-start.3
  132.4 1.3 copy-start.4
  135.3 12.9 %copy-start.8 = (s32[128,2]{0,1:T(2,128)S(1)}, s32[128,2]{0,1:T(2,128)}, u32[]{:S(2)}) copy-start(s32[128,2]{0,1:T(2,128)} %param.12) | copy-start | bytes 3076
  135.3 44.0 %all-to-all-start.1 = ((bf16[16,576,128]{2,1,0:T(8,128)(2,1)}), bf16[16,576,128]{2,1,0:T(8,128)(2,1)S(1)}, u32[]{:S(2)}, u32[]{:S(2)}) async-start(bf16[16,576,128]{2,1,0:T(8,128)(2,1)} %pad_maximum_fusion), calls=%async_computation.1 | async-start | bytes 4718592 | tf_op jit(solution)/shard_map/all_to_all | solution.py:96
  179.5 9.3 %copy-start.2 = (bf16[1024,1024]{1,0:T(8,128)(2,1)S(1)}, bf16[1024,1024]{1,0:T(8,128)(2,1)}, u32[]{:S(2)}) copy-start(bf16[1024,1024]{1,0:T(8,128)(2,1)} %copy-done.1) | copy-start | bytes 6291460
  182.3 13.6 %all-to-all-start.2 = ((f32[16,1,8]{2,1,0:T(1,128)}), f32[16,1,8]{2,1,0:T(1,128)S(1)}, u32[]{:S(2)}, u32[]{:S(2)}) async-start(f32[16,1,8]{2,1,0:T(1,128)} %bitcast.32), calls=%async_computation.2 | async-start | bytes 16384 | tf_op jit(solution)/shard_map/all_to_all | solution.py:104
where the time goes:
time: 197 us; the launch traced here: 196 us
  waiting for transfers between devices  96.8 us (49%)
  matrix products  41.8 us (21%)
  starting transfers between devices  31.9 us (16%)
  local copies, waits for them, and re-layouts  21.3 us (11%)
  other arithmetic  3.4 us (2%)
    all_to_all x1, waiting for transfers between devices, body(): received = lax.all_to_all(slices, 'mom', 0, 0)  31.1 us
    all_to_all x1, waiting for transfers between devices, source_pieces(): received = lax.all_to_all(pieces, 'tsink', 0, 0)  30.6 us
    ppermute x6, waiting for transfers between devices, shifted(): return lax.ppermute(block, 'tsink', pairs)  30.4 us
    dot_general x8, matrix products, body(): jnp.einsum('sik,sjk->sij', piece, propagators, preferred_element_type=jnp...  23.5 us
    dot_general x4, matrix products, body(): jnp.dot(propagators[source], halves[source], preferred_element_type=jnp.f...  17.6 us
    all_to_all x1, starting transfers between devices, body(): received = lax.all_to_all(slices, 'mom', 0, 0)  12.9 us
    unnamed x22, local copies, waits for them, and re-layouts  6.96 us
    all_to_all x1, starting transfers between devices, body(): spread = lax.all_to_all(per_diagram.reshape(n_m, -1), 'mom', 0, 0)  6.53 us
  transfers between devices with their start and end apart: 12, of which 7 were waited for; matrix products, arithmetic and copies ran while one was open for 14% of the time, Pallas kernels for 0%

commit v1 on v0

--- a/solution.py
+++ b/solution.py
@@ -68,11 +68,11 @@
             "sik,sjk->sij", piece, propagators, preferred_element_type=jnp.float32
         ).astype(jnp.bfloat16)
         halves = lax.dynamic_update_slice_in_dim(halves, block, origin * rows, 1)
-    summed = jnp.zeros((block_order, block_order), jnp.float32)
-    for source in range(NSRC):
-        summed = summed + jnp.dot(
-            propagators[source], halves[source], preferred_element_type=jnp.float32
-        )
+    side_by_side = jnp.concatenate([propagators[source] for source in range(NSRC)], axis=1)
+    summed = jnp.dot(
+        side_by_side, halves.reshape(NSRC * block_order, block_order),
+        preferred_element_type=jnp.float32,
+    )
     meson = summed.astype(jnp.bfloat16)
 
     n_m = lax.axis_size("mom")

time: 197 us -> 194 us (0.985)
  blocking collectives: 0 us -> 13.3 us
  starting transfers between devices: 31.9 us -> 24.9 us
  waiting for transfers between devices: 96.8 us -> 91.2 us
  local copies, waits for them, and re-layouts: 21.3 us -> 18.7 us
    all_to_all x0 -> x1, blocking collectives: none -> 13.3 us  [body(): spread = lax.all_to_all(per_diagram.reshape(n_m, -1), 'mom', 0, 0)]
    dot_general x4 -> x1, matrix products: 17.6 us -> 11 us  [body(): jnp.dot(side_by_side, halves.reshape(NSRC * block_order, block_order), pr...]
    all_to_all x1 -> x0, starting transfers between devices: 6.53 us -> none  [body(): spread = lax.all_to_all(per_diagram.reshape(n_m, -1), 'mom', 0, 0)]
    unnamed x22 -> x25, local copies, waits for them, and re-layouts: 6.96 us -> 0.93 us
    squeeze x0 -> x1, local copies, waits for them, and re-layouts: none -> 5.97 us  [body(): propagators[source]]
    dot_general x8, matrix products: 23.5 us -> 28.5 us  [body(): jnp.einsum('sik,sjk->sij', piece, propagators, preferred_element_type=jnp...]
    all_to_all x1 -> x0, waiting for transfers between devices: 4.45 us -> none  [body(): spread = lax.all_to_all(per_diagram.reshape(n_m, -1), 'mom', 0, 0)]
    reshape x1, local copies, waits for them, and re-layouts: 3.28 us -> 0.57 us  [body(): meson.reshape(n_b, width, n_b, width).transpose(0, 2, 1, 3)]
  transfers between devices with their start and end apart: 12 -> 11, of which waited for: 7 -> 6; matrix products, arithmetic and copies ran while one was open for 14% -> 18% of each run, Pallas kernels for 0% -> 0%
where the time goes in v1:
time: 194 us
  waiting for transfers between devices  91.2 us (47%)
  matrix products  40.2 us (21%)
  starting transfers between devices  24.9 us (13%)
  local copies, waits for them, and re-layouts  18.7 us (10%)
  blocking collectives  13.3 us (7%)
  other arithmetic  4.46 us (2%)
    all_to_all x1, waiting for transfers between devices, body(): received = lax.all_to_all(slices, 'mom', 0, 0)  31.1 us
    all_to_all x1, waiting for transfers between devices, source_pieces(): received = lax.all_to_all(pieces, 'tsink', 0, 0)  30.6 us
    ppermute x6, waiting for transfers between devices, shifted(): return lax.ppermute(block, 'tsink', pairs)  29.2 us
    dot_general x8, matrix products, body(): jnp.einsum('sik,sjk->sij', piece, propagators, preferred_element_type=jnp...  28.5 us
    all_to_all x1, blocking collectives, body(): spread = lax.all_to_all(per_diagram.reshape(n_m, -1), 'mom', 0, 0)  13.3 us
    all_to_all x1, starting transfers between devices, body(): received = lax.all_to_all(slices, 'mom', 0, 0)  12.8 us
    dot_general x1, matrix products, body(): jnp.dot(side_by_side, halves.reshape(NSRC * block_order, block_order), pr...  11 us
    all_to_all x1, starting transfers between devices, source_pieces(): received = lax.all_to_all(pieces, 'tsink', 0, 0)  6.2 us
  transfers between devices with their start and end apart: 11, of which 6 were waited for; matrix products, arithmetic and copies ran while one was open for 18% of the time, Pallas kernels for 0%

profile of v1, /device:TPU:1, one launch (start us, length us, event | category | flops | bytes accessed | tf_op | source)
XLA Modules:
  0.0 193.9 jit_solution(10915906360670354601)
XLA Ops:
  0.6 6.2 %all-to-all-start = ((bf16[8,128,1024]{2,1,0:T(8,128)(2,1)}), bf16[8,128,1024]{2,1,0:T(8,128)(2,1)S(1)}, u32[]{:S(2)}, u32[]{:S(2)}) async-start(bf16[8,128,1024]{2,1,0:T(8,128)(2,1)} %bitcast.114), calls=%async_computation | async-start | bytes 4194304 | tf_op jit(solution)/shard_map/all_to_all | solution.py:26
  6.9 30.6 %all-to-all-done = bf16[8,128,1024]{2,1,0:T(8,128)(2,1)S(1)} async-done(((bf16[8,128,1024]{2,1,0:T(8,128)(2,1)}), bf16[8,128,1024]{2,1,0:T(8,128)(2,1)S(1)}, u32[]{:S(2)}, u32[]{:S(2)}) %all-to-all-start) | async-done | bytes 2097184 | tf_op jit(solution)/shard_map/all_to_all | solution.py:26
  37.5 0.6 gather_fusion
  38.1 0.1 collective-permute-start.2
  38.2 6.0 %slice_bitcast_fusion.3 = (bf16[1024,1024]{1,0:T(8,128)(2,1)}, bf16[1024,1024]{1,0:T(8,128)(2,1)}, bf16[1024,1024]{1,0:T(8,128)(2,1)}, bf16[1024,1024]{1,0:T(8,128)(2,1)}) fusion(bf16[1,4,1024,1024]{3,2,1,0:T(8,128)(2,1)} %param.9), kind=kLoop, calls=%fused_computation.33 | loop fusion | bytes 16777216 | tf_op jit(solution)/shard_map/squeeze | solution.py:71
  44.3 0.1 broadcast_in_dim.65
  44.4 1.5 collective-permute-start.1
  46.0 0.1 collective-permute-start
  46.1 1.1 broadcast_in_dim.59
  47.2 6.5 %fusion.72 = bf16[4,1024,1024]{2,1,0:T(8,128)(2,1)S(1)} fusion(bf16[4,1024,1024]{2,1,0:T(8,128)(2,1)S(1)} %broadcast_in_dim.59, s32[]{:T(128)S(6)} %select_n.84, bf16[4,128,1024]{2,1,0:T(8,128)(2,1)S(1)} %gather_fusion, bf16[1,4,1024,1024]{3,2,1,0:T(8,128)(2,1)} %param.9), kind=kOutput, calls=%fused_computation.50 | convolution fusion | flops 1074266112 | bytes 10485764 | tf_op jit(solution)/shard_map/sik,sjk->sij/dot_general | solution.py:67
  53.6 7.7 %collective-permute-done.2 = bf16[4,128,1024]{2,1,0:T(8,128)(2,1)S(1)} collective-permute-done((bf16[4,128,1024]{2,1,0:T(8,128)(2,1)S(1)}, bf16[4,128,1024]{2,1,0:T(8,128)(2,1)S(1)}, u32[]{:S(2)}, u32[]{:S(2)}) %collective-permute-start.2) | collective-permute-done | bytes 1048608 | tf_op jit(solution)/shard_map/ppermute | solution.py:12
  61.4 7.5 %collective-permute-done.1 = bf16[4,128,1024]{2,1,0:T(8,128)(2,1)S(1)} collective-permute-done((bf16[4,128,1024]{2,1,0:T(8,128)(2,1)S(1)}, bf16[4,128,1024]{2,1,0:T(8,128)(2,1)S(1)}, u32[]{:S(2)}, u32[]{:S(2)}) %collective-permute-start.1) | collective-permute-done | bytes 1048608 | tf_op jit(solution)/shard_map/ppermute | solution.py:12
  69.0 1.3 pad_maximum_fusion.3
  70.3 1.2 collective-permute-start.4
  71.5 0.3 collective-permute-start.3
  71.8 3.0 %fusion.69 = bf16[4,1024,1024]{2,1,0:T(8,128)(2,1)S(1)} fusion(bf16[4,1024,1024]{2,1,0:T(8,128)(2,1)S(1)} %fusion.72, s32[]{:T(128)S(6)} %select_n.85, bf16[4,128,1024]{2,1,0:T(8,128)(2,1)S(1)} %collective-permute-done, bf16[1,4,1024,1024]{3,2,1,0:T(8,128)(2,1)S(1)} %bitcast.105), kind=kOutput, calls=%fused_computation.49 | convolution fusion | flops 1074266112 | bytes 10485764 | tf_op jit(solution)/shard_map/sik,sjk->sij/dot_general | solution.py:67
  74.8 2.9 %fusion.66 = bf16[4,1024,1024]{2,1,0:T(8,128)(2,1)S(1)} fusion(bf16[4,1024,1024]{2,1,0:T(8,128)(2,1)S(1)} %fusion.69, s32[]{:T(128)S(6)} %select_n.87, bf16[4,128,1024]{2,1,0:T(8,128)(2,1)S(1)} %collective-permute-done.1, bf16[1,4,1024,1024]{3,2,1,0:T(8,128)(2,1)S(1)} %bitcast.105), kind=kOutput, calls=%fused_computation.48 | convolution fusion | flops 1074266112 | bytes 10485764 | tf_op jit(solution)/shard_map/sik,sjk->sij/dot_general | solution.py:67
  77.7 3.0 %fusion.63 = bf16[4,1024,1024]{2,1,0:T(8,128)(2,1)S(1)} fusion(bf16[4,1024,1024]{2,1,0:T(8,128)(2,1)S(1)} %fusion.66, s32[]{:T(128)S(6)} %select_n.89, bf16[4,128,1024]{2,1,0:T(8,128)(2,1)S(1)} %collective-permute-done.2, bf16[1,4,1024,1024]{3,2,1,0:T(8,128)(2,1)S(1)} %bitcast.105), kind=kOutput, calls=%fused_computation.47 | convolution fusion | flops 1074266112 | bytes 10485764 | tf_op jit(solution)/shard_map/sik,sjk->sij/dot_general | solution.py:67
  80.7 14.1 %collective-permute-done.3 = bf16[2,4,64,1024]{3,2,1,0:T(8,128)(2,1)} collective-permute-done((bf16[2,4,64,1024]{3,2,1,0:T(8,128)(2,1)}, bf16[2,4,64,1024]{3,2,1,0:T(8,128)(2,1)}, u32[]{:S(2)}, u32[]{:S(2)}) %collective-permute-start.3) | collective-permute-done | bytes 1048608 | tf_op jit(solution)/shard_map/ppermute | solution.py:12
  94.8 1.3 slice_bitcast_fusion.8
  96.1 0.1 collective-permute-start.6
  96.2 1.3 slice_bitcast_fusion.5
  97.5 0.7 slice.105
  98.2 2.7 %collective-permute-start.7 = (bf16[4,32,1024]{2,1,0:T(8,128)(2,1)}, bf16[4,32,1024]{2,1,0:T(8,128)(2,1)}, u32[]{:S(2)}, u32[]{:S(2)}) collective-permute-start(bf16[4,32,1024]{2,1,0:T(8,128)(2,1)} %slice.105), channel_id=1, source_target_pairs={{0,96},{16,112},{32,0},{48,16},{64,32},{80,48},{96,64},{112,80},{1... | collective-permute-start | bytes 786440 | tf_op jit(solution)/shard_map/ppermute | solution.py:12
  100.8 2.9 %fusion.60 = bf16[4,1024,1024]{2,1,0:T(8,128)(2,1)S(1)} fusion(bf16[4,1024,1024]{2,1,0:T(8,128)(2,1)S(1)} %fusion.63, s32[]{:T(128)S(6)} %select_n.91, bf16[1,4,1024,1024]{3,2,1,0:T(8,128)(2,1)S(1)} %bitcast.105, bf16[4,64,1024]{2,1,0:T(8,128)(2,1)S(1)} %get-tuple-element.9, bf16[4,64,1024]{2,1,0:T(8,128)(2,1)S(1)} %get-tuple-element.13), kind=kOutput, calls=%fused_computation.46 | convolution fusion | flops 1076363264 | bytes 10485764 | tf_op jit(solution)/shard_map/sik,sjk->sij/dot_general | solution.py:67
  103.8 2.9 %fusion.57 = bf16[4,1024,1024]{2,1,0:T(8,128)(2,1)S(1)} fusion(bf16[4,1024,1024]{2,1,0:T(8,128)(2,1)S(1)} %fusion.60, s32[]{:T(128)S(6)} %select_n.92, bf16[1,4,1024,1024]{3,2,1,0:T(8,128)(2,1)S(1)} %bitcast.105, bf16[4,64,1024]{2,1,0:T(8,128)(2,1)S(1)} %get-tuple-element.11, bf16[4,64,1024]{2,1,0:T(8,128)(2,1)S(1)} %get-tuple-element.12), kind=kOutput, calls=%fused_computation.45 | convolution fusion | flops 1076363264 | bytes 10485764 | tf_op jit(solution)/shard_map/sik,sjk->sij/dot_general | solution.py:67
  106.8 2.9 %fusion.54 = bf16[4,1024,1024]{2,1,0:T(8,128)(2,1)S(1)} fusion(bf16[4,1024,1024]{2,1,0:T(8,128)(2,1)S(1)} %fusion.57, s32[]{:T(128)S(6)} %select_n.93, bf16[1,4,1024,1024]{3,2,1,0:T(8,128)(2,1)S(1)} %bitcast.105, bf16[4,64,1024]{2,1,0:T(8,128)(2,1)S(1)} %get-tuple-element.10, bf16[4,64,1024]{2,1,0:T(8,128)(2,1)S(1)} %get-tuple-element.8), kind=kOutput, calls=%fused_computation.44 | convolution fusion | flops 1076363264 | bytes 10485764 | tf_op jit(solution)/shard_map/sik,sjk->sij/dot_general | solution.py:67
  109.7 0.3 collective-permute-done.8
  110.0 4.3 %fusion.51 = bf16[4,1024,1024]{2,1,0:T(8,128)(2,1)S(1)} fusion(bf16[4,1024,1024]{2,1,0:T(8,128)(2,1)S(1)} %fusion.54, s32[]{:T(128)S(6)} %select_n.94, bf16[1,4,1024,1024]{3,2,1,0:T(8,128)(2,1)S(1)} %bitcast.105, bf16[4,64,1024]{2,1,0:T(8,128)(2,1)} %collective-permute-done.8, bf16[4,32,1024]{2,1,0:T(8,128)(2,1)} %collective-permute-done.7, ...), kind=kOutput, calls=%fused_computation.43 | convolution fusion | flops 1077411840 | bytes 10485764 | tf_op jit(solution)/shard_map/sik,sjk->sij/dot_general | solution.py:67
  114.4 11.0 %fusion.24 = bf16[1024,1024]{1,0:T(8,128)(2,1)S(1)} fusion(bf16[4096,1024]{1,0:T(8,128)(2,1)S(1)} %bitcast.108, bf16[1024,1024]{1,0:T(8,128)(2,1)} %get-tuple-element.5, bf16[1024,1024]{1,0:T(8,128)(2,1)S(1)} %copy-done.4, bf16[1024,1024]{1,0:T(8,128)(2,1)} %get-tuple-element.4, bf16[1024,1024]{1,0:T(8,128)(2,1)S(1)} %copy-done.3), kind=kOutput, calls=%fused_computation.34 | convolution fusion | flops 8624537600 | bytes 18874368 | tf_op jit(solution)/shard_map/dot_general | solution.py:72
  125.4 0.6 copy.27
  126.0 0.6 copy.19
  126.6 0.1 copy-done.2
  126.7 1.8 gather_fusion.1
  128.6 0.8 gather_fusion.2
  129.4 1.4 copy.20
  130.8 0.3 broadcast_in_dim.70
  131.1 0.9 fusion.75
  131.9 0.1 copy-done.1
  132.0 1.7 pad_maximum_fusion
  133.7 12.8 %all-to-all-start.1 = ((bf16[16,576,128]{2,1,0:T(8,128)(2,1)}), bf16[16,576,128]{2,1,0:T(8,128)(2,1)S(1)}, u32[]{:S(2)}, u32[]{:S(2)}) async-start(bf16[16,576,128]{2,1,0:T(8,128)(2,1)} %pad_maximum_fusion), calls=%async_computation.1 | async-start | bytes 4718592 | tf_op jit(solution)/shard_map/all_to_all | solution.py:96
  146.5 31.1 %all-to-all-done.1 = bf16[16,576,128]{2,1,0:T(8,128)(2,1)S(1)} async-done(((bf16[16,576,128]{2,1,0:T(8,128)(2,1)}), bf16[16,576,128]{2,1,0:T(8,128)(2,1)S(1)}, u32[]{:S(2)}, u32[]{:S(2)}) %all-to-all-start.1) | async-done | bytes 2359328 | tf_op jit(solution)/shard_map/all_to_all | solution.py:96
  177.6 0.2 fusion.109
  177.8 0.7 fusion.79
  178.6 1.3 gather_fusion.3
  179.9 0.1 all_to_all.14
  180.0 13.3 %all_to_all.19 = f32[16,1,8]{2,1,0:T(1,128)S(1)} all-to-all(f32[16,1,8]{2,1,0:T(1,128)S(1)} %bitcast.117), channel_id=1, replica_groups=mesh['tsink'=8,'mom'=16] {'mom'}, dimensions={0} | all-to-all | bytes 1024 | tf_op jit(solution)/shard_map/all_to_all | solution.py:104
  193.4 0.5 multiply_bitcast_fusion
  (45 shorter events, 0.6 us)
Async XLA Ops:
  0.6 6.2 %copy-start.9 = (s32[4]{0:T(128)S(1)}, s32[4]{0:T(128)}, u32[]{:S(2)}) copy-start(s32[4]{0:T(128)} %param.11) | copy-start | bytes 52
  0.6 36.8 %all-to-all-start = ((bf16[8,128,1024]{2,1,0:T(8,128)(2,1)}), bf16[8,128,1024]{2,1,0:T(8,128)(2,1)S(1)}, u32[]{:S(2)}, u32[]{:S(2)}) async-start(bf16[8,128,1024]{2,1,0:T(8,128)(2,1)} %bitcast.114), calls=%async_computation | async-start | bytes 4194304 | tf_op jit(solution)/shard_map/all_to_all | solution.py:26
  38.1 6.1 %copy-start.7 = (pred[36]{0:T(512)(128)(4,1)S(1)}, pred[36]{0:T(512)(128)(4,1)}, u32[]{:S(2)}) copy-start(pred[36]{0:T(512)(128)(4,1)} %constant.79) | copy-start | bytes 112
  38.1 6.3 %copy-start.6 = (s32[36]{0:T(128)S(1)}, s32[36]{0:T(128)}, u32[]{:S(2)}) copy-start(s32[36]{0:T(128)} %constant.94) | copy-start | bytes 436
  38.1 7.8 %copy-start.5 = (s32[36]{0:T(128)S(1)}, s32[36]{0:T(128)}, u32[]{:S(2)}) copy-start(s32[36]{0:T(128)} %constant.95) | copy-start | bytes 436
  38.1 23.2 %collective-permute-start.2 = (bf16[4,128,1024]{2,1,0:T(8,128)(2,1)S(1)}, bf16[4,128,1024]{2,1,0:T(8,128)(2,1)S(1)}, u32[]{:S(2)}, u32[]{:S(2)}) collective-permute-start(bf16[4,128,1024]{2,1,0:T(8,128)(2,1)S(1)} %gather_fusion), channel_id=1, source_target_pairs={{0,96},{16,112},{32,0},{48,16},{64,32},{80,48},{96,64},{112,80},{1... | collective-permute-start | bytes 3145736 | tf_op jit(solution)/shard_map/ppermute | solution.py:12
  44.4 24.4 %collective-permute-start.1 = (bf16[4,128,1024]{2,1,0:T(8,128)(2,1)S(1)}, bf16[4,128,1024]{2,1,0:T(8,128)(2,1)S(1)}, u32[]{:S(2)}, u32[]{:S(2)}) collective-permute-start(bf16[4,128,1024]{2,1,0:T(8,128)(2,1)S(1)} %gather_fusion), channel_id=1, source_target_pairs={{0,32},{16,48},{32,64},{48,80},{64,96},{80,112},{96,0},{112,16},{1... | collective-permute-start | bytes 3145736 | tf_op jit(solution)/shard_map/ppermute | solution.py:12
  46.0 23.0 %collective-permute-start = (bf16[4,128,1024]{2,1,0:T(8,128)(2,1)S(1)}, bf16[4,128,1024]{2,1,0:T(8,128)(2,1)S(1)}, u32[]{:S(2)}, u32[]{:S(2)}) collective-permute-start(bf16[4,128,1024]{2,1,0:T(8,128)(2,1)S(1)} %gather_fusion), channel_id=1, source_target_pairs={{0,16},{16,0},{32,48},{48,32},{64,80},{80,64},{96,112},{112,96},{1... | collective-permute-start | bytes 3145736 | tf_op jit(solution)/shard_map/ppermute | solution.py:16
  46.1 25.7 %slice-start = ((s8[8388608]{0:T(1024)(128)(4,1)}), s8[4194304]{0:T(1024)(128)(4,1)S(1)}, s32[]{:S(2)}) async-start(s8[8388608]{0:T(1024)(128)(4,1)} %bitcast.104), calls=%async_computation.3 | async-start | bytes 8388608
  47.1 24.6 %slice-start.1 = ((s8[8388608]{0:T(1024)(128)(4,1)}), s8[4194304]{0:T(1024)(128)(4,1)S(1)}, s32[]{:S(2)}) async-start(s8[8388608]{0:T(1024)(128)(4,1)} %bitcast.104), calls=%async_computation.4 | async-start | bytes 8388608
  70.3 25.9 %collective-permute-start.4 = (bf16[2,4,64,1024]{3,2,1,0:T(8,128)(2,1)S(1)}, bf16[2,4,64,1024]{3,2,1,0:T(8,128)(2,1)}, u32[]{:S(2)}, u32[]{:S(2)}) collective-permute-start(bf16[2,4,64,1024]{3,2,1,0:T(8,128)(2,1)S(1)} %get-tuple-element.17), channel_id=1, source_target_pairs={{0,96},{16,112},{32,0},{48,16},{64,32},{80,48},{96,64},{112,80},{1... | collective-permute-start | bytes 3145736 | tf_op jit(solution)/shard_map/ppermute | solution.py:12
  71.5 23.3 %collective-permute-start.3 = (bf16[2,4,64,1024]{3,2,1,0:T(8,128)(2,1)}, bf16[2,4,64,1024]{3,2,1,0:T(8,128)(2,1)}, u32[]{:S(2)}, u32[]{:S(2)}) collective-permute-start(bf16[2,4,64,1024]{3,2,1,0:T(8,128)(2,1)} %get-tuple-element.18), channel_id=1, source_target_pairs={{0,32},{16,48},{32,64},{48,80},{64,96},{80,112},{96,0},{112,16},{1... | collective-permute-start | bytes 3145736 | tf_op jit(solution)/shard_map/ppermute | solution.py:12
  71.8 32.0 %collective-permute-start.5 = (bf16[2,4,64,1024]{3,2,1,0:T(8,128)(2,1)S(1)}, bf16[2,4,64,1024]{3,2,1,0:T(8,128)(2,1)S(1)}, u32[]{:S(2)}, u32[]{:S(2)}) collective-permute-start(bf16[2,4,64,1024]{3,2,1,0:T(8,128)(2,1)S(1)} %get-tuple-element.16), channel_id=1, source_target_pairs={{0,16},{16,0},{32,48},{48,32},{64,80},{80,64},{96,112},{112,96},{1... | collective-permute-start | bytes 3145736 | tf_op jit(solution)/shard_map/ppermute | solution.py:16
  96.1 13.6 %collective-permute-start.6 = (bf16[4,32,1024]{2,1,0:T(8,128)(2,1)S(1)}, bf16[4,32,1024]{2,1,0:T(8,128)(2,1)}, u32[]{:S(2)}, u32[]{:S(2)}) collective-permute-start(bf16[4,32,1024]{2,1,0:T(8,128)(2,1)S(1)} %slice.104), channel_id=1, source_target_pairs={{0,32},{16,48},{32,64},{48,80},{64,96},{80,112},{96,0},{112,16},{1... | collective-permute-start | bytes 786440 | tf_op jit(solution)/shard_map/ppermute | solution.py:12
  98.2 11.5 %collective-permute-start.7 = (bf16[4,32,1024]{2,1,0:T(8,128)(2,1)}, bf16[4,32,1024]{2,1,0:T(8,128)(2,1)}, u32[]{:S(2)}, u32[]{:S(2)}) collective-permute-start(bf16[4,32,1024]{2,1,0:T(8,128)(2,1)} %slice.105), channel_id=1, source_target_pairs={{0,96},{16,112},{32,0},{48,16},{64,32},{80,48},{96,64},{112,80},{1... | collective-permute-start | bytes 786440 | tf_op jit(solution)/shard_map/ppermute | solution.py:12
  100.8 9.2 %collective-permute-start.8 = (bf16[4,64,1024]{2,1,0:T(8,128)(2,1)S(1)}, bf16[4,64,1024]{2,1,0:T(8,128)(2,1)}, u32[]{:S(2)}, u32[]{:S(2)}) collective-permute-start(bf16[4,64,1024]{2,1,0:T(8,128)(2,1)S(1)} %get-tuple-element.9), channel_id=1, source_target_pairs={{0,16},{16,0},{32,48},{48,32},{64,80},{80,64},{96,112},{112,96},{1... | collective-permute-start | bytes 1572872 | tf_op jit(solution)/shard_map/ppermute | solution.py:16
  109.7 4.7 %copy-start.3 = (bf16[1024,1024]{1,0:T(8,128)(2,1)S(1)}, bf16[1024,1024]{1,0:T(8,128)(2,1)}, u32[]{:S(2)}) copy-start(bf16[1024,1024]{1,0:T(8,128)(2,1)} %get-tuple-element.2) | copy-start | bytes 6291460
  109.7 4.7 %copy-start.4 = (bf16[1024,1024]{1,0:T(8,128)(2,1)S(1)}, bf16[1024,1024]{1,0:T(8,128)(2,1)}, u32[]{:S(2)}) copy-start(bf16[1024,1024]{1,0:T(8,128)(2,1)} %get-tuple-element.3) | copy-start | bytes 6291460
  125.4 1.4 copy-start.2
  129.3 1.7 copy-start
  130.8 1.3 copy-start.1
  133.7 12.8 %copy-start.8 = (s32[128,2]{0,1:T(2,128)S(1)}, s32[128,2]{0,1:T(2,128)}, u32[]{:S(2)}) copy-start(s32[128,2]{0,1:T(2,128)} %param.12) | copy-start | bytes 3076
  133.7 43.9 %all-to-all-start.1 = ((bf16[16,576,128]{2,1,0:T(8,128)(2,1)}), bf16[16,576,128]{2,1,0:T(8,128)(2,1)S(1)}, u32[]{:S(2)}, u32[]{:S(2)}) async-start(bf16[16,576,128]{2,1,0:T(8,128)(2,1)} %pad_maximum_fusion), calls=%async_computation.1 | async-start | bytes 4718592 | tf_op jit(solution)/shard_map/all_to_all | solution.py:96

commit v2 on v0

--- a/solution.py
+++ b/solution.py
@@ -62,17 +62,29 @@
     block_order = propagators.shape[1]
     pieces = source_pieces(own_elemental, src_times)
     rows = pieces[0][1].shape[1]
-    halves = jnp.zeros((NSRC, block_order, block_order), jnp.bfloat16)
-    for origin, piece in pieces:
-        block = jnp.einsum(
-            "sik,sjk->sij", piece, propagators, preferred_element_type=jnp.float32
-        ).astype(jnp.bfloat16)
-        halves = lax.dynamic_update_slice_in_dim(halves, block, origin * rows, 1)
-    summed = jnp.zeros((block_order, block_order), jnp.float32)
-    for source in range(NSRC):
-        summed = summed + jnp.dot(
-            propagators[source], halves[source], preferred_element_type=jnp.float32
+    def stacked(group):
+        columns = jnp.concatenate(
+            [
+                lax.dynamic_slice_in_dim(propagators[source], origin * rows, rows, 1)
+                for source in range(NSRC)
+                for origin, _ in group
+            ],
+            axis=1,
         )
+        blocks = jnp.stack(
+            [
+                jnp.einsum(
+                    "sik,sjk->sij", piece, propagators, preferred_element_type=jnp.float32
+                ).astype(jnp.bfloat16)
+                for _, piece in group
+            ],
+            axis=1,
+        )
+        return jnp.dot(
+            columns, blocks.reshape(-1, block_order), preferred_element_type=jnp.float32
+        )
+
+    summed = stacked(pieces[:4]) + stacked(pieces[4:])
     meson = summed.astype(jnp.bfloat16)
 
     n_m = lax.axis_size("mom")

time: 197 us -> 193 us (0.980)
  waiting for transfers between devices: 96.8 us -> 66.4 us
  local copies, waits for them, and re-layouts: 21.3 us -> 36.8 us
  blocking collectives: 0 us -> 13.3 us
  starting transfers between devices: 31.9 us -> 25.5 us
  matrix products: 41.8 us -> 44.2 us
    all_to_all x1, waiting for transfers between devices: 30.6 us -> 7.82 us  [source_pieces(): received = lax.all_to_all(pieces, 'tsink', 0, 0)]
    all_to_all x0 -> x1, blocking collectives: none -> 13.3 us  [body(): spread = lax.all_to_all(per_diagram.reshape(n_m, -1), 'mom', 0, 0)]
    unnamed x22 -> x40, local copies, waits for them, and re-layouts: 6.96 us -> 19.8 us
    all_to_all x1 -> x0, starting transfers between devices: 6.53 us -> none  [body(): spread = lax.all_to_all(per_diagram.reshape(n_m, -1), 'mom', 0, 0)]
    slice x0 -> x1, local copies, waits for them, and re-layouts: none -> 5.7 us  [stacked(): propagators[source]]
    all_to_all x1 -> x0, waiting for transfers between devices: 4.45 us -> none  [body(): spread = lax.all_to_all(per_diagram.reshape(n_m, -1), 'mom', 0, 0)]
    ppermute x6, waiting for transfers between devices: 30.4 us -> 26.7 us  [shifted(): return lax.ppermute(block, 'tsink', pairs)]
    reshape x1, local copies, waits for them, and re-layouts: 3.28 us -> 0.57 us  [body(): meson.reshape(n_b, width, n_b, width).transpose(0, 2, 1, 3)]
  transfers between devices with their start and end apart: 12 -> 11, of which waited for: 7 -> 5; matrix products, arithmetic and copies ran while one was open for 14% -> 30% of each run, Pallas kernels for 0% -> 0%
where the time goes in v2:
time: 193 us; the launch traced here: 192 us
  waiting for transfers between devices  66.4 us (34%)
  matrix products  44.2 us (23%)
  local copies, waits for them, and re-layouts  36.8 us (19%)
  starting transfers between devices  25.5 us (13%)
  blocking collectives  13.3 us (7%)
  other arithmetic  4.8 us (2%)
    all_to_all x1, waiting for transfers between devices, body(): received = lax.all_to_all(slices, 'mom', 0, 0)  31.1 us
    dot_general x8, matrix products, stacked(): jnp.einsum('sik,sjk->sij', piece, propagators, preferred_element_type=jnp...  30.2 us
    ppermute x6, waiting for transfers between devices, shifted(): return lax.ppermute(block, 'tsink', pairs)  26.7 us
    unnamed x40, local copies, waits for them, and re-layouts  19.8 us
    all_to_all x1, blocking collectives, body(): spread = lax.all_to_all(per_diagram.reshape(n_m, -1), 'mom', 0, 0)  13.3 us
    dot_general x2, matrix products, stacked(): jnp.dot(columns, blocks.reshape(-1, block_order), preferred_element_type=...  13.3 us
    all_to_all x1, starting transfers between devices, body(): received = lax.all_to_all(slices, 'mom', 0, 0)  12.2 us
    all_to_all x1, waiting for transfers between devices, source_pieces(): received = lax.all_to_all(pieces, 'tsink', 0, 0)  7.82 us
  transfers between devices with their start and end apart: 11, of which 5 were waited for; matrix products, arithmetic and copies ran while one was open for 30% of the time, Pallas kernels for 0%

profile of v2, /device:TPU:1, one launch (start us, length us, event | category | flops | bytes accessed | tf_op | source)
XLA Modules:
  0.0 192.1 jit_solution(2859665915123479006)
XLA Ops:
  0.6 6.2 %all-to-all-start = ((bf16[8,128,1024]{2,1,0:T(8,128)(2,1)}), bf16[8,128,1024]{2,1,0:T(8,128)(2,1)}, u32[]{:S(2)}, u32[]{:S(2)}) async-start(bf16[8,128,1024]{2,1,0:T(8,128)(2,1)} %bitcast.191), calls=%async_computation | async-start | bytes 4194304 | tf_op jit(solution)/shard_map/all_to_all | solution.py:26
  6.9 5.7 %fusion.97 = (bf16[1,1,1024,1024]{3,2,1,0:T(8,128)(2,1)S(1)}, bf16[1,1,1024,1024]{3,2,1,0:T(8,128)(2,1)}, bf16[1,1,1024,1024]{3,2,1,0:T(8,128)(2,1)}, bf16[1,1,1024,1024]{3,2,1,0:T(8,128)(2,1)}) fusion(bf16[1,4,1024,1024]{3,2,1,0:T(8,128)(2,1)} %param.9), kind=kLoop, calls=%fused_computation.126 | loop fusion | bytes 16777216 | tf_op jit(solution)/shard_map/slice | solution.py:68
  12.8 2.1 %bitcast_dynamic-update-slice_fusion.15 = (bf16[1024,2048]{1,0:T(8,128)(2,1)}, bf16[1024,2048]{1,0:T(8,128)(2,1)}) fusion(bf16[1,1,1024,1024]{3,2,1,0:T(8,128)(2,1)} %get-tuple-element.5, s32[]{:T(128)S(6)} %select_n.115, s32[]{:T(128)S(6)} %select_n.107), kind=kLoop, calls=%fused_computation.88 | loop fusion | bytes 1048584
  14.9 1.9 %bitcast_dynamic-update-slice_fusion.14 = (bf16[1024,2048]{1,0:T(8,128)(2,1)}, bf16[1024,2048]{1,0:T(8,128)(2,1)}) fusion(bf16[1024,2048]{1,0:T(8,128)(2,1)} %get-tuple-element.38, bf16[1,1,1024,1024]{3,2,1,0:T(8,128)(2,1)} %get-tuple-element.5, s32[]{:T(128)S(6)} %select_n.116, bf16[1024,2048]{1,0:T(8,128)(2,1)} %get-tuple-element.39, s32[]{:T(128)S(6)} %select_n.108), kind=kLoop, calls=%fused_computation.87 | loop fusion | bytes 1048584
  16.9 2.0 %bitcast_dynamic-update-slice_fusion.13 = (bf16[1024,2048]{1,0:T(8,128)(2,1)}, bf16[1024,2048]{1,0:T(8,128)(2,1)}) fusion(bf16[1024,2048]{1,0:T(8,128)(2,1)} %get-tuple-element.36, bf16[1,1,1024,1024]{3,2,1,0:T(8,128)(2,1)} %get-tuple-element.5, s32[]{:T(128)S(6)} %select_n.117, bf16[1024,2048]{1,0:T(8,128)(2,1)} %get-tuple-element.37, s32[]{:T(128)S(6)} %select_n.110), kind=kLoop, calls=%fused_computation.86 | loop fusion | bytes 1048584
  18.8 2.0 %bitcast_dynamic-update-slice_fusion.12 = (bf16[1024,2048]{1,0:T(8,128)(2,1)}, bf16[1024,2048]{1,0:T(8,128)(2,1)}) fusion(bf16[1024,2048]{1,0:T(8,128)(2,1)} %get-tuple-element.34, bf16[1,1,1024,1024]{3,2,1,0:T(8,128)(2,1)} %get-tuple-element.5, s32[]{:T(128)S(6)} %select_n.118, bf16[1024,2048]{1,0:T(8,128)(2,1)} %get-tuple-element.35, s32[]{:T(128)S(6)} %select_n.112), kind=kLoop, calls=%fused_computation.85 | loop fusion | bytes 1048584
  20.8 1.0 bitcast_dynamic-update-slice_fusion.11
  21.8 1.0 bitcast_dynamic-update-slice_fusion.10
  22.8 1.0 bitcast_dynamic-update-slice_fusion.9
  23.8 1.0 bitcast_dynamic-update-slice_fusion.8
  24.8 1.0 bitcast_dynamic-update-slice_fusion.7
  25.8 1.0 bitcast_dynamic-update-slice_fusion.6
  26.8 1.0 bitcast_dynamic-update-slice_fusion.5
  27.8 1.0 bitcast_dynamic-update-slice_fusion.4
  28.8 1.0 bitcast_dynamic-update-slice_fusion.3
  29.7 7.8 %all-to-all-done = bf16[8,128,1024]{2,1,0:T(8,128)(2,1)} async-done(((bf16[8,128,1024]{2,1,0:T(8,128)(2,1)}), bf16[8,128,1024]{2,1,0:T(8,128)(2,1)}, u32[]{:S(2)}, u32[]{:S(2)}) %all-to-all-start) | async-done | bytes 2097184 | tf_op jit(solution)/shard_map/all_to_all | solution.py:26
  37.6 2.2 %gather_fusion = bf16[4,128,1024]{2,1,0:T(8,128)(2,1)S(1)} fusion(bf16[8,128,1024]{2,1,0:T(8,128)(2,1)} %all-to-all-done, s32[1024]{0:T(1024)S(1)} %pad_clamp_fusion.2), kind=kCustom, calls=%fused_computation | custom fusion | bytes 2097168 | tf_op jit(solution)/shard_map/gather | solution.py:27
  39.9 1.0 bitcast_dynamic-update-slice_fusion.2
  40.9 1.0 bitcast_dynamic-update-slice_fusion.1
  41.9 1.0 bitcast_dynamic-update-slice_fusion
  42.9 1.4 collective-permute-start.1
  44.3 6.4 %fusion.61 = bf16[4,1,128,1024]{3,2,0,1:T(8,128)(2,1)S(1)} fusion(bf16[4,128,1024]{2,1,0:T(8,128)(2,1)S(1)} %gather_fusion, bf16[1,4,1024,1024]{3,2,1,0:T(8,128)(2,1)} %param.9), kind=kOutput, calls=%fused_computation.40 | convolution fusion | flops 1074266112 | bytes 10485760 | tf_op jit(solution)/shard_map/sik,sjk->sij/dot_general | solution.py:76
  50.8 12.2 %collective-permute-done.2 = bf16[4,128,1024]{2,1,0:T(8,128)(2,1)S(1)} collective-permute-done((bf16[4,128,1024]{2,1,0:T(8,128)(2,1)S(1)}, bf16[4,128,1024]{2,1,0:T(8,128)(2,1)S(1)}, u32[]{:S(2)}, u32[]{:S(2)}) %collective-permute-start.2) | collective-permute-done | bytes 1048608 | tf_op jit(solution)/shard_map/ppermute | solution.py:12
  63.0 6.3 %fusion.52 = bf16[4,1,128,1024]{3,2,0,1:T(8,128)(2,1)S(1)} fusion(bf16[4,128,1024]{2,1,0:T(8,128)(2,1)S(1)} %collective-permute-done.2, bf16[1,4,1024,1024]{3,2,1,0:T(8,128)(2,1)} %param.9), kind=kOutput, calls=%fused_computation.37 | convolution fusion | flops 1074266112 | bytes 10485760 | tf_op jit(solution)/shard_map/sik,sjk->sij/dot_general | solution.py:76
  69.3 2.9 %fusion.55 = bf16[4,1,128,1024]{3,2,0,1:T(8,128)(2,1)S(1)} fusion(bf16[4,128,1024]{2,1,0:T(8,128)(2,1)S(1)} %collective-permute-done.1, bf16[1,4,1024,1024]{3,2,1,0:T(8,128)(2,1)S(1)} %bitcast.181), kind=kOutput, calls=%fused_computation.38 | convolution fusion | flops 1074266112 | bytes 10485760 | tf_op jit(solution)/shard_map/sik,sjk->sij/dot_general | solution.py:76
  72.2 2.9 %fusion.58 = bf16[4,1,128,1024]{3,2,0,1:T(8,128)(2,1)S(1)} fusion(bf16[4,128,1024]{2,1,0:T(8,128)(2,1)S(1)} %collective-permute-done, bf16[1,4,1024,1024]{3,2,1,0:T(8,128)(2,1)S(1)} %bitcast.181), kind=kOutput, calls=%fused_computation.39 | convolution fusion | flops 1074266112 | bytes 10485760 | tf_op jit(solution)/shard_map/sik,sjk->sij/dot_general | solution.py:76
  76.7 2.7 %collective-permute-start.4 = (bf16[2,4,64,1024]{3,2,1,0:T(8,128)(2,1)S(1)}, bf16[2,4,64,1024]{3,2,1,0:T(8,128)(2,1)S(1)}, u32[]{:S(2)}, u32[]{:S(2)}) collective-permute-start(bf16[2,4,64,1024]{3,2,1,0:T(8,128)(2,1)S(1)} %get-tuple-element.49), channel_id=1, source_target_pairs={{0,96},{16,112},{32,0},{48,16},{64,32},{80,48},{96,64},{112,80},{1... | collective-permute-start | bytes 3145736 | tf_op jit(solution)/shard_map/ppermute | solution.py:12
  79.4 6.3 %fusion.99 = f32[1024,1024]{1,0:T(8,128)S(1)} fusion(bf16[1024,2048]{1,0:T(8,128)(2,1)} %get-tuple-element.9, bf16[2048,1024]{1,0:T(8,128)(2,1)S(1)} %bitcast.189), kind=kOutput, calls=%fused_computation.128 | convolution fusion | flops 4294967296 | bytes 12582912 | tf_op jit(solution)/shard_map/dot_general | solution.py:83
  85.8 14.5 %collective-permute-done.3 = bf16[2,4,64,1024]{3,2,1,0:T(8,128)(2,1)S(1)} collective-permute-done((bf16[2,4,64,1024]{3,2,1,0:T(8,128)(2,1)S(1)}, bf16[2,4,64,1024]{3,2,1,0:T(8,128)(2,1)S(1)}, u32[]{:S(2)}, u32[]{:S(2)}) %collective-permute-start.3) | collective-permute-done | bytes 1048608 | tf_op jit(solution)/shard_map/ppermute | solution.py:12
  100.5 2.7 %collective-permute-start.7 = (bf16[4,32,1024]{2,1,0:T(8,128)(2,1)S(1)}, bf16[4,32,1024]{2,1,0:T(8,128)(2,1)S(1)}, u32[]{:S(2)}, u32[]{:S(2)}) collective-permute-start(bf16[4,32,1024]{2,1,0:T(8,128)(2,1)S(1)} %slice.133), channel_id=1, source_target_pairs={{0,96},{16,112},{32,0},{48,16},{64,32},{80,48},{96,64},{112,80},{1... | collective-permute-start | bytes 786440 | tf_op jit(solution)/shard_map/ppermute | solution.py:12
  103.3 2.9 %fusion.43 = bf16[4,1,128,1024]{3,2,0,1:T(8,128)(2,1)S(1)} fusion(bf16[1,4,1024,1024]{3,2,1,0:T(8,128)(2,1)S(1)} %bitcast.181, bf16[4,64,1024]{2,1,0:T(8,128)(2,1)S(1)} %get-tuple-element.43, bf16[4,64,1024]{2,1,0:T(8,128)(2,1)S(1)} %get-tuple-element.46), kind=kOutput, calls=%fused_computation.34 | convolution fusion | flops 1076363264 | bytes 10485760 | tf_op jit(solution)/shard_map/sik,sjk->sij/dot_general | solution.py:76
  106.2 2.9 %fusion.46 = bf16[4,1,128,1024]{3,2,0,1:T(8,128)(2,1)S(1)} fusion(bf16[1,4,1024,1024]{3,2,1,0:T(8,128)(2,1)S(1)} %bitcast.181, bf16[4,64,1024]{2,1,0:T(8,128)(2,1)S(1)} %get-tuple-element.42, bf16[4,64,1024]{2,1,0:T(8,128)(2,1)S(1)} %get-tuple-element.41), kind=kOutput, calls=%fused_computation.35 | convolution fusion | flops 1076363264 | bytes 10485760 | tf_op jit(solution)/shard_map/sik,sjk->sij/dot_general | solution.py:76
  109.2 2.9 %fusion.49 = bf16[4,1,128,1024]{3,2,0,1:T(8,128)(2,1)S(1)} fusion(bf16[1,4,1024,1024]{3,2,1,0:T(8,128)(2,1)S(1)} %bitcast.181, bf16[4,64,1024]{2,1,0:T(8,128)(2,1)S(1)} %get-tuple-element.47, bf16[4,64,1024]{2,1,0:T(8,128)(2,1)S(1)} %get-tuple-element.40), kind=kOutput, calls=%fused_computation.36 | convolution fusion | flops 1076363264 | bytes 10485760 | tf_op jit(solution)/shard_map/sik,sjk->sij/dot_general | solution.py:76
  112.1 0.8 collective-permute-done.8
  112.9 2.9 %fusion.40 = bf16[4,1,128,1024]{3,2,0,1:T(8,128)(2,1)S(1)} fusion(bf16[1,4,1024,1024]{3,2,1,0:T(8,128)(2,1)S(1)} %bitcast.181, bf16[4,64,1024]{2,1,0:T(8,128)(2,1)S(1)} %collective-permute-done.8, bf16[4,32,1024]{2,1,0:T(8,128)(2,1)S(1)} %collective-permute-done.7, bf16[4,32,1024]{2,1,0:T(8,128)(2,1)S(1)} %collective-permute-done.6), kind=kOutput, calls=%fused_computation.33 | convolution fusion | flops 1077411840 | bytes 10485760 | tf_op jit(solution)/shard_map/sik,sjk->sij/dot_general | solution.py:76
  115.8 0.8 pad_maximum_fusion.1
  117.3 7.0 %add_convert_fusion = bf16[1024,1024]{1,0:T(8,128)(2,1)S(1)} fusion(f32[1024,1024]{1,0:T(8,128)S(1)} %fusion.99, bf16[1024,2048]{1,0:T(8,128)(2,1)} %get-tuple-element.8, bf16[2048,1024]{1,0:T(8,128)(2,1)S(1)} %bitcast.190), kind=kOutput, calls=%fused_computation.22 | convolution fusion | flops 4297064448 | bytes 14680064 | tf_op jit(solution)/shard_map/dot_general | solution.py:83
  124.2 0.6 copy.31
  125.6 1.8 gather_fusion.1
  127.4 0.8 gather_fusion.2
  128.2 1.4 copy.24
  129.9 0.9 fusion.64
  130.9 1.7 pad_maximum_fusion.2
  132.6 12.2 %all-to-all-start.1 = ((bf16[16,576,128]{2,1,0:T(8,128)(2,1)}), bf16[16,576,128]{2,1,0:T(8,128)(2,1)S(1)}, u32[]{:S(2)}, u32[]{:S(2)}) async-start(bf16[16,576,128]{2,1,0:T(8,128)(2,1)} %pad_maximum_fusion.2), calls=%async_computation.1 | async-start | bytes 4718592 | tf_op jit(solution)/shard_map/all_to_all | solution.py:108
  144.8 31.1 %all-to-all-done.1 = bf16[16,576,128]{2,1,0:T(8,128)(2,1)S(1)} async-done(((bf16[16,576,128]{2,1,0:T(8,128)(2,1)}), bf16[16,576,128]{2,1,0:T(8,128)(2,1)S(1)}, u32[]{:S(2)}, u32[]{:S(2)}) %all-to-all-start.1) | async-done | bytes 2359328 | tf_op jit(solution)/shard_map/all_to_all | solution.py:108
  176.0 0.7 fusion.68
  176.8 1.3 gather_fusion.3
  178.2 13.3 %all_to_all.19 = f32[16,1,8]{2,1,0:T(1,128)S(1)} all-to-all(f32[16,1,8]{2,1,0:T(1,128)S(1)} %bitcast.194), channel_id=1, replica_groups=mesh['tsink'=8,'mom'=16] {'mom'}, dimensions={0} | all-to-all | bytes 1024 | tf_op jit(solution)/shard_map/all_to_all | solution.py:116
  (64 shorter events, 4.7 us)
Async XLA Ops:
  0.6 36.9 %all-to-all-start = ((bf16[8,128,1024]{2,1,0:T(8,128)(2,1)}), bf16[8,128,1024]{2,1,0:T(8,128)(2,1)}, u32[]{:S(2)}, u32[]{:S(2)}) async-start(bf16[8,128,1024]{2,1,0:T(8,128)(2,1)} %bitcast.191), calls=%async_computation | async-start | bytes 4194304 | tf_op jit(solution)/shard_map/all_to_all | solution.py:26
  6.8 5.7 %copy-start.9 = (s32[4]{0:T(128)S(1)}, s32[4]{0:T(128)}, u32[]{:S(2)}) copy-start(s32[4]{0:T(128)} %param.11) | copy-start | bytes 52
  6.8 5.7 %copy-start.7 = (pred[36]{0:T(512)(128)(4,1)S(1)}, pred[36]{0:T(512)(128)(4,1)}, u32[]{:S(2)}) copy-start(pred[36]{0:T(512)(128)(4,1)} %constant.109) | copy-start | bytes 112
  12.8 8.0 %copy-start.1 = (bf16[1,1,1024,1024]{3,2,1,0:T(8,128)(2,1)S(1)}, bf16[1,1,1024,1024]{3,2,1,0:T(8,128)(2,1)}, u32[]{:S(2)}) copy-start(bf16[1,1,1024,1024]{3,2,1,0:T(8,128)(2,1)} %get-tuple-element.4) | copy-start | bytes 6291460
  12.8 11.9 %copy-start = (bf16[1,1,1024,1024]{3,2,1,0:T(8,128)(2,1)S(1)}, bf16[1,1,1024,1024]{3,2,1,0:T(8,128)(2,1)}, u32[]{:S(2)}) copy-start(bf16[1,1,1024,1024]{3,2,1,0:T(8,128)(2,1)} %get-tuple-element.3) | copy-start | bytes 6291460
  23.8 16.1 %copy-start.5 = (s32[36]{0:T(128)S(1)}, s32[36]{0:T(128)}, u32[]{:S(2)}) copy-start(s32[36]{0:T(128)} %constant.124) | copy-start | bytes 436
  23.8 16.1 %copy-start.6 = (s32[36]{0:T(128)S(1)}, s32[36]{0:T(128)}, u32[]{:S(2)}) copy-start(s32[36]{0:T(128)} %constant.125) | copy-start | bytes 436
  39.8 23.2 %collective-permute-start.2 = (bf16[4,128,1024]{2,1,0:T(8,128)(2,1)S(1)}, bf16[4,128,1024]{2,1,0:T(8,128)(2,1)S(1)}, u32[]{:S(2)}, u32[]{:S(2)}) collective-permute-start(bf16[4,128,1024]{2,1,0:T(8,128)(2,1)S(1)} %gather_fusion), channel_id=1, source_target_pairs={{0,96},{16,112},{32,0},{48,16},{64,32},{80,48},{96,64},{112,80},{1... | collective-permute-start | bytes 3145736 | tf_op jit(solution)/shard_map/ppermute | solution.py:12
  42.9 26.4 %collective-permute-start.1 = (bf16[4,128,1024]{2,1,0:T(8,128)(2,1)S(1)}, bf16[4,128,1024]{2,1,0:T(8,128)(2,1)S(1)}, u32[]{:S(2)}, u32[]{:S(2)}) collective-permute-start(bf16[4,128,1024]{2,1,0:T(8,128)(2,1)S(1)} %gather_fusion), channel_id=1, source_target_pairs={{0,32},{16,48},{32,64},{48,80},{64,96},{80,112},{96,0},{112,16},{1... | collective-permute-start | bytes 3145736 | tf_op jit(solution)/shard_map/ppermute | solution.py:12
  44.3 27.9 %collective-permute-start = (bf16[4,128,1024]{2,1,0:T(8,128)(2,1)S(1)}, bf16[4,128,1024]{2,1,0:T(8,128)(2,1)S(1)}, u32[]{:S(2)}, u32[]{:S(2)}) collective-permute-start(bf16[4,128,1024]{2,1,0:T(8,128)(2,1)S(1)} %gather_fusion), channel_id=1, source_target_pairs={{0,16},{16,0},{32,48},{48,32},{64,80},{80,64},{96,112},{112,96},{1... | collective-permute-start | bytes 3145736 | tf_op jit(solution)/shard_map/ppermute | solution.py:16
  44.3 25.0 %slice-start = ((s8[8388608]{0:T(1024)(128)(4,1)}), s8[4194304]{0:T(1024)(128)(4,1)S(1)}, s32[]{:S(2)}) async-start(s8[8388608]{0:T(1024)(128)(4,1)} %bitcast.180), calls=%async_computation.3 | async-start | bytes 8388608
  50.8 18.5 %slice-start.1 = ((s8[8388608]{0:T(1024)(128)(4,1)}), s8[4194304]{0:T(1024)(128)(4,1)S(1)}, s32[]{:S(2)}) async-start(s8[8388608]{0:T(1024)(128)(4,1)} %bitcast.180), calls=%async_computation.4 | async-start | bytes 8388608
  76.7 23.6 %collective-permute-start.3 = (bf16[2,4,64,1024]{3,2,1,0:T(8,128)(2,1)S(1)}, bf16[2,4,64,1024]{3,2,1,0:T(8,128)(2,1)S(1)}, u32[]{:S(2)}, u32[]{:S(2)}) collective-permute-start(bf16[2,4,64,1024]{3,2,1,0:T(8,128)(2,1)S(1)} %get-tuple-element.50), channel_id=1, source_target_pairs={{0,32},{16,48},{32,64},{48,80},{64,96},{80,112},{96,0},{112,16},{1... | collective-permute-start | bytes 3145736 | tf_op jit(solution)/shard_map/ppermute | solution.py:12
  76.7 23.7 %collective-permute-start.4 = (bf16[2,4,64,1024]{3,2,1,0:T(8,128)(2,1)S(1)}, bf16[2,4,64,1024]{3,2,1,0:T(8,128)(2,1)S(1)}, u32[]{:S(2)}, u32[]{:S(2)}) collective-permute-start(bf16[2,4,64,1024]{3,2,1,0:T(8,128)(2,1)S(1)} %get-tuple-element.49), channel_id=1, source_target_pairs={{0,96},{16,112},{32,0},{48,16},{64,32},{80,48},{96,64},{112,80},{1... | collective-permute-start | bytes 3145736 | tf_op jit(solution)/shard_map/ppermute | solution.py:12
  79.4 23.9 %collective-permute-start.5 = (bf16[2,4,64,1024]{3,2,1,0:T(8,128)(2,1)S(1)}, bf16[2,4,64,1024]{3,2,1,0:T(8,128)(2,1)S(1)}, u32[]{:S(2)}, u32[]{:S(2)}) collective-permute-start(bf16[2,4,64,1024]{3,2,1,0:T(8,128)(2,1)S(1)} %get-tuple-element.48), channel_id=1, source_target_pairs={{0,16},{16,0},{32,48},{48,32},{64,80},{80,64},{96,112},{112,96},{1... | collective-permute-start | bytes 3145736 | tf_op jit(solution)/shard_map/ppermute | solution.py:16
  100.3 11.8 %collective-permute-start.6 = (bf16[4,32,1024]{2,1,0:T(8,128)(2,1)S(1)}, bf16[4,32,1024]{2,1,0:T(8,128)(2,1)S(1)}, u32[]{:S(2)}, u32[]{:S(2)}) collective-permute-start(bf16[4,32,1024]{2,1,0:T(8,128)(2,1)S(1)} %slice.132), channel_id=1, source_target_pairs={{0,32},{16,48},{32,64},{48,80},{64,96},{80,112},{96,0},{112,16},{1... | collective-permute-start | bytes 786440 | tf_op jit(solution)/shard_map/ppermute | solution.py:12
  100.5 11.6 %collective-permute-start.7 = (bf16[4,32,1024]{2,1,0:T(8,128)(2,1)S(1)}, bf16[4,32,1024]{2,1,0:T(8,128)(2,1)S(1)}, u32[]{:S(2)}, u32[]{:S(2)}) collective-permute-start(bf16[4,32,1024]{2,1,0:T(8,128)(2,1)S(1)} %slice.133), channel_id=1, source_target_pairs={{0,96},{16,112},{32,0},{48,16},{64,32},{80,48},{96,64},{112,80},{1... | collective-permute-start | bytes 786440 | tf_op jit(solution)/shard_map/ppermute | solution.py:12
  103.3 9.6 %collective-permute-start.8 = (bf16[4,64,1024]{2,1,0:T(8,128)(2,1)S(1)}, bf16[4,64,1024]{2,1,0:T(8,128)(2,1)S(1)}, u32[]{:S(2)}, u32[]{:S(2)}) collective-permute-start(bf16[4,64,1024]{2,1,0:T(8,128)(2,1)S(1)} %get-tuple-element.47), channel_id=1, source_target_pairs={{0,16},{16,0},{32,48},{48,32},{64,80},{80,64},{96,112},{112,96},{1... | collective-permute-start | bytes 1572872 | tf_op jit(solution)/shard_map/ppermute | solution.py:16
  124.2 1.4 copy-start.4
  128.2 1.7 copy-start.2
  129.6 1.3 copy-start.3
  130.9 13.9 %copy-start.8 = (s32[128,2]{0,1:T(2,128)S(1)}, s32[128,2]{0,1:T(2,128)}, u32[]{:S(2)}) copy-start(s32[128,2]{0,1:T(2,128)} %param.12) | copy-start | bytes 3076
  132.6 43.3 %all-to-all-start.1 = ((bf16[16,576,128]{2,1,0:T(8,128)(2,1)}), bf16[16,576,128]{2,1,0:T(8,128)(2,1)S(1)}, u32[]{:S(2)}, u32[]{:S(2)}) async-start(bf16[16,576,128]{2,1,0:T(8,128)(2,1)} %pad_maximum_fusion.2), calls=%async_computation.1 | async-start | bytes 4718592 | tf_op jit(solution)/shard_map/all_to_all | solution.py:108

commit v3 on v2

--- a/solution.py
+++ b/solution.py
@@ -66,8 +66,8 @@
         columns = jnp.concatenate(
             [
                 lax.dynamic_slice_in_dim(propagators[source], origin * rows, rows, 1)
+                for origin, _ in group
                 for source in range(NSRC)
-                for origin, _ in group
             ],
             axis=1,
         )
@@ -77,8 +77,7 @@
                     "sik,sjk->sij", piece, propagators, preferred_element_type=jnp.float32
                 ).astype(jnp.bfloat16)
                 for _, piece in group
-            ],
-            axis=1,
+            ]
         )
         return jnp.dot(
             columns, blocks.reshape(-1, block_order), preferred_element_type=jnp.float32

time: 193 us -> 182 us (0.943)
  waiting for transfers between devices: 66.4 us -> 57.8 us
  matrix products: 44.2 us -> 41.3 us
    ppermute x6, waiting for transfers between devices: 26.7 us -> 19.4 us  [shifted(): return lax.ppermute(block, 'tsink', pairs)]
    dot_general x8, matrix products: 30.2 us -> 27.2 us  [stacked(): jnp.einsum('sik,sjk->sij', piece, propagators, preferred_element_type=jnp...]
    unnamed x40 -> x42, local copies, waits for them, and re-layouts: 19.8 us -> 20.8 us
  transfers between devices with their start and end apart: 11 -> 11, of which waited for: 5 -> 6; matrix products, arithmetic and copies ran while one was open for 30% -> 32% of each run, Pallas kernels for 0% -> 0%
where the time goes in v3:
time: 182 us; the launch traced here: 181 us
  waiting for transfers between devices  57.8 us (32%)
  matrix products  41.3 us (23%)
  local copies, waits for them, and re-layouts  36.8 us (20%)
  starting transfers between devices  26.4 us (15%)
  blocking collectives  13.3 us (7%)
  other arithmetic  4.79 us (3%)
    all_to_all x1, waiting for transfers between devices, body(): received = lax.all_to_all(slices, 'mom', 0, 0)  31.1 us
    dot_general x8, matrix products, stacked(): jnp.einsum('sik,sjk->sij', piece, propagators, preferred_element_type=jnp...  27.2 us
    unnamed x42, local copies, waits for them, and re-layouts  20.8 us
    ppermute x6, waiting for transfers between devices, shifted(): return lax.ppermute(block, 'tsink', pairs)  19.4 us
    dot_general x2, matrix products, stacked(): jnp.dot(columns, blocks.reshape(-1, block_order), preferred_element_type=...  13.4 us
    all_to_all x1, blocking collectives, body(): spread = lax.all_to_all(per_diagram.reshape(n_m, -1), 'mom', 0, 0)  13.3 us
    all_to_all x1, starting transfers between devices, body(): received = lax.all_to_all(slices, 'mom', 0, 0)  12.7 us
    ppermute x6, starting transfers between devices, shifted(): return lax.ppermute(block, 'tsink', pairs)  7.06 us
  transfers between devices with their start and end apart: 11, of which 6 were waited for; matrix products, arithmetic and copies ran while one was open for 32% of the time, Pallas kernels for 0%

profile of v3, /device:TPU:1, one launch (start us, length us, event | category | flops | bytes accessed | tf_op | source)
XLA Modules:
  0.0 181.4 jit_solution(5261776593860011261)
XLA Ops:
  0.6 6.2 %all-to-all-start = ((bf16[8,128,1024]{2,1,0:T(8,128)(2,1)}), bf16[8,128,1024]{2,1,0:T(8,128)(2,1)}, u32[]{:S(2)}, u32[]{:S(2)}) async-start(bf16[8,128,1024]{2,1,0:T(8,128)(2,1)} %bitcast.191), calls=%async_computation | async-start | bytes 4194304 | tf_op jit(solution)/shard_map/all_to_all | solution.py:26
  6.9 5.8 %fusion.97 = (bf16[1,1,1024,1024]{3,2,1,0:T(8,128)(2,1)S(1)}, bf16[1,1,1024,1024]{3,2,1,0:T(8,128)(2,1)}, bf16[1,1,1024,1024]{3,2,1,0:T(8,128)(2,1)}, bf16[1,1,1024,1024]{3,2,1,0:T(8,128)(2,1)}) fusion(bf16[1,4,1024,1024]{3,2,1,0:T(8,128)(2,1)} %param.9), kind=kLoop, calls=%fused_computation.126 | loop fusion | bytes 16777216 | tf_op jit(solution)/shard_map/slice | solution.py:68
  12.9 2.1 %bitcast_dynamic-update-slice_fusion.15 = (bf16[1024,2048]{1,0:T(8,128)(2,1)}, bf16[1024,2048]{1,0:T(8,128)(2,1)}) fusion(bf16[1,1,1024,1024]{3,2,1,0:T(8,128)(2,1)} %get-tuple-element.5, s32[]{:T(128)S(6)} %select_n.115, s32[]{:T(128)S(6)} %select_n.107), kind=kLoop, calls=%fused_computation.88 | loop fusion | bytes 1048584
  15.0 2.0 %bitcast_dynamic-update-slice_fusion.14 = (bf16[1024,2048]{1,0:T(8,128)(2,1)}, bf16[1024,2048]{1,0:T(8,128)(2,1)}) fusion(bf16[1024,2048]{1,0:T(8,128)(2,1)} %get-tuple-element.38, bf16[1,1,1024,1024]{3,2,1,0:T(8,128)(2,1)} %get-tuple-element.4, s32[]{:T(128)S(6)} %select_n.115, bf16[1024,2048]{1,0:T(8,128)(2,1)} %get-tuple-element.39, s32[]{:T(128)S(6)} %select_n.107), kind=kLoop, calls=%fused_computation.87 | loop fusion | bytes 1048584
  17.0 2.0 %bitcast_dynamic-update-slice_fusion.13 = (bf16[1024,2048]{1,0:T(8,128)(2,1)}, bf16[1024,2048]{1,0:T(8,128)(2,1)}) fusion(bf16[1024,2048]{1,0:T(8,128)(2,1)} %get-tuple-element.36, bf16[1,1,1024,1024]{3,2,1,0:T(8,128)(2,1)} %get-tuple-element.3, s32[]{:T(128)S(6)} %select_n.115, bf16[1024,2048]{1,0:T(8,128)(2,1)} %get-tuple-element.37, s32[]{:T(128)S(6)} %select_n.107), kind=kLoop, calls=%fused_computation.86 | loop fusion | bytes 1048584
  19.0 1.0 bitcast_dynamic-update-slice_fusion.12
  19.9 1.9 %bitcast_dynamic-update-slice_fusion.11 = (bf16[1024,2048]{1,0:T(8,128)(2,1)}, bf16[1024,2048]{1,0:T(8,128)(2,1)}) fusion(bf16[1024,2048]{1,0:T(8,128)(2,1)} %get-tuple-element.32, bf16[1,1,1024,1024]{3,2,1,0:T(8,128)(2,1)} %get-tuple-element.5, s32[]{:T(128)S(6)} %select_n.116, bf16[1024,2048]{1,0:T(8,128)(2,1)} %get-tuple-element.33, s32[]{:T(128)S(6)} %select_n.108), kind=kLoop, calls=%fused_computation.84 | loop fusion | bytes 1048584
  21.8 1.0 bitcast_dynamic-update-slice_fusion.10
  22.8 1.0 bitcast_dynamic-update-slice_fusion.9
  23.8 1.0 bitcast_dynamic-update-slice_fusion.8
  24.8 1.0 bitcast_dynamic-update-slice_fusion.7
  25.8 1.0 bitcast_dynamic-update-slice_fusion.6
  26.8 1.0 bitcast_dynamic-update-slice_fusion.5
  27.8 1.0 bitcast_dynamic-update-slice_fusion.4
  28.9 1.0 bitcast_dynamic-update-slice_fusion.3
  29.9 1.0 bitcast_dynamic-update-slice_fusion.2
  30.9 6.7 %all-to-all-done = bf16[8,128,1024]{2,1,0:T(8,128)(2,1)} async-done(((bf16[8,128,1024]{2,1,0:T(8,128)(2,1)}), bf16[8,128,1024]{2,1,0:T(8,128)(2,1)}, u32[]{:S(2)}, u32[]{:S(2)}) %all-to-all-start) | async-done | bytes 2097184 | tf_op jit(solution)/shard_map/all_to_all | solution.py:26
  37.6 2.2 %gather_fusion = bf16[4,128,1024]{2,1,0:T(8,128)(2,1)S(1)} fusion(bf16[8,128,1024]{2,1,0:T(8,128)(2,1)} %all-to-all-done, s32[1024]{0:T(1024)S(1)} %pad_clamp_fusion.2), kind=kCustom, calls=%fused_computation | custom fusion | bytes 2097168 | tf_op jit(solution)/shard_map/gather | solution.py:27
  39.9 1.9 %bitcast_dynamic-update-slice_fusion.1 = (bf16[1024,2048]{1,0:T(8,128)(2,1)}, bf16[1024,2048]{1,0:T(8,128)(2,1)}) fusion(bf16[1024,2048]{1,0:T(8,128)(2,1)} %get-tuple-element.12, bf16[1,1,1024,1024]{3,2,1,0:T(8,128)(2,1)} %get-tuple-element.3, s32[]{:T(128)S(6)} %select_n.118, bf16[1024,2048]{1,0:T(8,128)(2,1)} %get-tuple-element.13, s32[]{:T(128)S(6)} %select_n.112), kind=kLoop, calls=%fused_computation.74 | loop fusion | bytes 1048584
  41.8 1.4 collective-permute-start.1
  43.3 1.0 bitcast_dynamic-update-slice_fusion
  44.3 6.8 %fusion.61 = bf16[1,4,128,1024]{3,2,1,0:T(8,128)(2,1)S(1)} fusion(bf16[4,128,1024]{2,1,0:T(8,128)(2,1)S(1)} %gather_fusion, bf16[1,4,1024,1024]{3,2,1,0:T(8,128)(2,1)} %param.9), kind=kOutput, calls=%fused_computation.40 | convolution fusion | flops 1074266112 | bytes 10485760 | tf_op jit(solution)/shard_map/sik,sjk->sij/dot_general | solution.py:76
  51.0 12.0 %collective-permute-done.2 = bf16[4,128,1024]{2,1,0:T(8,128)(2,1)S(1)} collective-permute-done((bf16[4,128,1024]{2,1,0:T(8,128)(2,1)S(1)}, bf16[4,128,1024]{2,1,0:T(8,128)(2,1)S(1)}, u32[]{:S(2)}, u32[]{:S(2)}) %collective-permute-start.2) | collective-permute-done | bytes 1048608 | tf_op jit(solution)/shard_map/ppermute | solution.py:12
  63.0 3.1 %collective-permute-done.1 = bf16[4,128,1024]{2,1,0:T(8,128)(2,1)S(1)} collective-permute-done((bf16[4,128,1024]{2,1,0:T(8,128)(2,1)S(1)}, bf16[4,128,1024]{2,1,0:T(8,128)(2,1)S(1)}, u32[]{:S(2)}, u32[]{:S(2)}) %collective-permute-start.1) | collective-permute-done | bytes 1048608 | tf_op jit(solution)/shard_map/ppermute | solution.py:12
  67.5 2.4 %collective-permute-start.4 = (bf16[2,4,64,1024]{3,2,1,0:T(8,128)(2,1)S(1)}, bf16[2,4,64,1024]{3,2,1,0:T(8,128)(2,1)S(1)}, u32[]{:S(2)}, u32[]{:S(2)}) collective-permute-start(bf16[2,4,64,1024]{3,2,1,0:T(8,128)(2,1)S(1)} %get-tuple-element.49), channel_id=1, source_target_pairs={{0,96},{16,112},{32,0},{48,16},{64,32},{80,48},{96,64},{112,80},{1... | collective-permute-start | bytes 3145736 | tf_op jit(solution)/shard_map/ppermute | solution.py:12
  70.0 2.9 %fusion.52 = bf16[1,4,128,1024]{3,2,1,0:T(8,128)(2,1)S(1)} fusion(bf16[4,128,1024]{2,1,0:T(8,128)(2,1)S(1)} %collective-permute-done.2, bf16[1,4,1024,1024]{3,2,1,0:T(8,128)(2,1)S(1)} %bitcast.181), kind=kOutput, calls=%fused_computation.37 | convolution fusion | flops 1074266112 | bytes 10485760 | tf_op jit(solution)/shard_map/sik,sjk->sij/dot_general | solution.py:76
  73.0 3.0 %fusion.55 = bf16[1,4,128,1024]{3,2,1,0:T(8,128)(2,1)S(1)} fusion(bf16[4,128,1024]{2,1,0:T(8,128)(2,1)S(1)} %collective-permute-done.1, bf16[1,4,1024,1024]{3,2,1,0:T(8,128)(2,1)S(1)} %bitcast.181), kind=kOutput, calls=%fused_computation.38 | convolution fusion | flops 1074266112 | bytes 10485760 | tf_op jit(solution)/shard_map/sik,sjk->sij/dot_general | solution.py:76
  75.9 2.9 %fusion.58 = bf16[1,4,128,1024]{3,2,1,0:T(8,128)(2,1)S(1)} fusion(bf16[4,128,1024]{2,1,0:T(8,128)(2,1)S(1)} %collective-permute-done, bf16[1,4,1024,1024]{3,2,1,0:T(8,128)(2,1)S(1)} %bitcast.181), kind=kOutput, calls=%fused_computation.39 | convolution fusion | flops 1074266112 | bytes 10485760 | tf_op jit(solution)/shard_map/sik,sjk->sij/dot_general | solution.py:76
  79.4 6.4 %fusion.99 = f32[1024,1024]{1,0:T(8,128)S(1)} fusion(bf16[1024,2048]{1,0:T(8,128)(2,1)} %get-tuple-element.9, bf16[2048,1024]{1,0:T(8,128)(2,1)S(1)} %bitcast.190), kind=kOutput, calls=%fused_computation.128 | convolution fusion | flops 4294967296 | bytes 12582912 | tf_op jit(solution)/shard_map/dot_general | solution.py:82
  85.8 4.3 %collective-permute-done.3 = bf16[2,4,64,1024]{3,2,1,0:T(8,128)(2,1)S(1)} collective-permute-done((bf16[2,4,64,1024]{3,2,1,0:T(8,128)(2,1)S(1)}, bf16[2,4,64,1024]{3,2,1,0:T(8,128)(2,1)S(1)}, u32[]{:S(2)}, u32[]{:S(2)}) %collective-permute-start.3) | collective-permute-done | bytes 1048608 | tf_op jit(solution)/shard_map/ppermute | solution.py:12
  90.4 2.7 %collective-permute-start.7 = (bf16[4,32,1024]{2,1,0:T(8,128)(2,1)S(1)}, bf16[4,32,1024]{2,1,0:T(8,128)(2,1)S(1)}, u32[]{:S(2)}, u32[]{:S(2)}) collective-permute-start(bf16[4,32,1024]{2,1,0:T(8,128)(2,1)S(1)} %slice.133), channel_id=1, source_target_pairs={{0,96},{16,112},{32,0},{48,16},{64,32},{80,48},{96,64},{112,80},{1... | collective-permute-start | bytes 786440 | tf_op jit(solution)/shard_map/ppermute | solution.py:12
  93.5 2.9 %fusion.43 = bf16[1,4,128,1024]{3,2,1,0:T(8,128)(2,1)S(1)} fusion(bf16[1,4,1024,1024]{3,2,1,0:T(8,128)(2,1)S(1)} %bitcast.181, bf16[4,64,1024]{2,1,0:T(8,128)(2,1)S(1)} %get-tuple-element.43, bf16[4,64,1024]{2,1,0:T(8,128)(2,1)S(1)} %get-tuple-element.46), kind=kOutput, calls=%fused_computation.34 | convolution fusion | flops 1076363264 | bytes 10485760 | tf_op jit(solution)/shard_map/sik,sjk->sij/dot_general | solution.py:76
  96.5 2.9 %fusion.46 = bf16[1,4,128,1024]{3,2,1,0:T(8,128)(2,1)S(1)} fusion(bf16[1,4,1024,1024]{3,2,1,0:T(8,128)(2,1)S(1)} %bitcast.181, bf16[4,64,1024]{2,1,0:T(8,128)(2,1)S(1)} %get-tuple-element.42, bf16[4,64,1024]{2,1,0:T(8,128)(2,1)S(1)} %get-tuple-element.41), kind=kOutput, calls=%fused_computation.35 | convolution fusion | flops 1076363264 | bytes 10485760 | tf_op jit(solution)/shard_map/sik,sjk->sij/dot_general | solution.py:76
  99.4 2.9 %fusion.49 = bf16[1,4,128,1024]{3,2,1,0:T(8,128)(2,1)S(1)} fusion(bf16[1,4,1024,1024]{3,2,1,0:T(8,128)(2,1)S(1)} %bitcast.181, bf16[4,64,1024]{2,1,0:T(8,128)(2,1)S(1)} %get-tuple-element.47, bf16[4,64,1024]{2,1,0:T(8,128)(2,1)S(1)} %get-tuple-element.40), kind=kOutput, calls=%fused_computation.36 | convolution fusion | flops 1076363264 | bytes 10485760 | tf_op jit(solution)/shard_map/sik,sjk->sij/dot_general | solution.py:76
  102.3 2.9 %fusion.40 = bf16[1,4,128,1024]{3,2,1,0:T(8,128)(2,1)S(1)} fusion(bf16[1,4,1024,1024]{3,2,1,0:T(8,128)(2,1)S(1)} %bitcast.181, bf16[4,64,1024]{2,1,0:T(8,128)(2,1)S(1)} %collective-permute-done.8, bf16[4,32,1024]{2,1,0:T(8,128)(2,1)S(1)} %collective-permute-done.7, bf16[4,32,1024]{2,1,0:T(8,128)(2,1)S(1)} %collective-permute-done.6), kind=kOutput, calls=%fused_computation.33 | convolution fusion | flops 1077411840 | bytes 10485760 | tf_op jit(solution)/shard_map/sik,sjk->sij/dot_general | solution.py:76
  105.2 0.8 pad_maximum_fusion.1
  106.1 7.0 %add_convert_fusion = bf16[1024,1024]{1,0:T(8,128)(2,1)S(1)} fusion(f32[1024,1024]{1,0:T(8,128)S(1)} %fusion.99, bf16[1024,2048]{1,0:T(8,128)(2,1)} %get-tuple-element.8, bf16[2048,1024]{1,0:T(8,128)(2,1)S(1)} %bitcast.189), kind=kOutput, calls=%fused_computation.22 | convolution fusion | flops 4297064448 | bytes 14680064 | tf_op jit(solution)/shard_map/dot_general | solution.py:82
  113.1 0.6 copy.27
  114.4 1.8 %gather_fusion.1 = bf16[36,128,128]{2,1,0:T(8,128)(2,1)} fusion(bf16[64,128,128]{2,1,0:T(8,128)(2,1)S(1)} %bitcast.182, s32[1024]{0:T(1024)S(1)} %get-tuple-element.52), kind=kCustom, calls=%fused_computation.1 | custom fusion | bytes 2359440 | tf_op jit(solution)/shard_map/gather | solution.py:94
  116.2 0.8 gather_fusion.2
  117.0 1.4 copy.20
  118.7 0.9 fusion.64
  119.7 1.7 pad_maximum_fusion.2
  121.4 12.7 %all-to-all-start.1 = ((bf16[16,576,128]{2,1,0:T(8,128)(2,1)}), bf16[16,576,128]{2,1,0:T(8,128)(2,1)S(1)}, u32[]{:S(2)}, u32[]{:S(2)}) async-start(bf16[16,576,128]{2,1,0:T(8,128)(2,1)} %pad_maximum_fusion.2), calls=%async_computation.1 | async-start | bytes 4718592 | tf_op jit(solution)/shard_map/all_to_all | solution.py:107
  134.1 31.1 %all-to-all-done.1 = bf16[16,576,128]{2,1,0:T(8,128)(2,1)S(1)} async-done(((bf16[16,576,128]{2,1,0:T(8,128)(2,1)}), bf16[16,576,128]{2,1,0:T(8,128)(2,1)S(1)}, u32[]{:S(2)}, u32[]{:S(2)}) %all-to-all-start.1) | async-done | bytes 2359328 | tf_op jit(solution)/shard_map/all_to_all | solution.py:107
  165.4 0.7 fusion.68
  166.2 1.3 gather_fusion.3
  167.5 13.3 %all_to_all.19 = f32[16,1,8]{2,1,0:T(1,128)S(1)} all-to-all(f32[16,1,8]{2,1,0:T(1,128)S(1)} %bitcast.194), channel_id=1, replica_groups=mesh['tsink'=8,'mom'=16] {'mom'}, dimensions={0} | all-to-all | bytes 1024 | tf_op jit(solution)/shard_map/all_to_all | solution.py:115
  (64 shorter events, 5.0 us)
Async XLA Ops:
  0.6 36.9 %all-to-all-start = ((bf16[8,128,1024]{2,1,0:T(8,128)(2,1)}), bf16[8,128,1024]{2,1,0:T(8,128)(2,1)}, u32[]{:S(2)}, u32[]{:S(2)}) async-start(bf16[8,128,1024]{2,1,0:T(8,128)(2,1)} %bitcast.191), calls=%async_computation | async-start | bytes 4194304 | tf_op jit(solution)/shard_map/all_to_all | solution.py:26
  6.8 5.8 %copy-start.10 = (s32[4]{0:T(128)S(1)}, s32[4]{0:T(128)}, u32[]{:S(2)}) copy-start(s32[4]{0:T(128)} %param.11) | copy-start | bytes 52
  6.8 5.8 %copy-start.8 = (pred[36]{0:T(512)(128)(4,1)S(1)}, pred[36]{0:T(512)(128)(4,1)}, u32[]{:S(2)}) copy-start(pred[36]{0:T(512)(128)(4,1)} %constant.109) | copy-start | bytes 112
  12.8 9.0 %copy-start.1 = (bf16[1,1,1024,1024]{3,2,1,0:T(8,128)(2,1)S(1)}, bf16[1,1,1024,1024]{3,2,1,0:T(8,128)(2,1)}, u32[]{:S(2)}) copy-start(bf16[1,1,1024,1024]{3,2,1,0:T(8,128)(2,1)} %get-tuple-element.4) | copy-start | bytes 6291460
  12.8 10.0 %copy-start = (bf16[1,1,1024,1024]{3,2,1,0:T(8,128)(2,1)S(1)}, bf16[1,1,1024,1024]{3,2,1,0:T(8,128)(2,1)}, u32[]{:S(2)}) copy-start(bf16[1,1,1024,1024]{3,2,1,0:T(8,128)(2,1)} %get-tuple-element.3) | copy-start | bytes 6291460
  12.9 12.0 %copy-start.2 = (bf16[1,1,1024,1024]{3,2,1,0:T(8,128)(2,1)S(1)}, bf16[1,1,1024,1024]{3,2,1,0:T(8,128)(2,1)}, u32[]{:S(2)}) copy-start(bf16[1,1,1024,1024]{3,2,1,0:T(8,128)(2,1)} %get-tuple-element.5) | copy-start | bytes 6291460
  25.8 17.4 %copy-start.6 = (s32[36]{0:T(128)S(1)}, s32[36]{0:T(128)}, u32[]{:S(2)}) copy-start(s32[36]{0:T(128)} %constant.124) | copy-start | bytes 436
  25.8 17.4 %copy-start.7 = (s32[36]{0:T(128)S(1)}, s32[36]{0:T(128)}, u32[]{:S(2)}) copy-start(s32[36]{0:T(128)} %constant.125) | copy-start | bytes 436
  39.8 23.2 %collective-permute-start.2 = (bf16[4,128,1024]{2,1,0:T(8,128)(2,1)S(1)}, bf16[4,128,1024]{2,1,0:T(8,128)(2,1)S(1)}, u32[]{:S(2)}, u32[]{:S(2)}) collective-permute-start(bf16[4,128,1024]{2,1,0:T(8,128)(2,1)S(1)} %gather_fusion), channel_id=1, source_target_pairs={{0,96},{16,112},{32,0},{48,16},{64,32},{80,48},{96,64},{112,80},{1... | collective-permute-start | bytes 3145736 | tf_op jit(solution)/shard_map/ppermute | solution.py:12
  41.8 24.4 %collective-permute-start.1 = (bf16[4,128,1024]{2,1,0:T(8,128)(2,1)S(1)}, bf16[4,128,1024]{2,1,0:T(8,128)(2,1)S(1)}, u32[]{:S(2)}, u32[]{:S(2)}) collective-permute-start(bf16[4,128,1024]{2,1,0:T(8,128)(2,1)S(1)} %gather_fusion), channel_id=1, source_target_pairs={{0,32},{16,48},{32,64},{48,80},{64,96},{80,112},{96,0},{112,16},{1... | collective-permute-start | bytes 3145736 | tf_op jit(solution)/shard_map/ppermute | solution.py:12
  43.3 26.8 %slice-start = ((s8[8388608]{0:T(1024)(128)(4,1)}), s8[4194304]{0:T(1024)(128)(4,1)S(1)}, s32[]{:S(2)}) async-start(s8[8388608]{0:T(1024)(128)(4,1)} %bitcast.180), calls=%async_computation.3 | async-start | bytes 8388608
  44.3 25.8 %slice-start.1 = ((s8[8388608]{0:T(1024)(128)(4,1)}), s8[4194304]{0:T(1024)(128)(4,1)S(1)}, s32[]{:S(2)}) async-start(s8[8388608]{0:T(1024)(128)(4,1)} %bitcast.180), calls=%async_computation.4 | async-start | bytes 8388608
  44.3 22.6 %collective-permute-start = (bf16[4,128,1024]{2,1,0:T(8,128)(2,1)S(1)}, bf16[4,128,1024]{2,1,0:T(8,128)(2,1)S(1)}, u32[]{:S(2)}, u32[]{:S(2)}) collective-permute-start(bf16[4,128,1024]{2,1,0:T(8,128)(2,1)S(1)} %gather_fusion), channel_id=1, source_target_pairs={{0,16},{16,0},{32,48},{48,32},{64,80},{80,64},{96,112},{112,96},{1... | collective-permute-start | bytes 3145736 | tf_op jit(solution)/shard_map/ppermute | solution.py:16
  67.1 23.0 %collective-permute-start.3 = (bf16[2,4,64,1024]{3,2,1,0:T(8,128)(2,1)S(1)}, bf16[2,4,64,1024]{3,2,1,0:T(8,128)(2,1)S(1)}, u32[]{:S(2)}, u32[]{:S(2)}) collective-permute-start(bf16[2,4,64,1024]{3,2,1,0:T(8,128)(2,1)S(1)} %get-tuple-element.50), channel_id=1, source_target_pairs={{0,32},{16,48},{32,64},{48,80},{64,96},{80,112},{96,0},{112,16},{1... | collective-permute-start | bytes 3145736 | tf_op jit(solution)/shard_map/ppermute | solution.py:12
  67.5 22.8 %collective-permute-start.4 = (bf16[2,4,64,1024]{3,2,1,0:T(8,128)(2,1)S(1)}, bf16[2,4,64,1024]{3,2,1,0:T(8,128)(2,1)S(1)}, u32[]{:S(2)}, u32[]{:S(2)}) collective-permute-start(bf16[2,4,64,1024]{3,2,1,0:T(8,128)(2,1)S(1)} %get-tuple-element.49), channel_id=1, source_target_pairs={{0,96},{16,112},{32,0},{48,16},{64,32},{80,48},{96,64},{112,80},{1... | collective-permute-start | bytes 3145736 | tf_op jit(solution)/shard_map/ppermute | solution.py:12
  69.9 23.6 %collective-permute-start.5 = (bf16[2,4,64,1024]{3,2,1,0:T(8,128)(2,1)S(1)}, bf16[2,4,64,1024]{3,2,1,0:T(8,128)(2,1)S(1)}, u32[]{:S(2)}, u32[]{:S(2)}) collective-permute-start(bf16[2,4,64,1024]{3,2,1,0:T(8,128)(2,1)S(1)} %get-tuple-element.48), channel_id=1, source_target_pairs={{0,16},{16,0},{32,48},{48,32},{64,80},{80,64},{96,112},{112,96},{1... | collective-permute-start | bytes 3145736 | tf_op jit(solution)/shard_map/ppermute | solution.py:16
  90.2 12.1 %collective-permute-start.6 = (bf16[4,32,1024]{2,1,0:T(8,128)(2,1)S(1)}, bf16[4,32,1024]{2,1,0:T(8,128)(2,1)S(1)}, u32[]{:S(2)}, u32[]{:S(2)}) collective-permute-start(bf16[4,32,1024]{2,1,0:T(8,128)(2,1)S(1)} %slice.132), channel_id=1, source_target_pairs={{0,32},{16,48},{32,64},{48,80},{64,96},{80,112},{96,0},{112,16},{1... | collective-permute-start | bytes 786440 | tf_op jit(solution)/shard_map/ppermute | solution.py:12
  90.4 11.9 %collective-permute-start.7 = (bf16[4,32,1024]{2,1,0:T(8,128)(2,1)S(1)}, bf16[4,32,1024]{2,1,0:T(8,128)(2,1)S(1)}, u32[]{:S(2)}, u32[]{:S(2)}) collective-permute-start(bf16[4,32,1024]{2,1,0:T(8,128)(2,1)S(1)} %slice.133), channel_id=1, source_target_pairs={{0,96},{16,112},{32,0},{48,16},{64,32},{80,48},{96,64},{112,80},{1... | collective-permute-start | bytes 786440 | tf_op jit(solution)/shard_map/ppermute | solution.py:12
  93.2 9.2 %collective-permute-start.8 = (bf16[4,64,1024]{2,1,0:T(8,128)(2,1)S(1)}, bf16[4,64,1024]{2,1,0:T(8,128)(2,1)S(1)}, u32[]{:S(2)}, u32[]{:S(2)}) collective-permute-start(bf16[4,64,1024]{2,1,0:T(8,128)(2,1)S(1)} %get-tuple-element.47), channel_id=1, source_target_pairs={{0,16},{16,0},{32,48},{48,32},{64,80},{80,64},{96,112},{112,96},{1... | collective-permute-start | bytes 1572872 | tf_op jit(solution)/shard_map/ppermute | solution.py:16
  113.1 1.4 copy-start.5
  117.0 1.7 copy-start.3
  118.5 1.3 copy-start.4
  119.7 14.3 %copy-start.9 = (s32[128,2]{0,1:T(2,128)S(1)}, s32[128,2]{0,1:T(2,128)}, u32[]{:S(2)}) copy-start(s32[128,2]{0,1:T(2,128)} %param.12) | copy-start | bytes 3076
  121.4 43.8 %all-to-all-start.1 = ((bf16[16,576,128]{2,1,0:T(8,128)(2,1)}), bf16[16,576,128]{2,1,0:T(8,128)(2,1)S(1)}, u32[]{:S(2)}, u32[]{:S(2)}) async-start(bf16[16,576,128]{2,1,0:T(8,128)(2,1)} %pad_maximum_fusion.2), calls=%async_computation.1 | async-start | bytes 4718592 | tf_op jit(solution)/shard_map/all_to_all | solution.py:107

commit v4 on v3

--- a/solution.py
+++ b/solution.py
@@ -24,7 +24,7 @@
     quarter = half // 2
     pieces = own_elemental.reshape(n_t, rows, order)
     received = lax.all_to_all(pieces, "tsink", 0, 0)
-    own = received[src_times]
+    own = jnp.stack([lax.dynamic_index_in_dim(received, time, 0, False) for time in src_times])
     t = lax.axis_index("tsink")
     step = 2
     partner = swapped(own, n_t)
@@ -110,8 +110,7 @@
     partial = lax.dot_general(
         own_rows, own_cols, (((1,), (1,)), ((), ())), preferred_element_type=jnp.float32
     )
-    partial = partial + partial.T
-    per_diagram = partial[diagrams[:, 0], diagrams[:, 1]]
+    per_diagram = partial[diagrams[:, 0], diagrams[:, 1]] + partial[diagrams[:, 1], diagrams[:, 0]]
     spread = lax.all_to_all(per_diagram.reshape(n_m, -1), "mom", 0, 0)
     correlators = (jnp.sum(spread, axis=0) / block_order)[:, None]
     return (meson[None, None], correlators)

time: 182 us -> 186 us (1.022)
  waiting for transfers between devices: 57.8 us -> 47.2 us
  between operations: 1.07 us -> 8.89 us
  starting transfers between devices: 26.4 us -> 29.9 us
    all_to_all x1, waiting for transfers between devices: 6.66 us -> 0.01 us  [source_pieces(): received = lax.all_to_all(pieces, 'tsink', 0, 0)]
    ppermute x6, waiting for transfers between devices: 19.4 us -> 15.9 us  [shifted(): return lax.ppermute(block, 'tsink', pairs)]
    ppermute x3, starting transfers between devices: 0.45 us -> 3.63 us  [swapped(): return lax.ppermute(block, 'tsink', [(t, t ^ 1) for t in range(n_t)])]
    unnamed x42 -> x46, local copies, waits for them, and re-layouts: 20.8 us -> 20.8 us
  transfers between devices with their start and end apart: 11 -> 11, of which waited for: 6 -> 5; matrix products, arithmetic and copies ran while one was open for 32% -> 33% of each run, Pallas kernels for 0% -> 0%
where the time goes in v4:
time: 186 us
  waiting for transfers between devices  47.2 us (25%)
  matrix products  42.8 us (23%)
  local copies, waits for them, and re-layouts  37.8 us (20%)
  starting transfers between devices  29.9 us (16%)
  blocking collectives  13.3 us (7%)
  between operations  8.89 us (5%)
  other arithmetic  5.97 us (3%)
    all_to_all x1, waiting for transfers between devices, body(): received = lax.all_to_all(slices, 'mom', 0, 0)  31.1 us
    dot_general x8, matrix products, stacked(): jnp.einsum('sik,sjk->sij', piece, propagators, preferred_element_type=jnp...  28.7 us
    unnamed x46, local copies, waits for them, and re-layouts  20.8 us
    ppermute x6, waiting for transfers between devices, shifted(): return lax.ppermute(block, 'tsink', pairs)  15.9 us
    dot_general x2, matrix products, stacked(): jnp.dot(columns, blocks.reshape(-1, block_order), preferred_element_type=...  13.4 us
    all_to_all x1, blocking collectives, body(): spread = lax.all_to_all(per_diagram.reshape(n_m, -1), 'mom', 0, 0)  13.3 us
    all_to_all x1, starting transfers between devices, body(): received = lax.all_to_all(slices, 'mom', 0, 0)  11.4 us
    ppermute x6, starting transfers between devices, shifted(): return lax.ppermute(block, 'tsink', pairs)  8.63 us
  transfers between devices with their start and end apart: 11, of which 5 were waited for; matrix products, arithmetic and copies ran while one was open for 33% of the time, Pallas kernels for 0%

profile of v4, /device:TPU:1, one launch (start us, length us, event | category | flops | bytes accessed | tf_op | source)
XLA Modules:
  0.0 185.8 jit_solution(4187666229927427930)
XLA Ops:
  0.6 6.2 %all-to-all-start = ((bf16[8,128,1024]{2,1,0:T(8,128)(2,1)}), bf16[8,128,1024]{2,1,0:T(8,128)(2,1)}, u32[]{:S(2)}, u32[]{:S(2)}) async-start(bf16[8,128,1024]{2,1,0:T(8,128)(2,1)} %bitcast.194), calls=%async_computation | async-start | bytes 4194304 | tf_op jit(solution)/shard_map/all_to_all | solution.py:26
  6.8 5.8 %fusion.93 = (bf16[1,1,1024,1024]{3,2,1,0:T(8,128)(2,1)S(1)}, bf16[1,1,1024,1024]{3,2,1,0:T(8,128)(2,1)}, bf16[1,1,1024,1024]{3,2,1,0:T(8,128)(2,1)}, bf16[1,1,1024,1024]{3,2,1,0:T(8,128)(2,1)}) fusion(bf16[1,4,1024,1024]{3,2,1,0:T(8,128)(2,1)} %param.9), kind=kLoop, calls=%fused_computation.126 | loop fusion | bytes 16777216 | tf_op jit(solution)/shard_map/slice | solution.py:68
  21.1 2.1 %bitcast_dynamic-update-slice_fusion.15 = (bf16[1024,2048]{1,0:T(8,128)(2,1)}, bf16[1024,2048]{1,0:T(8,128)(2,1)}) fusion(bf16[1,1,1024,1024]{3,2,1,0:T(8,128)(2,1)} %get-tuple-element.5, s32[]{:T(128)S(6)} %select_n.130, s32[]{:T(128)S(6)} %select_n.119), kind=kLoop, calls=%fused_computation.89 | loop fusion | bytes 1048584
  23.2 2.0 %bitcast_dynamic-update-slice_fusion.14 = (bf16[1024,2048]{1,0:T(8,128)(2,1)}, bf16[1024,2048]{1,0:T(8,128)(2,1)}) fusion(bf16[1024,2048]{1,0:T(8,128)(2,1)} %get-tuple-element.38, bf16[1,1,1024,1024]{3,2,1,0:T(8,128)(2,1)} %get-tuple-element.4, s32[]{:T(128)S(6)} %select_n.130, bf16[1024,2048]{1,0:T(8,128)(2,1)} %get-tuple-element.39, s32[]{:T(128)S(6)} %select_n.119), kind=kLoop, calls=%fused_computation.88 | loop fusion | bytes 1048584
  25.3 1.9 %bitcast_dynamic-update-slice_fusion.13 = (bf16[1024,2048]{1,0:T(8,128)(2,1)}, bf16[1024,2048]{1,0:T(8,128)(2,1)}) fusion(bf16[1024,2048]{1,0:T(8,128)(2,1)} %get-tuple-element.36, bf16[1,1,1024,1024]{3,2,1,0:T(8,128)(2,1)} %get-tuple-element.3, s32[]{:T(128)S(6)} %select_n.130, bf16[1024,2048]{1,0:T(8,128)(2,1)} %get-tuple-element.37, s32[]{:T(128)S(6)} %select_n.119), kind=kLoop, calls=%fused_computation.87 | loop fusion | bytes 1048584
  27.2 1.0 bitcast_dynamic-update-slice_fusion.12
  28.2 1.9 %bitcast_dynamic-update-slice_fusion.11 = (bf16[1024,2048]{1,0:T(8,128)(2,1)}, bf16[1024,2048]{1,0:T(8,128)(2,1)}) fusion(bf16[1024,2048]{1,0:T(8,128)(2,1)} %get-tuple-element.32, bf16[1,1,1024,1024]{3,2,1,0:T(8,128)(2,1)} %get-tuple-element.5, s32[]{:T(128)S(6)} %select_n.131, bf16[1024,2048]{1,0:T(8,128)(2,1)} %get-tuple-element.33, s32[]{:T(128)S(6)} %select_n.120), kind=kLoop, calls=%fused_computation.85 | loop fusion | bytes 1048584
  30.2 1.0 bitcast_dynamic-update-slice_fusion.10
  31.2 1.0 bitcast_dynamic-update-slice_fusion.9
  32.2 1.0 bitcast_dynamic-update-slice_fusion.8
  33.1 1.0 bitcast_dynamic-update-slice_fusion.7
  34.1 1.0 bitcast_dynamic-update-slice_fusion.6
  35.1 1.0 bitcast_dynamic-update-slice_fusion.5
  36.2 1.0 bitcast_dynamic-update-slice_fusion.4
  37.2 1.0 bitcast_dynamic-update-slice_fusion.3
  38.1 1.0 bitcast_dynamic-update-slice_fusion.2
  39.1 1.3 constant_dynamic-slice_fusion.3
  40.4 1.2 pad_maximum_fusion.5
  41.6 2.7 %collective-permute-start.2 = (bf16[4,128,1024]{2,1,0:T(8,128)(2,1)}, bf16[4,128,1024]{2,1,0:T(8,128)(2,1)}, u32[]{:S(2)}, u32[]{:S(2)}) collective-permute-start(bf16[4,128,1024]{2,1,0:T(8,128)(2,1)} %pad_maximum_fusion.5), channel_id=1, source_target_pairs={{0,96},{16,112},{32,0},{48,16},{64,32},{80,48},{96,64},{112,80},{1... | collective-permute-start | bytes 3145736 | tf_op jit(solution)/shard_map/ppermute | solution.py:12
  44.3 1.9 %bitcast_dynamic-update-slice_fusion.1 = (bf16[1024,2048]{1,0:T(8,128)(2,1)}, bf16[1024,2048]{1,0:T(8,128)(2,1)}) fusion(bf16[1024,2048]{1,0:T(8,128)(2,1)} %get-tuple-element.12, bf16[1,1,1024,1024]{3,2,1,0:T(8,128)(2,1)} %get-tuple-element.3, s32[]{:T(128)S(6)} %select_n.133, bf16[1024,2048]{1,0:T(8,128)(2,1)} %get-tuple-element.13, s32[]{:T(128)S(6)} %select_n.124), kind=kLoop, calls=%fused_computation.75 | loop fusion | bytes 1048584
  46.5 1.0 bitcast_dynamic-update-slice_fusion
  47.5 1.2 collective-permute-start
  48.7 6.9 %fusion.61 = bf16[1,4,128,1024]{3,2,1,0:T(8,128)(2,1)S(1)} fusion(bf16[1,4,1024,1024]{3,2,1,0:T(8,128)(2,1)} %param.9, bf16[1,128,1024]{2,1,0:T(8,128)(2,1)} %copy-done.5, bf16[1,128,1024]{2,1,0:T(8,128)(2,1)} %copy-done.6, bf16[1,128,1024]{2,1,0:T(8,128)(2,1)} %copy-done.7, bf16[1,128,1024]{2,1,0:T(8,128)(2,1)S(1)} %get-tuple-element.40), kind=kOutput, calls=%fused_computation.40 | convolution fusion | flops 1075838976 | bytes 10485760 | tf_op jit(solution)/shard_map/sik,sjk->sij/dot_general | solution.py:76
  55.6 10.3 %collective-permute-done.2 = bf16[4,128,1024]{2,1,0:T(8,128)(2,1)} collective-permute-done((bf16[4,128,1024]{2,1,0:T(8,128)(2,1)}, bf16[4,128,1024]{2,1,0:T(8,128)(2,1)}, u32[]{:S(2)}, u32[]{:S(2)}) %collective-permute-start.2) | collective-permute-done | bytes 1048608 | tf_op jit(solution)/shard_map/ppermute | solution.py:12
  65.9 1.1 slice_bitcast_fusion.6
  67.0 3.9 %collective-permute-done.1 = bf16[4,128,1024]{2,1,0:T(8,128)(2,1)S(1)} collective-permute-done((bf16[4,128,1024]{2,1,0:T(8,128)(2,1)}, bf16[4,128,1024]{2,1,0:T(8,128)(2,1)S(1)}, u32[]{:S(2)}, u32[]{:S(2)}) %collective-permute-start.1) | collective-permute-done | bytes 1048608 | tf_op jit(solution)/shard_map/ppermute | solution.py:12
  71.3 2.4 %collective-permute-start.4 = (bf16[2,4,64,1024]{3,2,1,0:T(8,128)(2,1)S(1)}, bf16[2,4,64,1024]{3,2,1,0:T(8,128)(2,1)S(1)}, u32[]{:S(2)}, u32[]{:S(2)}) collective-permute-start(bf16[2,4,64,1024]{3,2,1,0:T(8,128)(2,1)S(1)} %get-tuple-element.53), channel_id=1, source_target_pairs={{0,96},{16,112},{32,0},{48,16},{64,32},{80,48},{96,64},{112,80},{1... | collective-permute-start | bytes 3145736 | tf_op jit(solution)/shard_map/ppermute | solution.py:12
  73.7 1.2 collective-permute-start.5
  74.9 4.2 %fusion.52 = bf16[1,4,128,1024]{3,2,1,0:T(8,128)(2,1)S(1)} fusion(bf16[4,128,1024]{2,1,0:T(8,128)(2,1)} %collective-permute-done.2, bf16[1,4,1024,1024]{3,2,1,0:T(8,128)(2,1)S(1)} %bitcast.184), kind=kOutput, calls=%fused_computation.37 | convolution fusion | flops 1074266112 | bytes 10485760 | tf_op jit(solution)/shard_map/sik,sjk->sij/dot_general | solution.py:76
  79.1 3.0 %fusion.55 = bf16[1,4,128,1024]{3,2,1,0:T(8,128)(2,1)S(1)} fusion(bf16[4,128,1024]{2,1,0:T(8,128)(2,1)S(1)} %collective-permute-done.1, bf16[1,4,1024,1024]{3,2,1,0:T(8,128)(2,1)S(1)} %bitcast.184), kind=kOutput, calls=%fused_computation.38 | convolution fusion | flops 1074266112 | bytes 10485760 | tf_op jit(solution)/shard_map/sik,sjk->sij/dot_general | solution.py:76
  82.1 2.9 %fusion.58 = bf16[1,4,128,1024]{3,2,1,0:T(8,128)(2,1)S(1)} fusion(bf16[4,128,1024]{2,1,0:T(8,128)(2,1)S(1)} %collective-permute-done, bf16[1,4,1024,1024]{3,2,1,0:T(8,128)(2,1)S(1)} %bitcast.184), kind=kOutput, calls=%fused_computation.39 | convolution fusion | flops 1074266112 | bytes 10485760 | tf_op jit(solution)/shard_map/sik,sjk->sij/dot_general | solution.py:76
  85.6 6.4 %fusion.96 = f32[1024,1024]{1,0:T(8,128)S(1)} fusion(bf16[1024,2048]{1,0:T(8,128)(2,1)} %get-tuple-element.9, bf16[2048,1024]{1,0:T(8,128)(2,1)S(1)} %bitcast.193), kind=kOutput, calls=%fused_computation.129 | convolution fusion | flops 4294967296 | bytes 12582912 | tf_op jit(solution)/shard_map/dot_general | solution.py:82
  92.0 1.7 collective-permute-done.4
  93.8 1.3 collective-permute-start.8
  95.1 3.3 %collective-permute-start.7 = (bf16[4,32,1024]{2,1,0:T(8,128)(2,1)S(1)}, bf16[4,32,1024]{2,1,0:T(8,128)(2,1)S(1)}, u32[]{:S(2)}, u32[]{:S(2)}) collective-permute-start(bf16[4,32,1024]{2,1,0:T(8,128)(2,1)S(1)} %slice.135), channel_id=1, source_target_pairs={{0,96},{16,112},{32,0},{48,16},{64,32},{80,48},{96,64},{112,80},{1... | collective-permute-start | bytes 786440 | tf_op jit(solution)/shard_map/ppermute | solution.py:12
  98.9 2.9 %fusion.43 = bf16[1,4,128,1024]{3,2,1,0:T(8,128)(2,1)S(1)} fusion(bf16[1,4,1024,1024]{3,2,1,0:T(8,128)(2,1)S(1)} %bitcast.184, bf16[4,64,1024]{2,1,0:T(8,128)(2,1)S(1)} %get-tuple-element.47, bf16[4,64,1024]{2,1,0:T(8,128)(2,1)S(1)} %get-tuple-element.50), kind=kOutput, calls=%fused_computation.34 | convolution fusion | flops 1076363264 | bytes 10485760 | tf_op jit(solution)/shard_map/sik,sjk->sij/dot_general | solution.py:76
  101.8 2.9 %fusion.46 = bf16[1,4,128,1024]{3,2,1,0:T(8,128)(2,1)S(1)} fusion(bf16[1,4,1024,1024]{3,2,1,0:T(8,128)(2,1)S(1)} %bitcast.184, bf16[4,64,1024]{2,1,0:T(8,128)(2,1)S(1)} %get-tuple-element.46, bf16[4,64,1024]{2,1,0:T(8,128)(2,1)S(1)} %get-tuple-element.45), kind=kOutput, calls=%fused_computation.35 | convolution fusion | flops 1076363264 | bytes 10485760 | tf_op jit(solution)/shard_map/sik,sjk->sij/dot_general | solution.py:76
  104.7 2.9 %fusion.49 = bf16[1,4,128,1024]{3,2,1,0:T(8,128)(2,1)S(1)} fusion(bf16[1,4,1024,1024]{3,2,1,0:T(8,128)(2,1)S(1)} %bitcast.184, bf16[4,64,1024]{2,1,0:T(8,128)(2,1)S(1)} %get-tuple-element.51, bf16[4,64,1024]{2,1,0:T(8,128)(2,1)S(1)} %get-tuple-element.44), kind=kOutput, calls=%fused_computation.36 | convolution fusion | flops 1076363264 | bytes 10485760 | tf_op jit(solution)/shard_map/sik,sjk->sij/dot_general | solution.py:76
  107.8 2.9 %fusion.40 = bf16[1,4,128,1024]{3,2,1,0:T(8,128)(2,1)S(1)} fusion(bf16[1,4,1024,1024]{3,2,1,0:T(8,128)(2,1)S(1)} %bitcast.184, bf16[4,64,1024]{2,1,0:T(8,128)(2,1)S(1)} %collective-permute-done.8, bf16[4,32,1024]{2,1,0:T(8,128)(2,1)S(1)} %collective-permute-done.7, bf16[4,32,1024]{2,1,0:T(8,128)(2,1)S(1)} %collective-permute-done.6), kind=kOutput, calls=%fused_computation.33 | convolution fusion | flops 1077411840 | bytes 10485760 | tf_op jit(solution)/shard_map/sik,sjk->sij/dot_general | solution.py:76
  111.6 7.0 %add_convert_fusion = bf16[1024,1024]{1,0:T(8,128)(2,1)S(1)} fusion(f32[1024,1024]{1,0:T(8,128)S(1)} %fusion.96, bf16[1024,2048]{1,0:T(8,128)(2,1)} %get-tuple-element.8, bf16[2048,1024]{1,0:T(8,128)(2,1)S(1)} %bitcast.192), kind=kOutput, calls=%fused_computation.22 | convolution fusion | flops 4297064448 | bytes 14680064 | tf_op jit(solution)/shard_map/dot_general | solution.py:82
  120.7 1.4 copy.18
  123.2 0.9 fusion.64
  124.2 1.7 pad_maximum_fusion.2
  125.9 11.4 %all-to-all-start.1 = ((bf16[16,576,128]{2,1,0:T(8,128)(2,1)}), bf16[16,576,128]{2,1,0:T(8,128)(2,1)S(1)}, u32[]{:S(2)}, u32[]{:S(2)}) async-start(bf16[16,576,128]{2,1,0:T(8,128)(2,1)} %pad_maximum_fusion.2), calls=%async_computation.1 | async-start | bytes 4718592 | tf_op jit(solution)/shard_map/all_to_all | solution.py:107
  137.3 31.1 %all-to-all-done.1 = bf16[16,576,128]{2,1,0:T(8,128)(2,1)S(1)} async-done(((bf16[16,576,128]{2,1,0:T(8,128)(2,1)}), bf16[16,576,128]{2,1,0:T(8,128)(2,1)S(1)}, u32[]{:S(2)}, u32[]{:S(2)}) %all-to-all-start.1) | async-done | bytes 2359328 | tf_op jit(solution)/shard_map/all_to_all | solution.py:107
  169.3 1.3 gather_fusion.2
  170.6 1.3 gather_fusion.3
  171.9 13.3 %all_to_all.16 = f32[16,1,8]{2,1,0:T(1,128)S(1)} all-to-all(f32[16,1,8]{2,1,0:T(1,128)S(1)} %bitcast.197), channel_id=1, replica_groups=mesh['tsink'=8,'mom'=16] {'mom'}, dimensions={0} | all-to-all | bytes 1024 | tf_op jit(solution)/shard_map/all_to_all | solution.py:114
  (68 shorter events, 8.2 us)
Async XLA Ops:
  0.6 38.5 %all-to-all-start = ((bf16[8,128,1024]{2,1,0:T(8,128)(2,1)}), bf16[8,128,1024]{2,1,0:T(8,128)(2,1)}, u32[]{:S(2)}, u32[]{:S(2)}) async-start(bf16[8,128,1024]{2,1,0:T(8,128)(2,1)} %bitcast.194), calls=%async_computation | async-start | bytes 4194304 | tf_op jit(solution)/shard_map/all_to_all | solution.py:26
  6.8 5.8 %copy-start.8 = (s32[4]{0:T(128)S(1)}, s32[4]{0:T(128)}, u32[]{:S(2)}) copy-start(s32[4]{0:T(128)} %param.11) | copy-start | bytes 52
  21.1 9.1 %copy-start.1 = (bf16[1,1,1024,1024]{3,2,1,0:T(8,128)(2,1)S(1)}, bf16[1,1,1024,1024]{3,2,1,0:T(8,128)(2,1)}, u32[]{:S(2)}) copy-start(bf16[1,1,1024,1024]{3,2,1,0:T(8,128)(2,1)} %get-tuple-element.4) | copy-start | bytes 6291460
  21.1 10.1 %copy-start = (bf16[1,1,1024,1024]{3,2,1,0:T(8,128)(2,1)S(1)}, bf16[1,1,1024,1024]{3,2,1,0:T(8,128)(2,1)}, u32[]{:S(2)}) copy-start(bf16[1,1,1024,1024]{3,2,1,0:T(8,128)(2,1)} %get-tuple-element.3) | copy-start | bytes 6291460
  21.1 12.0 %copy-start.2 = (bf16[1,1,1024,1024]{3,2,1,0:T(8,128)(2,1)S(1)}, bf16[1,1,1024,1024]{3,2,1,0:T(8,128)(2,1)}, u32[]{:S(2)}) copy-start(bf16[1,1,1024,1024]{3,2,1,0:T(8,128)(2,1)} %get-tuple-element.5) | copy-start | bytes 6291460
  36.2 10.1 %copy-start.10 = (s32[36]{0:T(128)S(1)}, s32[36]{0:T(128)}, u32[]{:S(2)}) copy-start(s32[36]{0:T(128)} %constant.146) | copy-start | bytes 436
  36.2 10.1 %copy-start.11 = (s32[36]{0:T(128)S(1)}, s32[36]{0:T(128)}, u32[]{:S(2)}) copy-start(s32[36]{0:T(128)} %constant.145) | copy-start | bytes 436
  36.2 10.1 %copy-start.12 = (pred[36]{0:T(512)(128)(4,1)S(1)}, pred[36]{0:T(512)(128)(4,1)}, u32[]{:S(2)}) copy-start(pred[36]{0:T(512)(128)(4,1)} %constant.117) | copy-start | bytes 112
  40.4 3.9 %copy-start.5 = (bf16[1,128,1024]{2,1,0:T(8,128)(2,1)}, bf16[1,128,1024]{2,1,0:T(8,128)(2,1)S(1)}, u32[]{:S(2)}) copy-start(bf16[1,128,1024]{2,1,0:T(8,128)(2,1)S(1)} %get-tuple-element.41) | copy-start | bytes 786436
  40.4 3.9 %copy-start.6 = (bf16[1,128,1024]{2,1,0:T(8,128)(2,1)}, bf16[1,128,1024]{2,1,0:T(8,128)(2,1)S(1)}, u32[]{:S(2)}) copy-start(bf16[1,128,1024]{2,1,0:T(8,128)(2,1)S(1)} %get-tuple-element.42) | copy-start | bytes 786436
  40.4 3.9 %copy-start.7 = (bf16[1,128,1024]{2,1,0:T(8,128)(2,1)}, bf16[1,128,1024]{2,1,0:T(8,128)(2,1)S(1)}, u32[]{:S(2)}) copy-start(bf16[1,128,1024]{2,1,0:T(8,128)(2,1)S(1)} %get-tuple-element.43) | copy-start | bytes 786436
  41.6 24.3 %collective-permute-start.2 = (bf16[4,128,1024]{2,1,0:T(8,128)(2,1)}, bf16[4,128,1024]{2,1,0:T(8,128)(2,1)}, u32[]{:S(2)}, u32[]{:S(2)}) collective-permute-start(bf16[4,128,1024]{2,1,0:T(8,128)(2,1)} %pad_maximum_fusion.5), channel_id=1, source_target_pairs={{0,96},{16,112},{32,0},{48,16},{64,32},{80,48},{96,64},{112,80},{1... | collective-permute-start | bytes 3145736 | tf_op jit(solution)/shard_map/ppermute | solution.py:12
  46.3 24.6 %collective-permute-start.1 = (bf16[4,128,1024]{2,1,0:T(8,128)(2,1)}, bf16[4,128,1024]{2,1,0:T(8,128)(2,1)S(1)}, u32[]{:S(2)}, u32[]{:S(2)}) collective-permute-start(bf16[4,128,1024]{2,1,0:T(8,128)(2,1)} %pad_maximum_fusion.5), channel_id=1, source_target_pairs={{0,32},{16,48},{32,64},{48,80},{64,96},{80,112},{96,0},{112,16},{1... | collective-permute-start | bytes 3145736 | tf_op jit(solution)/shard_map/ppermute | solution.py:12
  46.5 28.4 %slice-start = ((s8[8388608]{0:T(1024)(128)(4,1)}), s8[4194304]{0:T(1024)(128)(4,1)S(1)}, s32[]{:S(2)}) async-start(s8[8388608]{0:T(1024)(128)(4,1)} %bitcast.183), calls=%async_computation.3 | async-start | bytes 8388608
  47.5 27.3 %slice-start.1 = ((s8[8388608]{0:T(1024)(128)(4,1)}), s8[4194304]{0:T(1024)(128)(4,1)S(1)}, s32[]{:S(2)}) async-start(s8[8388608]{0:T(1024)(128)(4,1)} %bitcast.183), calls=%async_computation.4 | async-start | bytes 8388608
  47.5 23.5 %collective-permute-start = (bf16[4,128,1024]{2,1,0:T(8,128)(2,1)}, bf16[4,128,1024]{2,1,0:T(8,128)(2,1)S(1)}, u32[]{:S(2)}, u32[]{:S(2)}) collective-permute-start(bf16[4,128,1024]{2,1,0:T(8,128)(2,1)} %pad_maximum_fusion.5), channel_id=1, source_target_pairs={{0,16},{16,0},{32,48},{48,32},{64,80},{80,64},{96,112},{112,96},{1... | collective-permute-start | bytes 3145736 | tf_op jit(solution)/shard_map/ppermute | solution.py:16
  71.3 22.4 %collective-permute-start.4 = (bf16[2,4,64,1024]{3,2,1,0:T(8,128)(2,1)S(1)}, bf16[2,4,64,1024]{3,2,1,0:T(8,128)(2,1)S(1)}, u32[]{:S(2)}, u32[]{:S(2)}) collective-permute-start(bf16[2,4,64,1024]{3,2,1,0:T(8,128)(2,1)S(1)} %get-tuple-element.53), channel_id=1, source_target_pairs={{0,96},{16,112},{32,0},{48,16},{64,32},{80,48},{96,64},{112,80},{1... | collective-permute-start | bytes 3145736 | tf_op jit(solution)/shard_map/ppermute | solution.py:12
  73.7 24.7 %collective-permute-start.3 = (bf16[2,4,64,1024]{3,2,1,0:T(8,128)(2,1)S(1)}, bf16[2,4,64,1024]{3,2,1,0:T(8,128)(2,1)S(1)}, u32[]{:S(2)}, u32[]{:S(2)}) collective-permute-start(bf16[2,4,64,1024]{3,2,1,0:T(8,128)(2,1)S(1)} %get-tuple-element.54), channel_id=1, source_target_pairs={{0,32},{16,48},{32,64},{48,80},{64,96},{80,112},{96,0},{112,16},{1... | collective-permute-start | bytes 3145736 | tf_op jit(solution)/shard_map/ppermute | solution.py:12
  73.7 25.1 %collective-permute-start.5 = (bf16[2,4,64,1024]{3,2,1,0:T(8,128)(2,1)S(1)}, bf16[2,4,64,1024]{3,2,1,0:T(8,128)(2,1)S(1)}, u32[]{:S(2)}, u32[]{:S(2)}) collective-permute-start(bf16[2,4,64,1024]{3,2,1,0:T(8,128)(2,1)S(1)} %get-tuple-element.52), channel_id=1, source_target_pairs={{0,16},{16,0},{32,48},{48,32},{64,80},{80,64},{96,112},{112,96},{1... | collective-permute-start | bytes 3145736 | tf_op jit(solution)/shard_map/ppermute | solution.py:16
  93.8 14.0 %collective-permute-start.8 = (bf16[4,64,1024]{2,1,0:T(8,128)(2,1)S(1)}, bf16[4,64,1024]{2,1,0:T(8,128)(2,1)S(1)}, u32[]{:S(2)}, u32[]{:S(2)}) collective-permute-start(bf16[4,64,1024]{2,1,0:T(8,128)(2,1)S(1)} %get-tuple-element.51), channel_id=1, source_target_pairs={{0,16},{16,0},{32,48},{48,32},{64,80},{80,64},{96,112},{112,96},{1... | collective-permute-start | bytes 1572872 | tf_op jit(solution)/shard_map/ppermute | solution.py:16
  95.1 12.5 %collective-permute-start.7 = (bf16[4,32,1024]{2,1,0:T(8,128)(2,1)S(1)}, bf16[4,32,1024]{2,1,0:T(8,128)(2,1)S(1)}, u32[]{:S(2)}, u32[]{:S(2)}) collective-permute-start(bf16[4,32,1024]{2,1,0:T(8,128)(2,1)S(1)} %slice.135), channel_id=1, source_target_pairs={{0,96},{16,112},{32,0},{48,16},{64,32},{80,48},{96,64},{112,80},{1... | collective-permute-start | bytes 786440 | tf_op jit(solution)/shard_map/ppermute | solution.py:12
  98.5 9.2 %collective-permute-start.6 = (bf16[4,32,1024]{2,1,0:T(8,128)(2,1)S(1)}, bf16[4,32,1024]{2,1,0:T(8,128)(2,1)S(1)}, u32[]{:S(2)}, u32[]{:S(2)}) collective-permute-start(bf16[4,32,1024]{2,1,0:T(8,128)(2,1)S(1)} %slice.134), channel_id=1, source_target_pairs={{0,32},{16,48},{32,64},{48,80},{64,96},{80,112},{96,0},{112,16},{1... | collective-permute-start | bytes 786440 | tf_op jit(solution)/shard_map/ppermute | solution.py:12
  118.6 1.4 copy-start.4
  122.9 1.3 copy-start.3
  124.2 13.1 %copy-start.9 = (s32[128,2]{0,1:T(2,128)S(1)}, s32[128,2]{0,1:T(2,128)}, u32[]{:S(2)}) copy-start(s32[128,2]{0,1:T(2,128)} %param.12) | copy-start | bytes 3076
  125.9 42.5 %all-to-all-start.1 = ((bf16[16,576,128]{2,1,0:T(8,128)(2,1)}), bf16[16,576,128]{2,1,0:T(8,128)(2,1)S(1)}, u32[]{:S(2)}, u32[]{:S(2)}) async-start(bf16[16,576,128]{2,1,0:T(8,128)(2,1)} %pad_maximum_fusion.2), calls=%async_computation.1 | async-start | bytes 4718592 | tf_op jit(solution)/shard_map/all_to_all | solution.py:107

commit v5 on v3

--- a/solution.py
+++ b/solution.py
@@ -63,14 +63,10 @@
     pieces = source_pieces(own_elemental, src_times)
     rows = pieces[0][1].shape[1]
     def stacked(group):
-        columns = jnp.concatenate(
-            [
-                lax.dynamic_slice_in_dim(propagators[source], origin * rows, rows, 1)
-                for origin, _ in group
-                for source in range(NSRC)
-            ],
-            axis=1,
-        )
+        origins = jnp.stack([origin for origin, _ in group])
+        by_block = propagators.reshape(NSRC, block_order, block_order // rows, rows)
+        columns = jnp.take(by_block, origins, axis=2, mode="clip")
+        columns = columns.transpose(1, 2, 0, 3).reshape(block_order, -1)
         blocks = jnp.stack(
             [
                 jnp.einsum(

time: 182 us -> 211 us (1.16)
  waiting for transfers between devices: 57.8 us -> 80.7 us
  local copies, waits for them, and re-layouts: 36.8 us -> 41.8 us
  matrix products: 41.3 us -> 43.9 us
    all_to_all x1, waiting for transfers between devices: 6.66 us -> 30.5 us  [source_pieces(): received = lax.all_to_all(pieces, 'tsink', 0, 0)]
    gather x0 -> x2, local copies, waits for them, and re-layouts: none -> 12.4 us  [stacked(): columns = jnp.take(by_block, origins, axis=2, mode='clip')]
    unnamed x42 -> x26, local copies, waits for them, and re-layouts: 20.8 us -> 12.4 us
    another operation x0 -> x1, local copies, waits for them, and re-layouts: none -> 8.24 us  [stacked(): by_block = propagators.reshape(NSRC, block_order, block_order // rows, rows)]
    slice x1 -> x0, local copies, waits for them, and re-layouts: 5.76 us -> none  [stacked(): propagators[source]]
    dot_general x8, matrix products: 27.2 us -> 30.3 us  [stacked(): jnp.einsum('sik,sjk->sij', piece, propagators, preferred_element_type=jnp...]
  transfers between devices with their start and end apart: 11 -> 11, of which waited for: 6 -> 5; matrix products, arithmetic and copies ran while one was open for 32% -> 32% of each run, Pallas kernels for 0% -> 0%
where the time goes in v5:
time: 211 us; the launch traced here: 210 us
  waiting for transfers between devices  80.7 us (38%)
  matrix products  43.9 us (21%)
  local copies, waits for them, and re-layouts  41.8 us (20%)
  starting transfers between devices  26 us (12%)
  blocking collectives  13.3 us (6%)
  other arithmetic  3.56 us (2%)
    all_to_all x1, waiting for transfers between devices, body(): received = lax.all_to_all(slices, 'mom', 0, 0)  31.1 us
    all_to_all x1, waiting for transfers between devices, source_pieces(): received = lax.all_to_all(pieces, 'tsink', 0, 0)  30.5 us
    dot_general x8, matrix products, stacked(): jnp.einsum('sik,sjk->sij', piece, propagators, preferred_element_type=jnp...  30.3 us
    ppermute x6, waiting for transfers between devices, shifted(): return lax.ppermute(block, 'tsink', pairs)  18.5 us
    all_to_all x1, blocking collectives, body(): spread = lax.all_to_all(per_diagram.reshape(n_m, -1), 'mom', 0, 0)  13.3 us
    dot_general x2, matrix products, stacked(): jnp.dot(columns, blocks.reshape(-1, block_order), preferred_element_type=...  12.8 us
    all_to_all x1, starting transfers between devices, body(): received = lax.all_to_all(slices, 'mom', 0, 0)  12.6 us
    unnamed x26, local copies, waits for them, and re-layouts  12.4 us
  transfers between devices with their start and end apart: 11, of which 5 were waited for; matrix products, arithmetic and copies ran while one was open for 32% of the time, Pallas kernels for 0%

profile of v5, /device:TPU:1, one launch (start us, length us, event | category | flops | bytes accessed | tf_op | source)
XLA Modules:
  0.0 210.3 jit_solution(17527719350313701383)
XLA Ops:
  0.6 6.2 %all-to-all-start = ((bf16[8,128,1024]{2,1,0:T(8,128)(2,1)}), bf16[8,128,1024]{2,1,0:T(8,128)(2,1)S(1)}, u32[]{:S(2)}, u32[]{:S(2)}) async-start(bf16[8,128,1024]{2,1,0:T(8,128)(2,1)} %bitcast.147), calls=%async_computation | async-start | bytes 4194304 | tf_op jit(solution)/shard_map/all_to_all | solution.py:26
  7.0 30.5 %all-to-all-done = bf16[8,128,1024]{2,1,0:T(8,128)(2,1)S(1)} async-done(((bf16[8,128,1024]{2,1,0:T(8,128)(2,1)}), bf16[8,128,1024]{2,1,0:T(8,128)(2,1)S(1)}, u32[]{:S(2)}, u32[]{:S(2)}) %all-to-all-start) | async-done | bytes 2097184 | tf_op jit(solution)/shard_map/all_to_all | solution.py:26
  37.5 0.6 gather_fusion.1
  38.2 0.1 pad_add_fusion.1
  38.2 11.4 %copy.33 = bf16[1,4,1024,1024]{2,3,1,0:T(8,128)(2,1)} copy(bf16[1,4,1024,1024]{3,2,1,0:T(8,128)(2,1)} %param.9) | data formatting | bytes 16777216 | tf_op args[0]
  49.7 8.2 %copy.34 = bf16[4,1024,8,128]{1,3,0,2:T(8,128)(2,1)} copy(bf16[4,1024,8,128]{1,3,2,0:T(8,128)(2,1)} %bitcast.139) | data formatting | bytes 16777216 | tf_op jit(solution)/shard_map/reshape;squeeze | solution.py:67
  57.9 6.1 %gather_fusion = bf16[4,4,1024,128]{2,3,1,0:T(8,128)(2,1)} fusion(bf16[4,1024,8,128]{1,3,0,2:T(8,128)(2,1)} %copy.34, s32[1024]{0:T(1024)S(1)} %pad_clamp_fusion.4), kind=kCustom, calls=%fused_computation | custom fusion | bytes 8388624 | tf_op jit(solution)/shard_map/jit(_take)/gather | solution.py:68
  64.1 6.2 %gather_fusion.2 = bf16[4,4,1024,128]{2,3,1,0:T(8,128)(2,1)} fusion(bf16[4,1024,8,128]{1,3,0,2:T(8,128)(2,1)} %copy.34, s32[1024]{0:T(1024)S(1)} %pad_clamp_fusion.2), kind=kCustom, calls=%fused_computation.2 | custom fusion | bytes 8388624 | tf_op jit(solution)/shard_map/jit(_take)/gather | solution.py:68
  70.4 0.1 broadcast_in_dim.70
  70.5 1.5 collective-permute-start.1
  72.1 0.1 collective-permute-start
  72.1 6.3 %fusion.84 = bf16[1,4,128,1024]{3,2,1,0:T(8,128)(2,1)S(1)} fusion(bf16[4,128,1024]{2,1,0:T(8,128)(2,1)S(1)} %gather_fusion.1, bf16[1,4,1024,1024]{3,2,1,0:T(8,128)(2,1)} %param.9), kind=kOutput, calls=%fused_computation.59 | convolution fusion | flops 1074266112 | bytes 10485760 | tf_op jit(solution)/shard_map/sik,sjk->sij/dot_general | solution.py:72
  78.5 16.4 %collective-permute-done.1 = bf16[4,128,1024]{2,1,0:T(8,128)(2,1)S(1)} collective-permute-done((bf16[4,128,1024]{2,1,0:T(8,128)(2,1)S(1)}, bf16[4,128,1024]{2,1,0:T(8,128)(2,1)S(1)}, u32[]{:S(2)}, u32[]{:S(2)}) %collective-permute-start.1) | collective-permute-done | bytes 1048608 | tf_op jit(solution)/shard_map/ppermute | solution.py:12
  94.9 0.1 slice_bitcast_fusion.3
  95.1 0.2 pad_maximum_fusion.3
  95.4 2.7 %collective-permute-start.4 = (bf16[2,4,64,1024]{3,2,1,0:T(8,128)(2,1)S(1)}, bf16[2,4,64,1024]{3,2,1,0:T(8,128)(2,1)S(1)}, u32[]{:S(2)}, u32[]{:S(2)}) collective-permute-start(bf16[2,4,64,1024]{3,2,1,0:T(8,128)(2,1)S(1)} %get-tuple-element.13), channel_id=1, source_target_pairs={{0,96},{16,112},{32,0},{48,16},{64,32},{80,48},{96,64},{112,80},{1... | collective-permute-start | bytes 3145736 | tf_op jit(solution)/shard_map/ppermute | solution.py:12
  98.1 6.4 %fusion.75 = bf16[1,4,128,1024]{3,2,1,0:T(8,128)(2,1)S(1)} fusion(bf16[4,128,1024]{2,1,0:T(8,128)(2,1)S(1)} %collective-permute-done.2, bf16[1,4,1024,1024]{3,2,1,0:T(8,128)(2,1)} %param.9), kind=kOutput, calls=%fused_computation.56 | convolution fusion | flops 1074266112 | bytes 10485760 | tf_op jit(solution)/shard_map/sik,sjk->sij/dot_general | solution.py:72
  104.6 3.0 %fusion.78 = bf16[1,4,128,1024]{3,2,1,0:T(8,128)(2,1)S(1)} fusion(bf16[4,128,1024]{2,1,0:T(8,128)(2,1)S(1)} %collective-permute-done.1, bf16[1,4,1024,1024]{3,2,1,0:T(8,128)(2,1)S(1)} %bitcast.138), kind=kOutput, calls=%fused_computation.57 | convolution fusion | flops 1074266112 | bytes 10485760 | tf_op jit(solution)/shard_map/sik,sjk->sij/dot_general | solution.py:72
  107.6 3.0 %fusion.81 = bf16[1,4,128,1024]{3,2,1,0:T(8,128)(2,1)S(1)} fusion(bf16[4,128,1024]{2,1,0:T(8,128)(2,1)S(1)} %collective-permute-done, bf16[1,4,1024,1024]{3,2,1,0:T(8,128)(2,1)S(1)} %bitcast.138), kind=kOutput, calls=%fused_computation.58 | convolution fusion | flops 1074266112 | bytes 10485760 | tf_op jit(solution)/shard_map/sik,sjk->sij/dot_general | solution.py:72
  110.6 6.1 %fusion.16 = f32[1024,1024,1,1]{1,0,3,2:T(8,128)} fusion(bf16[1,4,128,1024]{3,2,1,0:T(8,128)(2,1)S(1)} %fusion.75, bf16[1,4,128,1024]{3,2,1,0:T(8,128)(2,1)S(1)} %fusion.78, bf16[1,4,128,1024]{3,2,1,0:T(8,128)(2,1)S(1)} %fusion.81, bf16[1,4,128,1024]{3,2,1,0:T(8,128)(2,1)S(1)} %fusion.84, bf16[4,4,1024,128]{2,3,1,0:T(8,128)(2,1)S(1)} %copy-done.3), kind=kOutput, calls=%fused_computation.22 | convolution fusion | flops 4301258752 | bytes 12582912 | tf_op jit(solution)/shard_map/dot_general | solution.py:78
  116.7 2.1 collective-permute-done.3
  118.8 1.3 slice_bitcast_fusion.7
  120.2 0.1 slice_bitcast_fusion.1
  120.4 2.7 %collective-permute-start.7 = (bf16[4,32,1024]{2,1,0:T(8,128)(2,1)S(1)}, bf16[4,32,1024]{2,1,0:T(8,128)(2,1)S(1)}, u32[]{:S(2)}, u32[]{:S(2)}) collective-permute-start(bf16[4,32,1024]{2,1,0:T(8,128)(2,1)S(1)} %slice.89), channel_id=1, source_target_pairs={{0,96},{16,112},{32,0},{48,16},{64,32},{80,48},{96,64},{112,80},{1... | collective-permute-start | bytes 786440 | tf_op jit(solution)/shard_map/ppermute | solution.py:12
  123.2 2.9 %fusion.66 = bf16[1,4,128,1024]{3,2,1,0:T(8,128)(2,1)S(1)} fusion(bf16[1,4,1024,1024]{3,2,1,0:T(8,128)(2,1)S(1)} %bitcast.138, bf16[4,64,1024]{2,1,0:T(8,128)(2,1)S(1)} %get-tuple-element.7, bf16[4,64,1024]{2,1,0:T(8,128)(2,1)S(1)} %get-tuple-element.10), kind=kOutput, calls=%fused_computation.53 | convolution fusion | flops 1076363264 | bytes 10485760 | tf_op jit(solution)/shard_map/sik,sjk->sij/dot_general | solution.py:72
  126.1 2.9 %fusion.69 = bf16[1,4,128,1024]{3,2,1,0:T(8,128)(2,1)S(1)} fusion(bf16[1,4,1024,1024]{3,2,1,0:T(8,128)(2,1)S(1)} %bitcast.138, bf16[4,64,1024]{2,1,0:T(8,128)(2,1)S(1)} %get-tuple-element.6, bf16[4,64,1024]{2,1,0:T(8,128)(2,1)S(1)} %get-tuple-element.5), kind=kOutput, calls=%fused_computation.54 | convolution fusion | flops 1076363264 | bytes 10485760 | tf_op jit(solution)/shard_map/sik,sjk->sij/dot_general | solution.py:72
  129.0 2.9 %fusion.72 = bf16[1,4,128,1024]{3,2,1,0:T(8,128)(2,1)S(1)} fusion(bf16[1,4,1024,1024]{3,2,1,0:T(8,128)(2,1)S(1)} %bitcast.138, bf16[4,64,1024]{2,1,0:T(8,128)(2,1)S(1)} %get-tuple-element.11, bf16[4,64,1024]{2,1,0:T(8,128)(2,1)S(1)} %get-tuple-element.4), kind=kOutput, calls=%fused_computation.55 | convolution fusion | flops 1076363264 | bytes 10485760 | tf_op jit(solution)/shard_map/sik,sjk->sij/dot_general | solution.py:72
  131.9 0.5 collective-permute-done.8
  132.5 2.9 %fusion.63 = bf16[1,4,128,1024]{3,2,1,0:T(8,128)(2,1)S(1)} fusion(bf16[1,4,1024,1024]{3,2,1,0:T(8,128)(2,1)S(1)} %bitcast.138, bf16[4,64,1024]{2,1,0:T(8,128)(2,1)S(1)} %collective-permute-done.8, bf16[4,32,1024]{2,1,0:T(8,128)(2,1)S(1)} %collective-permute-done.7, bf16[4,32,1024]{2,1,0:T(8,128)(2,1)S(1)} %collective-permute-done.6), kind=kOutput, calls=%fused_computation.52 | convolution fusion | flops 1077411840 | bytes 10485760 | tf_op jit(solution)/shard_map/sik,sjk->sij/dot_general | solution.py:72
  135.4 6.7 %fusion.32 = bf16[1024,1024]{1,0:T(8,128)(2,1)S(1)} fusion(f32[1024,1024,1,1]{1,0,3,2:T(8,128)} %fusion.16, bf16[1,4,128,1024]{3,2,1,0:T(8,128)(2,1)S(1)} %fusion.63, bf16[1,4,128,1024]{3,2,1,0:T(8,128)(2,1)S(1)} %fusion.66, bf16[1,4,128,1024]{3,2,1,0:T(8,128)(2,1)S(1)} %fusion.69, bf16[1,4,128,1024]{3,2,1,0:T(8,128)(2,1)S(1)} %fusion.72, ...), kind=kOutput, calls=%fused_computation.39 | convolution fusion | flops 4303355904 | bytes 14680064 | tf_op jit(solution)/shard_map/dot_general | solution.py:78
  142.1 0.6 copy.50
  142.7 0.6 copy.38
  143.3 0.2 copy-done.4
  143.5 1.8 gather_fusion.3
  145.3 0.8 gather_fusion.4
  146.0 1.4 copy.39
  147.5 0.3 broadcast_in_dim.75
  147.7 0.9 fusion.87
  148.6 0.1 copy-done.1
  148.7 1.7 pad_maximum_fusion
  150.4 12.6 %all-to-all-start.1 = ((bf16[16,576,128]{2,1,0:T(8,128)(2,1)}), bf16[16,576,128]{2,1,0:T(8,128)(2,1)S(1)}, u32[]{:S(2)}, u32[]{:S(2)}) async-start(bf16[16,576,128]{2,1,0:T(8,128)(2,1)} %pad_maximum_fusion), calls=%async_computation.1 | async-start | bytes 4718592 | tf_op jit(solution)/shard_map/all_to_all | solution.py:103
  163.0 31.1 %all-to-all-done.1 = bf16[16,576,128]{2,1,0:T(8,128)(2,1)S(1)} async-done(((bf16[16,576,128]{2,1,0:T(8,128)(2,1)}), bf16[16,576,128]{2,1,0:T(8,128)(2,1)S(1)}, u32[]{:S(2)}, u32[]{:S(2)}) %all-to-all-start.1) | async-done | bytes 2359328 | tf_op jit(solution)/shard_map/all_to_all | solution.py:103
  194.1 0.2 fusion.122
  194.2 0.7 fusion.91
  195.1 1.3 gather_fusion.5
  196.3 0.1 all_to_all.14
  196.4 13.3 %all_to_all.19 = f32[16,1,8]{2,1,0:T(1,128)S(1)} all-to-all(f32[16,1,8]{2,1,0:T(1,128)S(1)} %bitcast.150), channel_id=1, replica_groups=mesh['tsink'=8,'mom'=16] {'mom'}, dimensions={0} | all-to-all | bytes 1024 | tf_op jit(solution)/shard_map/all_to_all | solution.py:111
  209.8 0.5 multiply_bitcast_fusion
  (52 shorter events, 0.8 us)
Async XLA Ops:
  0.6 6.3 %copy-start.9 = (s32[4]{0:T(128)S(1)}, s32[4]{0:T(128)}, u32[]{:S(2)}) copy-start(s32[4]{0:T(128)} %param.11) | copy-start | bytes 52
  0.6 36.8 %all-to-all-start = ((bf16[8,128,1024]{2,1,0:T(8,128)(2,1)}), bf16[8,128,1024]{2,1,0:T(8,128)(2,1)S(1)}, u32[]{:S(2)}, u32[]{:S(2)}) async-start(bf16[8,128,1024]{2,1,0:T(8,128)(2,1)} %bitcast.147), calls=%async_computation | async-start | bytes 4194304 | tf_op jit(solution)/shard_map/all_to_all | solution.py:26
  38.1 40.4 %collective-permute-start.2 = (bf16[4,128,1024]{2,1,0:T(8,128)(2,1)S(1)}, bf16[4,128,1024]{2,1,0:T(8,128)(2,1)S(1)}, u32[]{:S(2)}, u32[]{:S(2)}) collective-permute-start(bf16[4,128,1024]{2,1,0:T(8,128)(2,1)S(1)} %gather_fusion.1), channel_id=1, source_target_pairs={{0,96},{16,112},{32,0},{48,16},{64,32},{80,48},{96,64},{112,80},{1... | collective-permute-start | bytes 3145736 | tf_op jit(solution)/shard_map/ppermute | solution.py:12
  64.1 6.2 %copy-start.7 = (pred[36]{0:T(512)(128)(4,1)S(1)}, pred[36]{0:T(512)(128)(4,1)}, u32[]{:S(2)}) copy-start(pred[36]{0:T(512)(128)(4,1)} %constant.72) | copy-start | bytes 112
  64.1 6.4 %copy-start.6 = (s32[36]{0:T(128)S(1)}, s32[36]{0:T(128)}, u32[]{:S(2)}) copy-start(s32[36]{0:T(128)} %constant.87) | copy-start | bytes 436
  64.1 7.9 %copy-start.5 = (s32[36]{0:T(128)S(1)}, s32[36]{0:T(128)}, u32[]{:S(2)}) copy-start(s32[36]{0:T(128)} %constant.88) | copy-start | bytes 436
  70.5 24.4 %collective-permute-start.1 = (bf16[4,128,1024]{2,1,0:T(8,128)(2,1)S(1)}, bf16[4,128,1024]{2,1,0:T(8,128)(2,1)S(1)}, u32[]{:S(2)}, u32[]{:S(2)}) collective-permute-start(bf16[4,128,1024]{2,1,0:T(8,128)(2,1)S(1)} %gather_fusion.1), channel_id=1, source_target_pairs={{0,32},{16,48},{32,64},{48,80},{64,96},{80,112},{96,0},{112,16},{1... | collective-permute-start | bytes 3145736 | tf_op jit(solution)/shard_map/ppermute | solution.py:12
  72.1 23.0 %collective-permute-start = (bf16[4,128,1024]{2,1,0:T(8,128)(2,1)S(1)}, bf16[4,128,1024]{2,1,0:T(8,128)(2,1)S(1)}, u32[]{:S(2)}, u32[]{:S(2)}) collective-permute-start(bf16[4,128,1024]{2,1,0:T(8,128)(2,1)S(1)} %gather_fusion.1), channel_id=1, source_target_pairs={{0,16},{16,0},{32,48},{48,32},{64,80},{80,64},{96,112},{112,96},{1... | collective-permute-start | bytes 3145736 | tf_op jit(solution)/shard_map/ppermute | solution.py:16
  95.1 9.5 %slice-start = ((s8[8388608]{0:T(1024)(128)(4,1)}), s8[4194304]{0:T(1024)(128)(4,1)S(1)}, s32[]{:S(2)}) async-start(s8[8388608]{0:T(1024)(128)(4,1)} %bitcast.137), calls=%async_computation.3 | async-start | bytes 8388608
  95.4 23.4 %collective-permute-start.3 = (bf16[2,4,64,1024]{3,2,1,0:T(8,128)(2,1)S(1)}, bf16[2,4,64,1024]{3,2,1,0:T(8,128)(2,1)}, u32[]{:S(2)}, u32[]{:S(2)}) collective-permute-start(bf16[2,4,64,1024]{3,2,1,0:T(8,128)(2,1)S(1)} %get-tuple-element.14), channel_id=1, source_target_pairs={{0,32},{16,48},{32,64},{48,80},{64,96},{80,112},{96,0},{112,16},{1... | collective-permute-start | bytes 3145736 | tf_op jit(solution)/shard_map/ppermute | solution.py:12
  95.4 24.8 %collective-permute-start.4 = (bf16[2,4,64,1024]{3,2,1,0:T(8,128)(2,1)S(1)}, bf16[2,4,64,1024]{3,2,1,0:T(8,128)(2,1)S(1)}, u32[]{:S(2)}, u32[]{:S(2)}) collective-permute-start(bf16[2,4,64,1024]{3,2,1,0:T(8,128)(2,1)S(1)} %get-tuple-element.13), channel_id=1, source_target_pairs={{0,96},{16,112},{32,0},{48,16},{64,32},{80,48},{96,64},{112,80},{1... | collective-permute-start | bytes 3145736 | tf_op jit(solution)/shard_map/ppermute | solution.py:12
  98.1 6.5 %slice-start.1 = ((s8[8388608]{0:T(1024)(128)(4,1)}), s8[4194304]{0:T(1024)(128)(4,1)S(1)}, s32[]{:S(2)}) async-start(s8[8388608]{0:T(1024)(128)(4,1)} %bitcast.137), calls=%async_computation.4 | async-start | bytes 8388608
  98.1 25.0 %collective-permute-start.5 = (bf16[2,4,64,1024]{3,2,1,0:T(8,128)(2,1)S(1)}, bf16[2,4,64,1024]{3,2,1,0:T(8,128)(2,1)S(1)}, u32[]{:S(2)}, u32[]{:S(2)}) collective-permute-start(bf16[2,4,64,1024]{3,2,1,0:T(8,128)(2,1)S(1)} %get-tuple-element.12), channel_id=1, source_target_pairs={{0,16},{16,0},{32,48},{48,32},{64,80},{80,64},{96,112},{112,96},{1... | collective-permute-start | bytes 3145736 | tf_op jit(solution)/shard_map/ppermute | solution.py:16
  107.6 3.0 %copy-start.3 = (bf16[4,4,1024,128]{2,3,1,0:T(8,128)(2,1)S(1)}, bf16[4,4,1024,128]{2,3,1,0:T(8,128)(2,1)}, u32[]{:S(2)}) copy-start(bf16[4,4,1024,128]{2,3,1,0:T(8,128)(2,1)} %gather_fusion) | copy-start | bytes 12582916
  120.1 11.8 %collective-permute-start.6 = (bf16[4,32,1024]{2,1,0:T(8,128)(2,1)S(1)}, bf16[4,32,1024]{2,1,0:T(8,128)(2,1)S(1)}, u32[]{:S(2)}, u32[]{:S(2)}) collective-permute-start(bf16[4,32,1024]{2,1,0:T(8,128)(2,1)S(1)} %slice.88), channel_id=1, source_target_pairs={{0,32},{16,48},{32,64},{48,80},{64,96},{80,112},{96,0},{112,16},{1... | collective-permute-start | bytes 786440 | tf_op jit(solution)/shard_map/ppermute | solution.py:12
  120.4 11.6 %collective-permute-start.7 = (bf16[4,32,1024]{2,1,0:T(8,128)(2,1)S(1)}, bf16[4,32,1024]{2,1,0:T(8,128)(2,1)S(1)}, u32[]{:S(2)}, u32[]{:S(2)}) collective-permute-start(bf16[4,32,1024]{2,1,0:T(8,128)(2,1)S(1)} %slice.89), channel_id=1, source_target_pairs={{0,96},{16,112},{32,0},{48,16},{64,32},{80,48},{96,64},{112,80},{1... | collective-permute-start | bytes 786440 | tf_op jit(solution)/shard_map/ppermute | solution.py:12
  123.1 9.4 %collective-permute-start.8 = (bf16[4,64,1024]{2,1,0:T(8,128)(2,1)S(1)}, bf16[4,64,1024]{2,1,0:T(8,128)(2,1)S(1)}, u32[]{:S(2)}, u32[]{:S(2)}) collective-permute-start(bf16[4,64,1024]{2,1,0:T(8,128)(2,1)S(1)} %get-tuple-element.11), channel_id=1, source_target_pairs={{0,16},{16,0},{32,48},{48,32},{64,80},{80,64},{96,112},{112,96},{1... | collective-permute-start | bytes 1572872 | tf_op jit(solution)/shard_map/ppermute | solution.py:16
  131.9 3.5 %copy-start.2 = (bf16[4,4,1024,128]{2,3,1,0:T(8,128)(2,1)S(1)}, bf16[4,4,1024,128]{2,3,1,0:T(8,128)(2,1)}, u32[]{:S(2)}) copy-start(bf16[4,4,1024,128]{2,3,1,0:T(8,128)(2,1)} %gather_fusion.2) | copy-start | bytes 12582916
  142.1 1.4 copy-start.4
  146.0 1.7 copy-start
  147.5 1.3 copy-start.1
  150.4 12.6 %copy-start.8 = (s32[128,2]{0,1:T(2,128)S(1)}, s32[128,2]{0,1:T(2,128)}, u32[]{:S(2)}) copy-start(s32[128,2]{0,1:T(2,128)} %param.12) | copy-start | bytes 3076
  150.4 43.7 %all-to-all-start.1 = ((bf16[16,576,128]{2,1,0:T(8,128)(2,1)}), bf16[16,576,128]{2,1,0:T(8,128)(2,1)S(1)}, u32[]{:S(2)}, u32[]{:S(2)}) async-start(bf16[16,576,128]{2,1,0:T(8,128)(2,1)} %pad_maximum_fusion), calls=%async_computation.1 | async-start | bytes 4718592 | tf_op jit(solution)/shard_map/all_to_all | solution.py:103

commit v6 on v3

--- a/solution.py
+++ b/solution.py
@@ -110,8 +110,8 @@
     partial = lax.dot_general(
         own_rows, own_cols, (((1,), (1,)), ((), ())), preferred_element_type=jnp.float32
     )
-    partial = partial + partial.T
-    per_diagram = partial[diagrams[:, 0], diagrams[:, 1]]
+    first, second = diagrams[:, 0], diagrams[:, 1]
+    per_diagram = partial[first, second] + partial[second, first]
     spread = lax.all_to_all(per_diagram.reshape(n_m, -1), "mom", 0, 0)
     correlators = (jnp.sum(spread, axis=0) / block_order)[:, None]
     return (meson[None, None], correlators)

time: 182 us -> 183 us (level)
  no operation moved by 1% of the time
where the time goes in v6:
time: 183 us
  waiting for transfers between devices  57.8 us (32%)
  matrix products  41.3 us (23%)
  local copies, waits for them, and re-layouts  38 us (21%)
  starting transfers between devices  26.4 us (14%)
  blocking collectives  13.3 us (7%)
  other arithmetic  4.78 us (3%)
    all_to_all x1, waiting for transfers between devices, body(): received = lax.all_to_all(slices, 'mom', 0, 0)  31.1 us
    dot_general x8, matrix products, stacked(): jnp.einsum('sik,sjk->sij', piece, propagators, preferred_element_type=jnp...  27.2 us
    unnamed x42, local copies, waits for them, and re-layouts  20.8 us
    ppermute x6, waiting for transfers between devices, shifted(): return lax.ppermute(block, 'tsink', pairs)  19.4 us
    dot_general x2, matrix products, stacked(): jnp.dot(columns, blocks.reshape(-1, block_order), preferred_element_type=...  13.4 us
    all_to_all x1, blocking collectives, body(): spread = lax.all_to_all(per_diagram.reshape(n_m, -1), 'mom', 0, 0)  13.3 us
    all_to_all x1, starting transfers between devices, body(): received = lax.all_to_all(slices, 'mom', 0, 0)  12.7 us
    ppermute x6, starting transfers between devices, shifted(): return lax.ppermute(block, 'tsink', pairs)  7.06 us
  transfers between devices with their start and end apart: 11, of which 6 were waited for; matrix products, arithmetic and copies ran while one was open for 32% of the time, Pallas kernels for 0%

profile of v6, /device:TPU:1, one launch (start us, length us, event | category | flops | bytes accessed | tf_op | source)
XLA Modules:
  0.0 182.7 jit_solution(12675253619465861872)
XLA Ops:
  0.6 6.2 %all-to-all-start = ((bf16[8,128,1024]{2,1,0:T(8,128)(2,1)}), bf16[8,128,1024]{2,1,0:T(8,128)(2,1)}, u32[]{:S(2)}, u32[]{:S(2)}) async-start(bf16[8,128,1024]{2,1,0:T(8,128)(2,1)} %bitcast.191), calls=%async_computation | async-start | bytes 4194304 | tf_op jit(solution)/shard_map/all_to_all | solution.py:26
  6.9 5.8 %fusion.93 = (bf16[1,1,1024,1024]{3,2,1,0:T(8,128)(2,1)S(1)}, bf16[1,1,1024,1024]{3,2,1,0:T(8,128)(2,1)}, bf16[1,1,1024,1024]{3,2,1,0:T(8,128)(2,1)}, bf16[1,1,1024,1024]{3,2,1,0:T(8,128)(2,1)}) fusion(bf16[1,4,1024,1024]{3,2,1,0:T(8,128)(2,1)} %param.9), kind=kLoop, calls=%fused_computation.124 | loop fusion | bytes 16777216 | tf_op jit(solution)/shard_map/slice | solution.py:68
  12.9 2.1 %bitcast_dynamic-update-slice_fusion.15 = (bf16[1024,2048]{1,0:T(8,128)(2,1)}, bf16[1024,2048]{1,0:T(8,128)(2,1)}) fusion(bf16[1,1,1024,1024]{3,2,1,0:T(8,128)(2,1)} %get-tuple-element.5, s32[]{:T(128)S(6)} %select_n.117, s32[]{:T(128)S(6)} %select_n.109), kind=kLoop, calls=%fused_computation.89 | loop fusion | bytes 1048584
  15.0 2.0 %bitcast_dynamic-update-slice_fusion.14 = (bf16[1024,2048]{1,0:T(8,128)(2,1)}, bf16[1024,2048]{1,0:T(8,128)(2,1)}) fusion(bf16[1024,2048]{1,0:T(8,128)(2,1)} %get-tuple-element.38, bf16[1,1,1024,1024]{3,2,1,0:T(8,128)(2,1)} %get-tuple-element.4, s32[]{:T(128)S(6)} %select_n.117, bf16[1024,2048]{1,0:T(8,128)(2,1)} %get-tuple-element.39, s32[]{:T(128)S(6)} %select_n.109), kind=kLoop, calls=%fused_computation.88 | loop fusion | bytes 1048584
  17.0 1.9 %bitcast_dynamic-update-slice_fusion.13 = (bf16[1024,2048]{1,0:T(8,128)(2,1)}, bf16[1024,2048]{1,0:T(8,128)(2,1)}) fusion(bf16[1024,2048]{1,0:T(8,128)(2,1)} %get-tuple-element.36, bf16[1,1,1024,1024]{3,2,1,0:T(8,128)(2,1)} %get-tuple-element.3, s32[]{:T(128)S(6)} %select_n.117, bf16[1024,2048]{1,0:T(8,128)(2,1)} %get-tuple-element.37, s32[]{:T(128)S(6)} %select_n.109), kind=kLoop, calls=%fused_computation.87 | loop fusion | bytes 1048584
  19.0 1.0 bitcast_dynamic-update-slice_fusion.12
  20.0 1.9 %bitcast_dynamic-update-slice_fusion.11 = (bf16[1024,2048]{1,0:T(8,128)(2,1)}, bf16[1024,2048]{1,0:T(8,128)(2,1)}) fusion(bf16[1024,2048]{1,0:T(8,128)(2,1)} %get-tuple-element.32, bf16[1,1,1024,1024]{3,2,1,0:T(8,128)(2,1)} %get-tuple-element.5, s32[]{:T(128)S(6)} %select_n.118, bf16[1024,2048]{1,0:T(8,128)(2,1)} %get-tuple-element.33, s32[]{:T(128)S(6)} %select_n.110), kind=kLoop, calls=%fused_computation.85 | loop fusion | bytes 1048584
  21.9 1.0 bitcast_dynamic-update-slice_fusion.10
  23.0 1.0 bitcast_dynamic-update-slice_fusion.9
  23.9 1.0 bitcast_dynamic-update-slice_fusion.8
  24.9 1.0 bitcast_dynamic-update-slice_fusion.7
  25.9 1.0 bitcast_dynamic-update-slice_fusion.6
  26.9 1.0 bitcast_dynamic-update-slice_fusion.5
  27.9 1.0 bitcast_dynamic-update-slice_fusion.4
  28.9 1.0 bitcast_dynamic-update-slice_fusion.3
  29.9 1.0 bitcast_dynamic-update-slice_fusion.2
  30.9 6.7 %all-to-all-done = bf16[8,128,1024]{2,1,0:T(8,128)(2,1)} async-done(((bf16[8,128,1024]{2,1,0:T(8,128)(2,1)}), bf16[8,128,1024]{2,1,0:T(8,128)(2,1)}, u32[]{:S(2)}, u32[]{:S(2)}) %all-to-all-start) | async-done | bytes 2097184 | tf_op jit(solution)/shard_map/all_to_all | solution.py:26
  37.6 2.2 %gather_fusion = bf16[4,128,1024]{2,1,0:T(8,128)(2,1)S(1)} fusion(bf16[8,128,1024]{2,1,0:T(8,128)(2,1)} %all-to-all-done, s32[1024]{0:T(1024)S(1)} %pad_clamp_fusion.2), kind=kCustom, calls=%fused_computation | custom fusion | bytes 2097168 | tf_op jit(solution)/shard_map/gather | solution.py:27
  39.9 1.9 %bitcast_dynamic-update-slice_fusion.1 = (bf16[1024,2048]{1,0:T(8,128)(2,1)}, bf16[1024,2048]{1,0:T(8,128)(2,1)}) fusion(bf16[1024,2048]{1,0:T(8,128)(2,1)} %get-tuple-element.12, bf16[1,1,1024,1024]{3,2,1,0:T(8,128)(2,1)} %get-tuple-element.3, s32[]{:T(128)S(6)} %select_n.120, bf16[1024,2048]{1,0:T(8,128)(2,1)} %get-tuple-element.13, s32[]{:T(128)S(6)} %select_n.114), kind=kLoop, calls=%fused_computation.75 | loop fusion | bytes 1048584
  41.8 1.4 collective-permute-start.1
  43.3 1.0 bitcast_dynamic-update-slice_fusion
  44.3 6.7 %fusion.61 = bf16[1,4,128,1024]{3,2,1,0:T(8,128)(2,1)S(1)} fusion(bf16[4,128,1024]{2,1,0:T(8,128)(2,1)S(1)} %gather_fusion, bf16[1,4,1024,1024]{3,2,1,0:T(8,128)(2,1)} %param.9), kind=kOutput, calls=%fused_computation.41 | convolution fusion | flops 1074266112 | bytes 10485760 | tf_op jit(solution)/shard_map/sik,sjk->sij/dot_general | solution.py:76
  51.0 12.0 %collective-permute-done.2 = bf16[4,128,1024]{2,1,0:T(8,128)(2,1)S(1)} collective-permute-done((bf16[4,128,1024]{2,1,0:T(8,128)(2,1)S(1)}, bf16[4,128,1024]{2,1,0:T(8,128)(2,1)S(1)}, u32[]{:S(2)}, u32[]{:S(2)}) %collective-permute-start.2) | collective-permute-done | bytes 1048608 | tf_op jit(solution)/shard_map/ppermute | solution.py:12
  63.0 3.1 %collective-permute-done.1 = bf16[4,128,1024]{2,1,0:T(8,128)(2,1)S(1)} collective-permute-done((bf16[4,128,1024]{2,1,0:T(8,128)(2,1)S(1)}, bf16[4,128,1024]{2,1,0:T(8,128)(2,1)S(1)}, u32[]{:S(2)}, u32[]{:S(2)}) %collective-permute-start.1) | collective-permute-done | bytes 1048608 | tf_op jit(solution)/shard_map/ppermute | solution.py:12
  67.5 2.4 %collective-permute-start.4 = (bf16[2,4,64,1024]{3,2,1,0:T(8,128)(2,1)S(1)}, bf16[2,4,64,1024]{3,2,1,0:T(8,128)(2,1)S(1)}, u32[]{:S(2)}, u32[]{:S(2)}) collective-permute-start(bf16[2,4,64,1024]{3,2,1,0:T(8,128)(2,1)S(1)} %get-tuple-element.49), channel_id=1, source_target_pairs={{0,96},{16,112},{32,0},{48,16},{64,32},{80,48},{96,64},{112,80},{1... | collective-permute-start | bytes 3145736 | tf_op jit(solution)/shard_map/ppermute | solution.py:12
  70.1 2.9 %fusion.52 = bf16[1,4,128,1024]{3,2,1,0:T(8,128)(2,1)S(1)} fusion(bf16[4,128,1024]{2,1,0:T(8,128)(2,1)S(1)} %collective-permute-done.2, bf16[1,4,1024,1024]{3,2,1,0:T(8,128)(2,1)S(1)} %bitcast.181), kind=kOutput, calls=%fused_computation.38 | convolution fusion | flops 1074266112 | bytes 10485760 | tf_op jit(solution)/shard_map/sik,sjk->sij/dot_general | solution.py:76
  73.0 3.0 %fusion.55 = bf16[1,4,128,1024]{3,2,1,0:T(8,128)(2,1)S(1)} fusion(bf16[4,128,1024]{2,1,0:T(8,128)(2,1)S(1)} %collective-permute-done.1, bf16[1,4,1024,1024]{3,2,1,0:T(8,128)(2,1)S(1)} %bitcast.181), kind=kOutput, calls=%fused_computation.39 | convolution fusion | flops 1074266112 | bytes 10485760 | tf_op jit(solution)/shard_map/sik,sjk->sij/dot_general | solution.py:76
  76.0 2.9 %fusion.58 = bf16[1,4,128,1024]{3,2,1,0:T(8,128)(2,1)S(1)} fusion(bf16[4,128,1024]{2,1,0:T(8,128)(2,1)S(1)} %collective-permute-done, bf16[1,4,1024,1024]{3,2,1,0:T(8,128)(2,1)S(1)} %bitcast.181), kind=kOutput, calls=%fused_computation.40 | convolution fusion | flops 1074266112 | bytes 10485760 | tf_op jit(solution)/shard_map/sik,sjk->sij/dot_general | solution.py:76
  79.5 6.4 %fusion.95 = f32[1024,1024]{1,0:T(8,128)S(1)} fusion(bf16[1024,2048]{1,0:T(8,128)(2,1)} %get-tuple-element.9, bf16[2048,1024]{1,0:T(8,128)(2,1)S(1)} %bitcast.190), kind=kOutput, calls=%fused_computation.126 | convolution fusion | flops 4294967296 | bytes 12582912 | tf_op jit(solution)/shard_map/dot_general | solution.py:82
  85.9 4.3 %collective-permute-done.3 = bf16[2,4,64,1024]{3,2,1,0:T(8,128)(2,1)S(1)} collective-permute-done((bf16[2,4,64,1024]{3,2,1,0:T(8,128)(2,1)S(1)}, bf16[2,4,64,1024]{3,2,1,0:T(8,128)(2,1)S(1)}, u32[]{:S(2)}, u32[]{:S(2)}) %collective-permute-start.3) | collective-permute-done | bytes 1048608 | tf_op jit(solution)/shard_map/ppermute | solution.py:12
  90.5 2.7 %collective-permute-start.7 = (bf16[4,32,1024]{2,1,0:T(8,128)(2,1)S(1)}, bf16[4,32,1024]{2,1,0:T(8,128)(2,1)S(1)}, u32[]{:S(2)}, u32[]{:S(2)}) collective-permute-start(bf16[4,32,1024]{2,1,0:T(8,128)(2,1)S(1)} %slice.135), channel_id=1, source_target_pairs={{0,96},{16,112},{32,0},{48,16},{64,32},{80,48},{96,64},{112,80},{1... | collective-permute-start | bytes 786440 | tf_op jit(solution)/shard_map/ppermute | solution.py:12
  93.6 2.9 %fusion.43 = bf16[1,4,128,1024]{3,2,1,0:T(8,128)(2,1)S(1)} fusion(bf16[1,4,1024,1024]{3,2,1,0:T(8,128)(2,1)S(1)} %bitcast.181, bf16[4,64,1024]{2,1,0:T(8,128)(2,1)S(1)} %get-tuple-element.43, bf16[4,64,1024]{2,1,0:T(8,128)(2,1)S(1)} %get-tuple-element.46), kind=kOutput, calls=%fused_computation.35 | convolution fusion | flops 1076363264 | bytes 10485760 | tf_op jit(solution)/shard_map/sik,sjk->sij/dot_general | solution.py:76
  96.5 2.9 %fusion.46 = bf16[1,4,128,1024]{3,2,1,0:T(8,128)(2,1)S(1)} fusion(bf16[1,4,1024,1024]{3,2,1,0:T(8,128)(2,1)S(1)} %bitcast.181, bf16[4,64,1024]{2,1,0:T(8,128)(2,1)S(1)} %get-tuple-element.42, bf16[4,64,1024]{2,1,0:T(8,128)(2,1)S(1)} %get-tuple-element.41), kind=kOutput, calls=%fused_computation.36 | convolution fusion | flops 1076363264 | bytes 10485760 | tf_op jit(solution)/shard_map/sik,sjk->sij/dot_general | solution.py:76
  99.4 2.9 %fusion.49 = bf16[1,4,128,1024]{3,2,1,0:T(8,128)(2,1)S(1)} fusion(bf16[1,4,1024,1024]{3,2,1,0:T(8,128)(2,1)S(1)} %bitcast.181, bf16[4,64,1024]{2,1,0:T(8,128)(2,1)S(1)} %get-tuple-element.47, bf16[4,64,1024]{2,1,0:T(8,128)(2,1)S(1)} %get-tuple-element.40), kind=kOutput, calls=%fused_computation.37 | convolution fusion | flops 1076363264 | bytes 10485760 | tf_op jit(solution)/shard_map/sik,sjk->sij/dot_general | solution.py:76
  102.4 2.9 %fusion.40 = bf16[1,4,128,1024]{3,2,1,0:T(8,128)(2,1)S(1)} fusion(bf16[1,4,1024,1024]{3,2,1,0:T(8,128)(2,1)S(1)} %bitcast.181, bf16[4,64,1024]{2,1,0:T(8,128)(2,1)S(1)} %collective-permute-done.8, bf16[4,32,1024]{2,1,0:T(8,128)(2,1)S(1)} %collective-permute-done.7, bf16[4,32,1024]{2,1,0:T(8,128)(2,1)S(1)} %collective-permute-done.6), kind=kOutput, calls=%fused_computation.34 | convolution fusion | flops 1077411840 | bytes 10485760 | tf_op jit(solution)/shard_map/sik,sjk->sij/dot_general | solution.py:76
  105.3 0.8 pad_maximum_fusion.1
  106.1 7.0 %add_convert_fusion = bf16[1024,1024]{1,0:T(8,128)(2,1)S(1)} fusion(f32[1024,1024]{1,0:T(8,128)S(1)} %fusion.95, bf16[1024,2048]{1,0:T(8,128)(2,1)} %get-tuple-element.8, bf16[2048,1024]{1,0:T(8,128)(2,1)S(1)} %bitcast.189), kind=kOutput, calls=%fused_computation.23 | convolution fusion | flops 4297064448 | bytes 14680064 | tf_op jit(solution)/shard_map/dot_general | solution.py:82
  114.5 1.8 %gather_fusion.1 = bf16[36,128,128]{2,1,0:T(8,128)(2,1)} fusion(bf16[64,128,128]{2,1,0:T(8,128)(2,1)S(1)} %bitcast.182, s32[1024]{0:T(1024)S(1)} %get-tuple-element.54), kind=kCustom, calls=%fused_computation.1 | custom fusion | bytes 2359440 | tf_op jit(solution)/shard_map/gather | solution.py:94
  116.3 0.8 gather_fusion.2
  117.1 1.4 copy.18
  118.8 0.9 fusion.64
  119.8 1.7 pad_maximum_fusion.2
  121.5 12.7 %all-to-all-start.1 = ((bf16[16,576,128]{2,1,0:T(8,128)(2,1)}), bf16[16,576,128]{2,1,0:T(8,128)(2,1)S(1)}, u32[]{:S(2)}, u32[]{:S(2)}) async-start(bf16[16,576,128]{2,1,0:T(8,128)(2,1)} %pad_maximum_fusion.2), calls=%async_computation.1 | async-start | bytes 4718592 | tf_op jit(solution)/shard_map/all_to_all | solution.py:107
  134.2 31.1 %all-to-all-done.1 = bf16[16,576,128]{2,1,0:T(8,128)(2,1)S(1)} async-done(((bf16[16,576,128]{2,1,0:T(8,128)(2,1)}), bf16[16,576,128]{2,1,0:T(8,128)(2,1)S(1)}, u32[]{:S(2)}, u32[]{:S(2)}) %all-to-all-start.1) | async-done | bytes 2359328 | tf_op jit(solution)/shard_map/all_to_all | solution.py:107
  165.4 0.7 fusion.68
  166.2 1.3 gather_fusion.3
  167.4 1.3 gather_fusion.4
  168.8 13.3 %all_to_all.16 = f32[16,1,8]{2,1,0:T(1,128)S(1)} all-to-all(f32[16,1,8]{2,1,0:T(1,128)S(1)} %bitcast.194), channel_id=1, replica_groups=mesh['tsink'=8,'mom'=16] {'mom'}, dimensions={0} | all-to-all | bytes 1024 | tf_op jit(solution)/shard_map/all_to_all | solution.py:115
  (64 shorter events, 5.6 us)
Async XLA Ops:
  0.6 36.9 %all-to-all-start = ((bf16[8,128,1024]{2,1,0:T(8,128)(2,1)}), bf16[8,128,1024]{2,1,0:T(8,128)(2,1)}, u32[]{:S(2)}, u32[]{:S(2)}) async-start(bf16[8,128,1024]{2,1,0:T(8,128)(2,1)} %bitcast.191), calls=%async_computation | async-start | bytes 4194304 | tf_op jit(solution)/shard_map/all_to_all | solution.py:26
  6.8 5.8 %copy-start.10 = (s32[4]{0:T(128)S(1)}, s32[4]{0:T(128)}, u32[]{:S(2)}) copy-start(s32[4]{0:T(128)} %param.11) | copy-start | bytes 52
  6.8 5.8 %copy-start.9 = (pred[36]{0:T(512)(128)(4,1)S(1)}, pred[36]{0:T(512)(128)(4,1)}, u32[]{:S(2)}) copy-start(pred[36]{0:T(512)(128)(4,1)} %constant.109) | copy-start | bytes 112
  12.9 9.1 %copy-start.1 = (bf16[1,1,1024,1024]{3,2,1,0:T(8,128)(2,1)S(1)}, bf16[1,1,1024,1024]{3,2,1,0:T(8,128)(2,1)}, u32[]{:S(2)}) copy-start(bf16[1,1,1024,1024]{3,2,1,0:T(8,128)(2,1)} %get-tuple-element.4) | copy-start | bytes 6291460
  12.9 10.1 %copy-start = (bf16[1,1,1024,1024]{3,2,1,0:T(8,128)(2,1)S(1)}, bf16[1,1,1024,1024]{3,2,1,0:T(8,128)(2,1)}, u32[]{:S(2)}) copy-start(bf16[1,1,1024,1024]{3,2,1,0:T(8,128)(2,1)} %get-tuple-element.3) | copy-start | bytes 6291460
  12.9 12.0 %copy-start.2 = (bf16[1,1,1024,1024]{3,2,1,0:T(8,128)(2,1)S(1)}, bf16[1,1,1024,1024]{3,2,1,0:T(8,128)(2,1)}, u32[]{:S(2)}) copy-start(bf16[1,1,1024,1024]{3,2,1,0:T(8,128)(2,1)} %get-tuple-element.5) | copy-start | bytes 6291460
  25.9 17.3 %copy-start.7 = (s32[36]{0:T(128)S(1)}, s32[36]{0:T(128)}, u32[]{:S(2)}) copy-start(s32[36]{0:T(128)} %constant.137) | copy-start | bytes 436
  25.9 17.3 %copy-start.8 = (s32[36]{0:T(128)S(1)}, s32[36]{0:T(128)}, u32[]{:S(2)}) copy-start(s32[36]{0:T(128)} %constant.138) | copy-start | bytes 436
  39.8 23.2 %collective-permute-start.2 = (bf16[4,128,1024]{2,1,0:T(8,128)(2,1)S(1)}, bf16[4,128,1024]{2,1,0:T(8,128)(2,1)S(1)}, u32[]{:S(2)}, u32[]{:S(2)}) collective-permute-start(bf16[4,128,1024]{2,1,0:T(8,128)(2,1)S(1)} %gather_fusion), channel_id=1, source_target_pairs={{0,96},{16,112},{32,0},{48,16},{64,32},{80,48},{96,64},{112,80},{1... | collective-permute-start | bytes 3145736 | tf_op jit(solution)/shard_map/ppermute | solution.py:12
  41.8 24.4 %collective-permute-start.1 = (bf16[4,128,1024]{2,1,0:T(8,128)(2,1)S(1)}, bf16[4,128,1024]{2,1,0:T(8,128)(2,1)S(1)}, u32[]{:S(2)}, u32[]{:S(2)}) collective-permute-start(bf16[4,128,1024]{2,1,0:T(8,128)(2,1)S(1)} %gather_fusion), channel_id=1, source_target_pairs={{0,32},{16,48},{32,64},{48,80},{64,96},{80,112},{96,0},{112,16},{1... | collective-permute-start | bytes 3145736 | tf_op jit(solution)/shard_map/ppermute | solution.py:12
  43.3 26.8 %slice-start = ((s8[8388608]{0:T(1024)(128)(4,1)}), s8[4194304]{0:T(1024)(128)(4,1)S(1)}, s32[]{:S(2)}) async-start(s8[8388608]{0:T(1024)(128)(4,1)} %bitcast.180), calls=%async_computation.3 | async-start | bytes 8388608
  44.3 25.8 %slice-start.1 = ((s8[8388608]{0:T(1024)(128)(4,1)}), s8[4194304]{0:T(1024)(128)(4,1)S(1)}, s32[]{:S(2)}) async-start(s8[8388608]{0:T(1024)(128)(4,1)} %bitcast.180), calls=%async_computation.4 | async-start | bytes 8388608
  44.3 22.6 %collective-permute-start = (bf16[4,128,1024]{2,1,0:T(8,128)(2,1)S(1)}, bf16[4,128,1024]{2,1,0:T(8,128)(2,1)S(1)}, u32[]{:S(2)}, u32[]{:S(2)}) collective-permute-start(bf16[4,128,1024]{2,1,0:T(8,128)(2,1)S(1)} %gather_fusion), channel_id=1, source_target_pairs={{0,16},{16,0},{32,48},{48,32},{64,80},{80,64},{96,112},{112,96},{1... | collective-permute-start | bytes 3145736 | tf_op jit(solution)/shard_map/ppermute | solution.py:16
  67.2 23.0 %collective-permute-start.3 = (bf16[2,4,64,1024]{3,2,1,0:T(8,128)(2,1)S(1)}, bf16[2,4,64,1024]{3,2,1,0:T(8,128)(2,1)S(1)}, u32[]{:S(2)}, u32[]{:S(2)}) collective-permute-start(bf16[2,4,64,1024]{3,2,1,0:T(8,128)(2,1)S(1)} %get-tuple-element.50), channel_id=1, source_target_pairs={{0,32},{16,48},{32,64},{48,80},{64,96},{80,112},{96,0},{112,16},{1... | collective-permute-start | bytes 3145736 | tf_op jit(solution)/shard_map/ppermute | solution.py:12
  67.5 22.8 %collective-permute-start.4 = (bf16[2,4,64,1024]{3,2,1,0:T(8,128)(2,1)S(1)}, bf16[2,4,64,1024]{3,2,1,0:T(8,128)(2,1)S(1)}, u32[]{:S(2)}, u32[]{:S(2)}) collective-permute-start(bf16[2,4,64,1024]{3,2,1,0:T(8,128)(2,1)S(1)} %get-tuple-element.49), channel_id=1, source_target_pairs={{0,96},{16,112},{32,0},{48,16},{64,32},{80,48},{96,64},{112,80},{1... | collective-permute-start | bytes 3145736 | tf_op jit(solution)/shard_map/ppermute | solution.py:12
  69.9 23.6 %collective-permute-start.5 = (bf16[2,4,64,1024]{3,2,1,0:T(8,128)(2,1)S(1)}, bf16[2,4,64,1024]{3,2,1,0:T(8,128)(2,1)S(1)}, u32[]{:S(2)}, u32[]{:S(2)}) collective-permute-start(bf16[2,4,64,1024]{3,2,1,0:T(8,128)(2,1)S(1)} %get-tuple-element.48), channel_id=1, source_target_pairs={{0,16},{16,0},{32,48},{48,32},{64,80},{80,64},{96,112},{112,96},{1... | collective-permute-start | bytes 3145736 | tf_op jit(solution)/shard_map/ppermute | solution.py:16
  90.3 12.1 %collective-permute-start.6 = (bf16[4,32,1024]{2,1,0:T(8,128)(2,1)S(1)}, bf16[4,32,1024]{2,1,0:T(8,128)(2,1)S(1)}, u32[]{:S(2)}, u32[]{:S(2)}) collective-permute-start(bf16[4,32,1024]{2,1,0:T(8,128)(2,1)S(1)} %slice.134), channel_id=1, source_target_pairs={{0,32},{16,48},{32,64},{48,80},{64,96},{80,112},{96,0},{112,16},{1... | collective-permute-start | bytes 786440 | tf_op jit(solution)/shard_map/ppermute | solution.py:12
  90.5 11.9 %collective-permute-start.7 = (bf16[4,32,1024]{2,1,0:T(8,128)(2,1)S(1)}, bf16[4,32,1024]{2,1,0:T(8,128)(2,1)S(1)}, u32[]{:S(2)}, u32[]{:S(2)}) collective-permute-start(bf16[4,32,1024]{2,1,0:T(8,128)(2,1)S(1)} %slice.135), channel_id=1, source_target_pairs={{0,96},{16,112},{32,0},{48,16},{64,32},{80,48},{96,64},{112,80},{1... | collective-permute-start | bytes 786440 | tf_op jit(solution)/shard_map/ppermute | solution.py:12
  93.2 9.2 %collective-permute-start.8 = (bf16[4,64,1024]{2,1,0:T(8,128)(2,1)S(1)}, bf16[4,64,1024]{2,1,0:T(8,128)(2,1)S(1)}, u32[]{:S(2)}, u32[]{:S(2)}) collective-permute-start(bf16[4,64,1024]{2,1,0:T(8,128)(2,1)S(1)} %get-tuple-element.47), channel_id=1, source_target_pairs={{0,16},{16,0},{32,48},{48,32},{64,80},{80,64},{96,112},{112,96},{1... | collective-permute-start | bytes 1572872 | tf_op jit(solution)/shard_map/ppermute | solution.py:16
  113.1 1.4 copy-start.5
  117.1 1.7 copy-start.3
  118.5 1.3 copy-start.4
  119.8 14.3 %copy-start.6 = (s32[128,2]{0,1:T(2,128)S(1)}, s32[128,2]{0,1:T(2,128)}, u32[]{:S(2)}) copy-start(s32[128,2]{0,1:T(2,128)} %param.12) | copy-start | bytes 3076
  121.5 43.8 %all-to-all-start.1 = ((bf16[16,576,128]{2,1,0:T(8,128)(2,1)}), bf16[16,576,128]{2,1,0:T(8,128)(2,1)S(1)}, u32[]{:S(2)}, u32[]{:S(2)}) async-start(bf16[16,576,128]{2,1,0:T(8,128)(2,1)} %pad_maximum_fusion.2), calls=%async_computation.1 | async-start | bytes 4718592 | tf_op jit(solution)/shard_map/all_to_all | solution.py:107

commit v7 on v3

--- a/solution.py
+++ b/solution.py
@@ -16,7 +16,7 @@
     return lax.ppermute(block, "tsink", [(t, t ^ 1) for t in range(n_t)])
 
 
-def source_pieces(own_elemental, src_times):
+def source_pieces(own_elemental, src_times, ready):
     n_t = lax.axis_size("tsink")
     order = own_elemental.shape[0]
     rows = order // n_t
@@ -24,6 +24,7 @@
     quarter = half // 2
     pieces = own_elemental.reshape(n_t, rows, order)
     received = lax.all_to_all(pieces, "tsink", 0, 0)
+    received, ready = lax.optimization_barrier((received, ready))
     own = received[src_times]
     t = lax.axis_index("tsink")
     step = 2
@@ -44,7 +45,7 @@
         axis=1,
     )
     partner_far_b = swapped(far[:, half:], n_t)
-    return [
+    return ready, [
         (t, own),
         (t ^ 1, partner),
         ((t - step) % n_t, from_left),
@@ -60,17 +61,28 @@
     propagators = perambulators[0]
     own_elemental = elementals[0, 0]
     block_order = propagators.shape[1]
-    pieces = source_pieces(own_elemental, src_times)
-    rows = pieces[0][1].shape[1]
-    def stacked(group):
-        columns = jnp.concatenate(
+    n_t = lax.axis_size("tsink")
+    rows = block_order // n_t
+    t = lax.axis_index("tsink")
+    step = 2
+    origins = [
+        t, t ^ 1, (t - step) % n_t, (t + step) % n_t,
+        (t + 2 * step) % n_t, (t - step) % n_t ^ 1, (t + step) % n_t ^ 1, (t + 2 * step) % n_t ^ 1,
+    ]
+
+    def permuted(group):
+        return jnp.concatenate(
             [
                 lax.dynamic_slice_in_dim(propagators[source], origin * rows, rows, 1)
-                for origin, _ in group
+                for origin in group
                 for source in range(NSRC)
             ],
             axis=1,
         )
+
+    ready = (permuted(origins[:4]), permuted(origins[4:]))
+    ready, pieces = source_pieces(own_elemental, src_times, ready)
+    def stacked(group, columns):
         blocks = jnp.stack(
             [
                 jnp.einsum(
@@ -83,7 +95,7 @@
             columns, blocks.reshape(-1, block_order), preferred_element_type=jnp.float32
         )
 
-    summed = stacked(pieces[:4]) + stacked(pieces[4:])
+    summed = stacked(pieces[:4], ready[0]) + stacked(pieces[4:], ready[1])
     meson = summed.astype(jnp.bfloat16)
 
     n_m = lax.axis_size("mom")

time: 182 us -> 181 us (level)
    dot_general x2, matrix products: 13.4 us -> 15.3 us  [stacked(): jnp.dot(columns, blocks.reshape(-1, block_order), preferred_element_type=...]
    unnamed x42 -> x44, local copies, waits for them, and re-layouts: 20.8 us -> 21.5 us
  transfers between devices with their start and end apart: 11 -> 11, of which waited for: 6 -> 7; matrix products, arithmetic and copies ran while one was open for 32% -> 33% of each run, Pallas kernels for 0% -> 0%
where the time goes in v7:
time: 181 us
  waiting for transfers between devices  56.3 us (31%)
  matrix products  43 us (24%)
  local copies, waits for them, and re-layouts  37.5 us (21%)
  starting transfers between devices  25.3 us (14%)
  blocking collectives  13.3 us (7%)
  other arithmetic  4.52 us (2%)
    all_to_all x1, waiting for transfers between devices, body(): received = lax.all_to_all(slices, 'mom', 0, 0)  31.1 us
    dot_general x8, matrix products, stacked(): jnp.einsum('sik,sjk->sij', piece, propagators, preferred_element_type=jnp...  27 us
    unnamed x44, local copies, waits for them, and re-layouts  21.5 us
    ppermute x6, waiting for transfers between devices, shifted(): return lax.ppermute(block, 'tsink', pairs)  19.6 us
    dot_general x2, matrix products, stacked(): jnp.dot(columns, blocks.reshape(-1, block_order), preferred_element_type=...  15.3 us
    all_to_all x1, blocking collectives, body(): spread = lax.all_to_all(per_diagram.reshape(n_m, -1), 'mom', 0, 0)  13.3 us
    all_to_all x1, starting transfers between devices, body(): received = lax.all_to_all(slices, 'mom', 0, 0)  11.5 us
    ppermute x6, starting transfers between devices, shifted(): return lax.ppermute(block, 'tsink', pairs)  7.35 us
  transfers between devices with their start and end apart: 11, of which 7 were waited for; matrix products, arithmetic and copies ran while one was open for 33% of the time, Pallas kernels for 0%

profile of v7, /device:TPU:1, one launch (start us, length us, event | category | flops | bytes accessed | tf_op | source)
XLA Modules:
  0.0 181.0 jit_solution(16974695213079897144)
XLA Ops:
  0.6 6.2 %all-to-all-start = ((bf16[8,128,1024]{2,1,0:T(8,128)(2,1)}), bf16[8,128,1024]{2,1,0:T(8,128)(2,1)}, u32[]{:S(2)}, u32[]{:S(2)}) async-start(bf16[8,128,1024]{2,1,0:T(8,128)(2,1)} %bitcast.191), calls=%async_computation | async-start | bytes 4194304 | tf_op jit(solution)/shard_map/all_to_all | solution.py:26
  6.8 5.8 %fusion.97 = (bf16[1,1,1024,1024]{3,2,1,0:T(8,128)(2,1)S(1)}, bf16[1,1,1024,1024]{3,2,1,0:T(8,128)(2,1)}, bf16[1,1,1024,1024]{3,2,1,0:T(8,128)(2,1)}, bf16[1,1,1024,1024]{3,2,1,0:T(8,128)(2,1)}) fusion(bf16[1,4,1024,1024]{3,2,1,0:T(8,128)(2,1)} %param.9), kind=kLoop, calls=%fused_computation.126 | loop fusion | bytes 16777216 | tf_op jit(solution)/shard_map/slice | solution.py:76
  12.7 2.1 %bitcast_dynamic-update-slice_fusion.15 = (bf16[1024,2048]{1,0:T(8,128)(2,1)}, bf16[1024,2048]{1,0:T(8,128)(2,1)}) fusion(bf16[1,1,1024,1024]{3,2,1,0:T(8,128)(2,1)} %get-tuple-element.11, s32[]{:T(128)S(6)} %select_n.114, s32[]{:T(128)S(6)} %select_n.107), kind=kLoop, calls=%fused_computation.88 | loop fusion | bytes 1048584
  14.8 2.0 %bitcast_dynamic-update-slice_fusion.14 = (bf16[1024,2048]{1,0:T(8,128)(2,1)}, bf16[1024,2048]{1,0:T(8,128)(2,1)}) fusion(bf16[1024,2048]{1,0:T(8,128)(2,1)} %get-tuple-element.44, bf16[1,1,1024,1024]{3,2,1,0:T(8,128)(2,1)} %get-tuple-element.10, s32[]{:T(128)S(6)} %select_n.114, bf16[1024,2048]{1,0:T(8,128)(2,1)} %get-tuple-element.45, s32[]{:T(128)S(6)} %select_n.107), kind=kLoop, calls=%fused_computation.87 | loop fusion | bytes 1048584
  16.8 1.9 %bitcast_dynamic-update-slice_fusion.13 = (bf16[1024,2048]{1,0:T(8,128)(2,1)}, bf16[1024,2048]{1,0:T(8,128)(2,1)}) fusion(bf16[1024,2048]{1,0:T(8,128)(2,1)} %get-tuple-element.42, bf16[1,1,1024,1024]{3,2,1,0:T(8,128)(2,1)} %get-tuple-element.9, s32[]{:T(128)S(6)} %select_n.114, bf16[1024,2048]{1,0:T(8,128)(2,1)} %get-tuple-element.43, s32[]{:T(128)S(6)} %select_n.107), kind=kLoop, calls=%fused_computation.86 | loop fusion | bytes 1048584
  18.8 1.0 bitcast_dynamic-update-slice_fusion.12
  19.8 1.9 %bitcast_dynamic-update-slice_fusion.11 = (bf16[1024,2048]{1,0:T(8,128)(2,1)}, bf16[1024,2048]{1,0:T(8,128)(2,1)}) fusion(bf16[1024,2048]{1,0:T(8,128)(2,1)} %get-tuple-element.38, bf16[1,1,1024,1024]{3,2,1,0:T(8,128)(2,1)} %get-tuple-element.11, s32[]{:T(128)S(6)} %select_n.115, bf16[1024,2048]{1,0:T(8,128)(2,1)} %get-tuple-element.39, s32[]{:T(128)S(6)} %select_n.108), kind=kLoop, calls=%fused_computation.84 | loop fusion | bytes 1048584
  21.7 1.0 bitcast_dynamic-update-slice_fusion.10
  22.8 1.0 bitcast_dynamic-update-slice_fusion.9
  23.7 1.0 bitcast_dynamic-update-slice_fusion.8
  24.7 1.0 bitcast_dynamic-update-slice_fusion.7
  25.7 1.0 bitcast_dynamic-update-slice_fusion.6
  26.7 1.0 bitcast_dynamic-update-slice_fusion.5
  27.8 1.0 bitcast_dynamic-update-slice_fusion.4
  28.7 1.0 bitcast_dynamic-update-slice_fusion.3
  29.7 1.0 bitcast_dynamic-update-slice_fusion.2
  30.7 1.0 bitcast_dynamic-update-slice_fusion.1
  31.7 1.0 bitcast_dynamic-update-slice_fusion
  32.7 4.9 %all-to-all-done = bf16[8,128,1024]{2,1,0:T(8,128)(2,1)} async-done(((bf16[8,128,1024]{2,1,0:T(8,128)(2,1)}), bf16[8,128,1024]{2,1,0:T(8,128)(2,1)}, u32[]{:S(2)}, u32[]{:S(2)}) %all-to-all-start) | async-done | bytes 2097184 | tf_op jit(solution)/shard_map/all_to_all | solution.py:26
  37.6 2.2 %gather_fusion = bf16[4,128,1024]{2,1,0:T(8,128)(2,1)S(1)} fusion(bf16[8,128,1024]{2,1,0:T(8,128)(2,1)} %all-to-all-done, s32[1024]{0:T(1024)S(1)} %pad_clamp_fusion.2), kind=kCustom, calls=%fused_computation | custom fusion | bytes 2097168 | tf_op jit(solution)/shard_map/gather | solution.py:28
  40.0 1.5 collective-permute-start.1
  41.7 6.4 %fusion.61 = bf16[1,4,128,1024]{3,2,1,0:T(8,128)(2,1)S(1)} fusion(bf16[4,128,1024]{2,1,0:T(8,128)(2,1)S(1)} %gather_fusion, bf16[1,4,1024,1024]{3,2,1,0:T(8,128)(2,1)} %param.9), kind=kOutput, calls=%fused_computation.40 | convolution fusion | flops 1074266112 | bytes 10485760 | tf_op jit(solution)/shard_map/sik,sjk->sij/dot_general | solution.py:88
  48.2 14.8 %collective-permute-done.2 = bf16[4,128,1024]{2,1,0:T(8,128)(2,1)S(1)} collective-permute-done((bf16[4,128,1024]{2,1,0:T(8,128)(2,1)S(1)}, bf16[4,128,1024]{2,1,0:T(8,128)(2,1)S(1)}, u32[]{:S(2)}, u32[]{:S(2)}) %collective-permute-start.2) | collective-permute-done | bytes 1048608 | tf_op jit(solution)/shard_map/ppermute | solution.py:12
  63.0 1.4 collective-permute-done.1
  65.0 2.7 %collective-permute-start.4 = (bf16[2,4,64,1024]{3,2,1,0:T(8,128)(2,1)S(1)}, bf16[2,4,64,1024]{3,2,1,0:T(8,128)(2,1)S(1)}, u32[]{:S(2)}, u32[]{:S(2)}) collective-permute-start(bf16[2,4,64,1024]{3,2,1,0:T(8,128)(2,1)S(1)} %get-tuple-element.55), channel_id=1, source_target_pairs={{0,96},{16,112},{32,0},{48,16},{64,32},{80,48},{96,64},{112,80},{1... | collective-permute-start | bytes 3145736 | tf_op jit(solution)/shard_map/ppermute | solution.py:12
  67.6 3.0 %fusion.52 = bf16[1,4,128,1024]{3,2,1,0:T(8,128)(2,1)S(1)} fusion(bf16[4,128,1024]{2,1,0:T(8,128)(2,1)S(1)} %collective-permute-done.2, bf16[1,4,1024,1024]{3,2,1,0:T(8,128)(2,1)S(1)} %bitcast.181), kind=kOutput, calls=%fused_computation.37 | convolution fusion | flops 1074266112 | bytes 10485760 | tf_op jit(solution)/shard_map/sik,sjk->sij/dot_general | solution.py:88
  70.6 3.0 %fusion.55 = bf16[1,4,128,1024]{3,2,1,0:T(8,128)(2,1)S(1)} fusion(bf16[4,128,1024]{2,1,0:T(8,128)(2,1)S(1)} %collective-permute-done.1, bf16[1,4,1024,1024]{3,2,1,0:T(8,128)(2,1)S(1)} %bitcast.181), kind=kOutput, calls=%fused_computation.38 | convolution fusion | flops 1074266112 | bytes 10485760 | tf_op jit(solution)/shard_map/sik,sjk->sij/dot_general | solution.py:88
  73.6 2.9 %fusion.58 = bf16[1,4,128,1024]{3,2,1,0:T(8,128)(2,1)S(1)} fusion(bf16[4,128,1024]{2,1,0:T(8,128)(2,1)S(1)} %collective-permute-done, bf16[1,4,1024,1024]{3,2,1,0:T(8,128)(2,1)S(1)} %bitcast.181), kind=kOutput, calls=%fused_computation.39 | convolution fusion | flops 1074266112 | bytes 10485760 | tf_op jit(solution)/shard_map/sik,sjk->sij/dot_general | solution.py:88
  77.1 8.3 %fusion.99 = f32[1024,1024]{1,0:T(8,128)} fusion(bf16[1024,2048]{1,0:T(8,128)(2,1)} %get-tuple-element.5, bf16[2048,1024]{1,0:T(8,128)(2,1)S(1)} %bitcast.190), kind=kOutput, calls=%fused_computation.128 | convolution fusion | flops 4294967296 | bytes 12582912 | tf_op jit(solution)/shard_map/dot_general | solution.py:94
  85.4 2.7 %collective-permute-done.3 = bf16[2,4,64,1024]{3,2,1,0:T(8,128)(2,1)S(1)} collective-permute-done((bf16[2,4,64,1024]{3,2,1,0:T(8,128)(2,1)S(1)}, bf16[2,4,64,1024]{3,2,1,0:T(8,128)(2,1)S(1)}, u32[]{:S(2)}, u32[]{:S(2)}) %collective-permute-start.3) | collective-permute-done | bytes 1048608 | tf_op jit(solution)/shard_map/ppermute | solution.py:12
  88.5 2.9 %fusion.49 = bf16[1,4,128,1024]{3,2,1,0:T(8,128)(2,1)S(1)} fusion(bf16[1,4,1024,1024]{3,2,1,0:T(8,128)(2,1)S(1)} %bitcast.181, bf16[4,64,1024]{2,1,0:T(8,128)(2,1)S(1)} %get-tuple-element.53, bf16[4,64,1024]{2,1,0:T(8,128)(2,1)S(1)} %get-tuple-element.46), kind=kOutput, calls=%fused_computation.36 | convolution fusion | flops 1076363264 | bytes 10485760 | tf_op jit(solution)/shard_map/sik,sjk->sij/dot_general | solution.py:88
  91.5 2.9 %fusion.46 = bf16[1,4,128,1024]{3,2,1,0:T(8,128)(2,1)S(1)} fusion(bf16[1,4,1024,1024]{3,2,1,0:T(8,128)(2,1)S(1)} %bitcast.181, bf16[4,64,1024]{2,1,0:T(8,128)(2,1)S(1)} %get-tuple-element.48, bf16[4,64,1024]{2,1,0:T(8,128)(2,1)S(1)} %get-tuple-element.47), kind=kOutput, calls=%fused_computation.35 | convolution fusion | flops 1076363264 | bytes 10485760 | tf_op jit(solution)/shard_map/sik,sjk->sij/dot_general | solution.py:88
  94.5 2.9 %collective-permute-start.7 = (bf16[4,32,1024]{2,1,0:T(8,128)(2,1)S(1)}, bf16[4,32,1024]{2,1,0:T(8,128)(2,1)S(1)}, u32[]{:S(2)}, u32[]{:S(2)}) collective-permute-start(bf16[4,32,1024]{2,1,0:T(8,128)(2,1)S(1)} %slice.133), channel_id=1, source_target_pairs={{0,96},{16,112},{32,0},{48,16},{64,32},{80,48},{96,64},{112,80},{1... | collective-permute-start | bytes 786440 | tf_op jit(solution)/shard_map/ppermute | solution.py:12
  97.5 2.9 %fusion.43 = bf16[1,4,128,1024]{3,2,1,0:T(8,128)(2,1)S(1)} fusion(bf16[1,4,1024,1024]{3,2,1,0:T(8,128)(2,1)S(1)} %bitcast.181, bf16[4,64,1024]{2,1,0:T(8,128)(2,1)S(1)} %get-tuple-element.49, bf16[4,64,1024]{2,1,0:T(8,128)(2,1)S(1)} %get-tuple-element.52), kind=kOutput, calls=%fused_computation.34 | convolution fusion | flops 1076363264 | bytes 10485760 | tf_op jit(solution)/shard_map/sik,sjk->sij/dot_general | solution.py:88
  100.9 0.8 collective-permute-done.8
  101.7 2.9 %fusion.40 = bf16[1,4,128,1024]{3,2,1,0:T(8,128)(2,1)S(1)} fusion(bf16[1,4,1024,1024]{3,2,1,0:T(8,128)(2,1)S(1)} %bitcast.181, bf16[4,64,1024]{2,1,0:T(8,128)(2,1)S(1)} %collective-permute-done.8, bf16[4,32,1024]{2,1,0:T(8,128)(2,1)S(1)} %collective-permute-done.7, bf16[4,32,1024]{2,1,0:T(8,128)(2,1)S(1)} %collective-permute-done.6), kind=kOutput, calls=%fused_computation.33 | convolution fusion | flops 1077411840 | bytes 10485760 | tf_op jit(solution)/shard_map/sik,sjk->sij/dot_general | solution.py:88
  105.2 1.6 copy-done.11
  106.8 7.0 %add_convert_fusion = bf16[1024,1024]{1,0:T(8,128)(2,1)S(1)} fusion(f32[1024,1024]{1,0:T(8,128)S(1)} %copy-done.11, bf16[1024,2048]{1,0:T(8,128)(2,1)} %get-tuple-element.7, bf16[2048,1024]{1,0:T(8,128)(2,1)S(1)} %bitcast.189), kind=kOutput, calls=%fused_computation.22 | convolution fusion | flops 4297064448 | bytes 14680064 | tf_op jit(solution)/shard_map/dot_general | solution.py:94
  115.1 1.8 %gather_fusion.1 = bf16[36,128,128]{2,1,0:T(8,128)(2,1)} fusion(bf16[64,128,128]{2,1,0:T(8,128)(2,1)S(1)} %bitcast.182, s32[1024]{0:T(1024)S(1)} %get-tuple-element.58), kind=kCustom, calls=%fused_computation.1 | custom fusion | bytes 2359440 | tf_op jit(solution)/shard_map/gather | solution.py:106
  116.9 0.8 gather_fusion.2
  117.7 1.4 copy.20
  119.4 0.9 fusion.64
  120.4 1.7 pad_maximum_fusion.2
  122.1 11.5 %all-to-all-start.1 = ((bf16[16,576,128]{2,1,0:T(8,128)(2,1)}), bf16[16,576,128]{2,1,0:T(8,128)(2,1)S(1)}, u32[]{:S(2)}, u32[]{:S(2)}) async-start(bf16[16,576,128]{2,1,0:T(8,128)(2,1)} %pad_maximum_fusion.2), calls=%async_computation.1 | async-start | bytes 4718592 | tf_op jit(solution)/shard_map/all_to_all | solution.py:119
  133.7 31.1 %all-to-all-done.1 = bf16[16,576,128]{2,1,0:T(8,128)(2,1)S(1)} async-done(((bf16[16,576,128]{2,1,0:T(8,128)(2,1)}), bf16[16,576,128]{2,1,0:T(8,128)(2,1)S(1)}, u32[]{:S(2)}, u32[]{:S(2)}) %all-to-all-start.1) | async-done | bytes 2359328 | tf_op jit(solution)/shard_map/all_to_all | solution.py:119
  164.9 0.7 fusion.68
  165.7 1.3 gather_fusion.3
  167.1 13.3 %all_to_all.19 = f32[16,1,8]{2,1,0:T(1,128)S(1)} all-to-all(f32[16,1,8]{2,1,0:T(1,128)S(1)} %bitcast.194), channel_id=1, replica_groups=mesh['tsink'=8,'mom'=16] {'mom'}, dimensions={0} | all-to-all | bytes 1024 | tf_op jit(solution)/shard_map/all_to_all | solution.py:127
  (66 shorter events, 5.6 us)
Async XLA Ops:
  0.6 36.9 %all-to-all-start = ((bf16[8,128,1024]{2,1,0:T(8,128)(2,1)}), bf16[8,128,1024]{2,1,0:T(8,128)(2,1)}, u32[]{:S(2)}, u32[]{:S(2)}) async-start(bf16[8,128,1024]{2,1,0:T(8,128)(2,1)} %bitcast.191), calls=%async_computation | async-start | bytes 4194304 | tf_op jit(solution)/shard_map/all_to_all | solution.py:26
  6.8 5.8 %copy-start.10 = (s32[4]{0:T(128)S(1)}, s32[4]{0:T(128)}, u32[]{:S(2)}) copy-start(s32[4]{0:T(128)} %param.11) | copy-start | bytes 52
  12.7 9.1 %copy-start.1 = (bf16[1,1,1024,1024]{3,2,1,0:T(8,128)(2,1)S(1)}, bf16[1,1,1024,1024]{3,2,1,0:T(8,128)(2,1)}, u32[]{:S(2)}) copy-start(bf16[1,1,1024,1024]{3,2,1,0:T(8,128)(2,1)} %get-tuple-element.10) | copy-start | bytes 6291460
  12.7 10.1 %copy-start = (bf16[1,1,1024,1024]{3,2,1,0:T(8,128)(2,1)S(1)}, bf16[1,1,1024,1024]{3,2,1,0:T(8,128)(2,1)}, u32[]{:S(2)}) copy-start(bf16[1,1,1024,1024]{3,2,1,0:T(8,128)(2,1)} %get-tuple-element.9) | copy-start | bytes 6291460
  12.7 12.0 %copy-start.2 = (bf16[1,1,1024,1024]{3,2,1,0:T(8,128)(2,1)S(1)}, bf16[1,1,1024,1024]{3,2,1,0:T(8,128)(2,1)}, u32[]{:S(2)}) copy-start(bf16[1,1,1024,1024]{3,2,1,0:T(8,128)(2,1)} %get-tuple-element.11) | copy-start | bytes 6291460
  26.7 13.1 %copy-start.8 = (pred[36]{0:T(512)(128)(4,1)S(1)}, pred[36]{0:T(512)(128)(4,1)}, u32[]{:S(2)}) copy-start(pred[36]{0:T(512)(128)(4,1)} %constant.109) | copy-start | bytes 112
  26.7 14.8 %copy-start.6 = (s32[36]{0:T(128)S(1)}, s32[36]{0:T(128)}, u32[]{:S(2)}) copy-start(s32[36]{0:T(128)} %constant.124) | copy-start | bytes 436
  26.7 14.8 %copy-start.7 = (s32[36]{0:T(128)S(1)}, s32[36]{0:T(128)}, u32[]{:S(2)}) copy-start(s32[36]{0:T(128)} %constant.125) | copy-start | bytes 436
  39.8 23.2 %collective-permute-start.2 = (bf16[4,128,1024]{2,1,0:T(8,128)(2,1)S(1)}, bf16[4,128,1024]{2,1,0:T(8,128)(2,1)S(1)}, u32[]{:S(2)}, u32[]{:S(2)}) collective-permute-start(bf16[4,128,1024]{2,1,0:T(8,128)(2,1)S(1)} %gather_fusion), channel_id=1, source_target_pairs={{0,96},{16,112},{32,0},{48,16},{64,32},{80,48},{96,64},{112,80},{1... | collective-permute-start | bytes 3145736 | tf_op jit(solution)/shard_map/ppermute | solution.py:12
  40.0 24.4 %collective-permute-start.1 = (bf16[4,128,1024]{2,1,0:T(8,128)(2,1)S(1)}, bf16[4,128,1024]{2,1,0:T(8,128)(2,1)S(1)}, u32[]{:S(2)}, u32[]{:S(2)}) collective-permute-start(bf16[4,128,1024]{2,1,0:T(8,128)(2,1)S(1)} %gather_fusion), channel_id=1, source_target_pairs={{0,32},{16,48},{32,64},{48,80},{64,96},{80,112},{96,0},{112,16},{1... | collective-permute-start | bytes 3145736 | tf_op jit(solution)/shard_map/ppermute | solution.py:12
  41.6 26.1 %slice-start = ((s8[8388608]{0:T(1024)(128)(4,1)}), s8[4194304]{0:T(1024)(128)(4,1)S(1)}, s32[]{:S(2)}) async-start(s8[8388608]{0:T(1024)(128)(4,1)} %bitcast.180), calls=%async_computation.3 | async-start | bytes 8388608
  41.6 26.0 %slice-start.1 = ((s8[8388608]{0:T(1024)(128)(4,1)}), s8[4194304]{0:T(1024)(128)(4,1)S(1)}, s32[]{:S(2)}) async-start(s8[8388608]{0:T(1024)(128)(4,1)} %bitcast.180), calls=%async_computation.4 | async-start | bytes 8388608
  41.6 23.0 %collective-permute-start = (bf16[4,128,1024]{2,1,0:T(8,128)(2,1)S(1)}, bf16[4,128,1024]{2,1,0:T(8,128)(2,1)S(1)}, u32[]{:S(2)}, u32[]{:S(2)}) collective-permute-start(bf16[4,128,1024]{2,1,0:T(8,128)(2,1)S(1)} %gather_fusion), channel_id=1, source_target_pairs={{0,16},{16,0},{32,48},{48,32},{64,80},{80,64},{96,112},{112,96},{1... | collective-permute-start | bytes 3145736 | tf_op jit(solution)/shard_map/ppermute | solution.py:16
  64.9 23.3 %collective-permute-start.3 = (bf16[2,4,64,1024]{3,2,1,0:T(8,128)(2,1)S(1)}, bf16[2,4,64,1024]{3,2,1,0:T(8,128)(2,1)S(1)}, u32[]{:S(2)}, u32[]{:S(2)}) collective-permute-start(bf16[2,4,64,1024]{3,2,1,0:T(8,128)(2,1)S(1)} %get-tuple-element.56), channel_id=1, source_target_pairs={{0,32},{16,48},{32,64},{48,80},{64,96},{80,112},{96,0},{112,16},{1... | collective-permute-start | bytes 3145736 | tf_op jit(solution)/shard_map/ppermute | solution.py:12
  65.0 23.3 %collective-permute-start.4 = (bf16[2,4,64,1024]{3,2,1,0:T(8,128)(2,1)S(1)}, bf16[2,4,64,1024]{3,2,1,0:T(8,128)(2,1)S(1)}, u32[]{:S(2)}, u32[]{:S(2)}) collective-permute-start(bf16[2,4,64,1024]{3,2,1,0:T(8,128)(2,1)S(1)} %get-tuple-element.55), channel_id=1, source_target_pairs={{0,96},{16,112},{32,0},{48,16},{64,32},{80,48},{96,64},{112,80},{1... | collective-permute-start | bytes 3145736 | tf_op jit(solution)/shard_map/ppermute | solution.py:12
  67.6 23.8 %collective-permute-start.5 = (bf16[2,4,64,1024]{3,2,1,0:T(8,128)(2,1)S(1)}, bf16[2,4,64,1024]{3,2,1,0:T(8,128)(2,1)S(1)}, u32[]{:S(2)}, u32[]{:S(2)}) collective-permute-start(bf16[2,4,64,1024]{3,2,1,0:T(8,128)(2,1)S(1)} %get-tuple-element.54), channel_id=1, source_target_pairs={{0,16},{16,0},{32,48},{48,32},{64,80},{80,64},{96,112},{112,96},{1... | collective-permute-start | bytes 3145736 | tf_op jit(solution)/shard_map/ppermute | solution.py:16
  88.4 13.3 %collective-permute-start.8 = (bf16[4,64,1024]{2,1,0:T(8,128)(2,1)S(1)}, bf16[4,64,1024]{2,1,0:T(8,128)(2,1)S(1)}, u32[]{:S(2)}, u32[]{:S(2)}) collective-permute-start(bf16[4,64,1024]{2,1,0:T(8,128)(2,1)S(1)} %get-tuple-element.53), channel_id=1, source_target_pairs={{0,16},{16,0},{32,48},{48,32},{64,80},{80,64},{96,112},{112,96},{1... | collective-permute-start | bytes 1572872 | tf_op jit(solution)/shard_map/ppermute | solution.py:16
  94.4 6.5 %collective-permute-start.6 = (bf16[4,32,1024]{2,1,0:T(8,128)(2,1)S(1)}, bf16[4,32,1024]{2,1,0:T(8,128)(2,1)S(1)}, u32[]{:S(2)}, u32[]{:S(2)}) collective-permute-start(bf16[4,32,1024]{2,1,0:T(8,128)(2,1)S(1)} %slice.132), channel_id=1, source_target_pairs={{0,32},{16,48},{32,64},{48,80},{64,96},{80,112},{96,0},{112,16},{1... | collective-permute-start | bytes 786440 | tf_op jit(solution)/shard_map/ppermute | solution.py:12
  94.5 6.4 %collective-permute-start.7 = (bf16[4,32,1024]{2,1,0:T(8,128)(2,1)S(1)}, bf16[4,32,1024]{2,1,0:T(8,128)(2,1)S(1)}, u32[]{:S(2)}, u32[]{:S(2)}) collective-permute-start(bf16[4,32,1024]{2,1,0:T(8,128)(2,1)S(1)} %slice.133), channel_id=1, source_target_pairs={{0,96},{16,112},{32,0},{48,16},{64,32},{80,48},{96,64},{112,80},{1... | collective-permute-start | bytes 786440 | tf_op jit(solution)/shard_map/ppermute | solution.py:12
  104.6 2.2 %copy-start.11 = (f32[1024,1024]{1,0:T(8,128)S(1)}, f32[1024,1024]{1,0:T(8,128)}, u32[]{:S(2)}) copy-start(f32[1024,1024]{1,0:T(8,128)} %fusion.99) | copy-start | bytes 12582916
  113.7 1.4 copy-start.5
  117.7 1.7 copy-start.3
  119.1 1.3 copy-start.4
  120.4 13.2 %copy-start.9 = (s32[128,2]{0,1:T(2,128)S(1)}, s32[128,2]{0,1:T(2,128)}, u32[]{:S(2)}) copy-start(s32[128,2]{0,1:T(2,128)} %param.12) | copy-start | bytes 3076
  122.1 42.7 %all-to-all-start.1 = ((bf16[16,576,128]{2,1,0:T(8,128)(2,1)}), bf16[16,576,128]{2,1,0:T(8,128)(2,1)S(1)}, u32[]{:S(2)}, u32[]{:S(2)}) async-start(bf16[16,576,128]{2,1,0:T(8,128)(2,1)} %pad_maximum_fusion.2), calls=%async_computation.1 | async-start | bytes 4718592 | tf_op jit(solution)/shard_map/all_to_all | solution.py:119

commit v8 on v3

--- a/solution.py
+++ b/solution.py
@@ -96,9 +96,9 @@
     row_index = lax.broadcasted_iota(jnp.int32, (width, width), 0)
     col_index = lax.broadcasted_iota(jnp.int32, (width, width), 1)
     triangle = jnp.where(row_index < col_index, 1.0, jnp.where(row_index == col_index, 0.5, 0.0))
-    on_diagonal = np.array([row == col for row, col in pairs])[:, None, None]
-    weight = jnp.where(on_diagonal, triangle[None], 1.0).astype(jnp.bfloat16)
-    upper = (upper * weight).reshape(-1, width)
+    on_diagonal = np.array([index for index, (row, col) in enumerate(pairs) if row == col])
+    upper = upper.at[on_diagonal].multiply(triangle.astype(jnp.bfloat16)[None])
+    upper = upper.reshape(-1, width)
     upper_t = upper_t.reshape(-1, width)
     share = upper.shape[0] // n_m
     slices = jnp.concatenate(

time: 182 us -> 182 us (level)
    unnamed x42 -> x38, local copies, waits for them, and re-layouts: 20.8 us -> 20.7 us
where the time goes in v8:
time: 182 us
  waiting for transfers between devices  58 us (32%)
  matrix products  41.3 us (23%)
  local copies, waits for them, and re-layouts  36.6 us (20%)
  starting transfers between devices  26.4 us (15%)
  blocking collectives  13.3 us (7%)
  other arithmetic  5.2 us (3%)
    all_to_all x1, waiting for transfers between devices, body(): received = lax.all_to_all(slices, 'mom', 0, 0)  31.1 us
    dot_general x8, matrix products, stacked(): jnp.einsum('sik,sjk->sij', piece, propagators, preferred_element_type=jnp...  27.2 us
    unnamed x38, local copies, waits for them, and re-layouts  20.7 us
    ppermute x6, waiting for transfers between devices, shifted(): return lax.ppermute(block, 'tsink', pairs)  19.4 us
    dot_general x2, matrix products, stacked(): jnp.dot(columns, blocks.reshape(-1, block_order), preferred_element_type=...  13.4 us
    all_to_all x1, blocking collectives, body(): spread = lax.all_to_all(per_diagram.reshape(n_m, -1), 'mom', 0, 0)  13.3 us
    all_to_all x1, starting transfers between devices, body(): received = lax.all_to_all(slices, 'mom', 0, 0)  12.7 us
    ppermute x6, starting transfers between devices, shifted(): return lax.ppermute(block, 'tsink', pairs)  7.06 us
  transfers between devices with their start and end apart: 11, of which 6 were waited for; matrix products, arithmetic and copies ran while one was open for 32% of the time, Pallas kernels for 0%

profile of v8, /device:TPU:1, one launch (start us, length us, event | category | flops | bytes accessed | tf_op | source)
XLA Modules:
  0.0 181.8 jit_solution(13245537358837266708)
XLA Ops:
  0.6 6.2 %all-to-all-start = ((bf16[8,128,1024]{2,1,0:T(8,128)(2,1)}), bf16[8,128,1024]{2,1,0:T(8,128)(2,1)}, u32[]{:S(2)}, u32[]{:S(2)}) async-start(bf16[8,128,1024]{2,1,0:T(8,128)(2,1)} %bitcast.189), calls=%async_computation | async-start | bytes 4194304 | tf_op jit(solution)/shard_map/all_to_all | solution.py:26
  6.8 5.7 %fusion.96 = (bf16[1,1,1024,1024]{3,2,1,0:T(8,128)(2,1)S(1)}, bf16[1,1,1024,1024]{3,2,1,0:T(8,128)(2,1)}, bf16[1,1,1024,1024]{3,2,1,0:T(8,128)(2,1)}, bf16[1,1,1024,1024]{3,2,1,0:T(8,128)(2,1)}) fusion(bf16[1,4,1024,1024]{3,2,1,0:T(8,128)(2,1)} %param.10), kind=kLoop, calls=%fused_computation.125 | loop fusion | bytes 16777216 | tf_op jit(solution)/shard_map/slice | solution.py:68
  12.7 2.1 %bitcast_dynamic-update-slice_fusion.15 = (bf16[1024,2048]{1,0:T(8,128)(2,1)}, bf16[1024,2048]{1,0:T(8,128)(2,1)}) fusion(bf16[1,1,1024,1024]{3,2,1,0:T(8,128)(2,1)} %get-tuple-element.5, s32[]{:T(128)S(6)} %select_n.113, s32[]{:T(128)S(6)} %select_n.105), kind=kLoop, calls=%fused_computation.87 | loop fusion | bytes 1048584
  14.7 2.0 %bitcast_dynamic-update-slice_fusion.14 = (bf16[1024,2048]{1,0:T(8,128)(2,1)}, bf16[1024,2048]{1,0:T(8,128)(2,1)}) fusion(bf16[1024,2048]{1,0:T(8,128)(2,1)} %get-tuple-element.38, bf16[1,1,1024,1024]{3,2,1,0:T(8,128)(2,1)} %get-tuple-element.4, s32[]{:T(128)S(6)} %select_n.113, bf16[1024,2048]{1,0:T(8,128)(2,1)} %get-tuple-element.39, s32[]{:T(128)S(6)} %select_n.105), kind=kLoop, calls=%fused_computation.86 | loop fusion | bytes 1048584
  16.8 2.0 %bitcast_dynamic-update-slice_fusion.13 = (bf16[1024,2048]{1,0:T(8,128)(2,1)}, bf16[1024,2048]{1,0:T(8,128)(2,1)}) fusion(bf16[1024,2048]{1,0:T(8,128)(2,1)} %get-tuple-element.36, bf16[1,1,1024,1024]{3,2,1,0:T(8,128)(2,1)} %get-tuple-element.3, s32[]{:T(128)S(6)} %select_n.113, bf16[1024,2048]{1,0:T(8,128)(2,1)} %get-tuple-element.37, s32[]{:T(128)S(6)} %select_n.105), kind=kLoop, calls=%fused_computation.85 | loop fusion | bytes 1048584
  18.7 1.0 bitcast_dynamic-update-slice_fusion.12
  19.8 1.9 %bitcast_dynamic-update-slice_fusion.11 = (bf16[1024,2048]{1,0:T(8,128)(2,1)}, bf16[1024,2048]{1,0:T(8,128)(2,1)}) fusion(bf16[1024,2048]{1,0:T(8,128)(2,1)} %get-tuple-element.32, bf16[1,1,1024,1024]{3,2,1,0:T(8,128)(2,1)} %get-tuple-element.5, s32[]{:T(128)S(6)} %select_n.114, bf16[1024,2048]{1,0:T(8,128)(2,1)} %get-tuple-element.33, s32[]{:T(128)S(6)} %select_n.106), kind=kLoop, calls=%fused_computation.83 | loop fusion | bytes 1048584
  21.7 1.0 bitcast_dynamic-update-slice_fusion.10
  22.7 1.0 bitcast_dynamic-update-slice_fusion.9
  23.7 1.0 bitcast_dynamic-update-slice_fusion.8
  24.7 1.0 bitcast_dynamic-update-slice_fusion.7
  25.7 1.0 bitcast_dynamic-update-slice_fusion.6
  26.7 1.0 bitcast_dynamic-update-slice_fusion.5
  27.7 1.0 bitcast_dynamic-update-slice_fusion.4
  28.7 1.0 bitcast_dynamic-update-slice_fusion.3
  29.7 1.0 bitcast_dynamic-update-slice_fusion.2
  30.7 6.9 %all-to-all-done = bf16[8,128,1024]{2,1,0:T(8,128)(2,1)} async-done(((bf16[8,128,1024]{2,1,0:T(8,128)(2,1)}), bf16[8,128,1024]{2,1,0:T(8,128)(2,1)}, u32[]{:S(2)}, u32[]{:S(2)}) %all-to-all-start) | async-done | bytes 2097184 | tf_op jit(solution)/shard_map/all_to_all | solution.py:26
  37.6 2.2 %gather_fusion = bf16[4,128,1024]{2,1,0:T(8,128)(2,1)S(1)} fusion(bf16[8,128,1024]{2,1,0:T(8,128)(2,1)} %all-to-all-done, s32[1024]{0:T(1024)S(1)} %pad_clamp_fusion.2), kind=kCustom, calls=%fused_computation | custom fusion | bytes 2097168 | tf_op jit(solution)/shard_map/gather | solution.py:27
  39.9 1.9 %bitcast_dynamic-update-slice_fusion.1 = (bf16[1024,2048]{1,0:T(8,128)(2,1)}, bf16[1024,2048]{1,0:T(8,128)(2,1)}) fusion(bf16[1024,2048]{1,0:T(8,128)(2,1)} %get-tuple-element.12, bf16[1,1,1024,1024]{3,2,1,0:T(8,128)(2,1)} %get-tuple-element.3, s32[]{:T(128)S(6)} %select_n.116, bf16[1024,2048]{1,0:T(8,128)(2,1)} %get-tuple-element.13, s32[]{:T(128)S(6)} %select_n.110), kind=kLoop, calls=%fused_computation.73 | loop fusion | bytes 1048584
  41.8 1.4 collective-permute-start.1
  43.3 1.0 bitcast_dynamic-update-slice_fusion
  44.3 6.7 %fusion.61 = bf16[1,4,128,1024]{3,2,1,0:T(8,128)(2,1)S(1)} fusion(bf16[4,128,1024]{2,1,0:T(8,128)(2,1)S(1)} %gather_fusion, bf16[1,4,1024,1024]{3,2,1,0:T(8,128)(2,1)} %param.10), kind=kOutput, calls=%fused_computation.40 | convolution fusion | flops 1074266112 | bytes 10485760 | tf_op jit(solution)/shard_map/sik,sjk->sij/dot_general | solution.py:76
  51.0 12.0 %collective-permute-done.2 = bf16[4,128,1024]{2,1,0:T(8,128)(2,1)S(1)} collective-permute-done((bf16[4,128,1024]{2,1,0:T(8,128)(2,1)S(1)}, bf16[4,128,1024]{2,1,0:T(8,128)(2,1)S(1)}, u32[]{:S(2)}, u32[]{:S(2)}) %collective-permute-start.2) | collective-permute-done | bytes 1048608 | tf_op jit(solution)/shard_map/ppermute | solution.py:12
  63.0 3.1 %collective-permute-done.1 = bf16[4,128,1024]{2,1,0:T(8,128)(2,1)S(1)} collective-permute-done((bf16[4,128,1024]{2,1,0:T(8,128)(2,1)S(1)}, bf16[4,128,1024]{2,1,0:T(8,128)(2,1)S(1)}, u32[]{:S(2)}, u32[]{:S(2)}) %collective-permute-start.1) | collective-permute-done | bytes 1048608 | tf_op jit(solution)/shard_map/ppermute | solution.py:12
  66.3 0.6 collective-permute-done
  67.5 2.4 %collective-permute-start.4 = (bf16[2,4,64,1024]{3,2,1,0:T(8,128)(2,1)S(1)}, bf16[2,4,64,1024]{3,2,1,0:T(8,128)(2,1)S(1)}, u32[]{:S(2)}, u32[]{:S(2)}) collective-permute-start(bf16[2,4,64,1024]{3,2,1,0:T(8,128)(2,1)S(1)} %get-tuple-element.49), channel_id=1, source_target_pairs={{0,96},{16,112},{32,0},{48,16},{64,32},{80,48},{96,64},{112,80},{1... | collective-permute-start | bytes 3145736 | tf_op jit(solution)/shard_map/ppermute | solution.py:12
  70.1 2.9 %fusion.52 = bf16[1,4,128,1024]{3,2,1,0:T(8,128)(2,1)S(1)} fusion(bf16[4,128,1024]{2,1,0:T(8,128)(2,1)S(1)} %collective-permute-done.2, bf16[1,4,1024,1024]{3,2,1,0:T(8,128)(2,1)S(1)} %bitcast.180), kind=kOutput, calls=%fused_computation.37 | convolution fusion | flops 1074266112 | bytes 10485760 | tf_op jit(solution)/shard_map/sik,sjk->sij/dot_general | solution.py:76
  73.0 3.0 %fusion.55 = bf16[1,4,128,1024]{3,2,1,0:T(8,128)(2,1)S(1)} fusion(bf16[4,128,1024]{2,1,0:T(8,128)(2,1)S(1)} %collective-permute-done.1, bf16[1,4,1024,1024]{3,2,1,0:T(8,128)(2,1)S(1)} %bitcast.180), kind=kOutput, calls=%fused_computation.38 | convolution fusion | flops 1074266112 | bytes 10485760 | tf_op jit(solution)/shard_map/sik,sjk->sij/dot_general | solution.py:76
  76.0 2.9 %fusion.58 = bf16[1,4,128,1024]{3,2,1,0:T(8,128)(2,1)S(1)} fusion(bf16[4,128,1024]{2,1,0:T(8,128)(2,1)S(1)} %collective-permute-done, bf16[1,4,1024,1024]{3,2,1,0:T(8,128)(2,1)S(1)} %bitcast.180), kind=kOutput, calls=%fused_computation.39 | convolution fusion | flops 1074266112 | bytes 10485760 | tf_op jit(solution)/shard_map/sik,sjk->sij/dot_general | solution.py:76
  79.5 6.4 %fusion.98 = f32[1024,1024]{1,0:T(8,128)S(1)} fusion(bf16[1024,2048]{1,0:T(8,128)(2,1)} %get-tuple-element.9, bf16[2048,1024]{1,0:T(8,128)(2,1)S(1)} %bitcast.188), kind=kOutput, calls=%fused_computation.127 | convolution fusion | flops 4294967296 | bytes 12582912 | tf_op jit(solution)/shard_map/dot_general | solution.py:82
  85.9 4.3 %collective-permute-done.3 = bf16[2,4,64,1024]{3,2,1,0:T(8,128)(2,1)S(1)} collective-permute-done((bf16[2,4,64,1024]{3,2,1,0:T(8,128)(2,1)S(1)}, bf16[2,4,64,1024]{3,2,1,0:T(8,128)(2,1)S(1)}, u32[]{:S(2)}, u32[]{:S(2)}) %collective-permute-start.3) | collective-permute-done | bytes 1048608 | tf_op jit(solution)/shard_map/ppermute | solution.py:12
  90.5 2.7 %collective-permute-start.7 = (bf16[4,32,1024]{2,1,0:T(8,128)(2,1)S(1)}, bf16[4,32,1024]{2,1,0:T(8,128)(2,1)S(1)}, u32[]{:S(2)}, u32[]{:S(2)}) collective-permute-start(bf16[4,32,1024]{2,1,0:T(8,128)(2,1)S(1)} %slice.133), channel_id=1, source_target_pairs={{0,96},{16,112},{32,0},{48,16},{64,32},{80,48},{96,64},{112,80},{1... | collective-permute-start | bytes 786440 | tf_op jit(solution)/shard_map/ppermute | solution.py:12
  93.6 2.9 %fusion.43 = bf16[1,4,128,1024]{3,2,1,0:T(8,128)(2,1)S(1)} fusion(bf16[1,4,1024,1024]{3,2,1,0:T(8,128)(2,1)S(1)} %bitcast.180, bf16[4,64,1024]{2,1,0:T(8,128)(2,1)S(1)} %get-tuple-element.43, bf16[4,64,1024]{2,1,0:T(8,128)(2,1)S(1)} %get-tuple-element.46), kind=kOutput, calls=%fused_computation.34 | convolution fusion | flops 1076363264 | bytes 10485760 | tf_op jit(solution)/shard_map/sik,sjk->sij/dot_general | solution.py:76
  96.5 2.9 %fusion.46 = bf16[1,4,128,1024]{3,2,1,0:T(8,128)(2,1)S(1)} fusion(bf16[1,4,1024,1024]{3,2,1,0:T(8,128)(2,1)S(1)} %bitcast.180, bf16[4,64,1024]{2,1,0:T(8,128)(2,1)S(1)} %get-tuple-element.42, bf16[4,64,1024]{2,1,0:T(8,128)(2,1)S(1)} %get-tuple-element.41), kind=kOutput, calls=%fused_computation.35 | convolution fusion | flops 1076363264 | bytes 10485760 | tf_op jit(solution)/shard_map/sik,sjk->sij/dot_general | solution.py:76
  99.4 2.9 %fusion.49 = bf16[1,4,128,1024]{3,2,1,0:T(8,128)(2,1)S(1)} fusion(bf16[1,4,1024,1024]{3,2,1,0:T(8,128)(2,1)S(1)} %bitcast.180, bf16[4,64,1024]{2,1,0:T(8,128)(2,1)S(1)} %get-tuple-element.47, bf16[4,64,1024]{2,1,0:T(8,128)(2,1)S(1)} %get-tuple-element.40), kind=kOutput, calls=%fused_computation.36 | convolution fusion | flops 1076363264 | bytes 10485760 | tf_op jit(solution)/shard_map/sik,sjk->sij/dot_general | solution.py:76
  102.4 2.9 %fusion.40 = bf16[1,4,128,1024]{3,2,1,0:T(8,128)(2,1)S(1)} fusion(bf16[1,4,1024,1024]{3,2,1,0:T(8,128)(2,1)S(1)} %bitcast.180, bf16[4,64,1024]{2,1,0:T(8,128)(2,1)S(1)} %collective-permute-done.8, bf16[4,32,1024]{2,1,0:T(8,128)(2,1)S(1)} %collective-permute-done.7, bf16[4,32,1024]{2,1,0:T(8,128)(2,1)S(1)} %collective-permute-done.6), kind=kOutput, calls=%fused_computation.33 | convolution fusion | flops 1077411840 | bytes 10485760 | tf_op jit(solution)/shard_map/sik,sjk->sij/dot_general | solution.py:76
  105.3 0.8 pad_maximum_fusion.1
  106.1 7.0 %add_convert_fusion = bf16[1024,1024]{1,0:T(8,128)(2,1)S(1)} fusion(f32[1024,1024]{1,0:T(8,128)S(1)} %fusion.98, bf16[1024,2048]{1,0:T(8,128)(2,1)} %get-tuple-element.8, bf16[2048,1024]{1,0:T(8,128)(2,1)S(1)} %bitcast.187), kind=kOutput, calls=%fused_computation.23 | convolution fusion | flops 4297064448 | bytes 14680064 | tf_op jit(solution)/shard_map/dot_general | solution.py:82
  114.5 0.8 gather_fusion.1
  115.3 1.8 %gather_fusion.2 = bf16[36,128,128]{2,1,0:T(8,128)(2,1)} fusion(bf16[64,128,128]{2,1,0:T(8,128)(2,1)S(1)} %bitcast.182, s32[1024]{0:T(1024)S(1)} %get-tuple-element.51), kind=kCustom, calls=%fused_computation.2 | custom fusion | bytes 2359440 | tf_op jit(solution)/shard_map/gather | solution.py:95
  117.1 1.7 copy.19
  118.8 1.3 scatter_fusion
  120.1 1.7 pad_maximum_fusion.2
  121.8 12.7 %all-to-all-start.1 = ((bf16[16,576,128]{2,1,0:T(8,128)(2,1)}), bf16[16,576,128]{2,1,0:T(8,128)(2,1)S(1)}, u32[]{:S(2)}, u32[]{:S(2)}) async-start(bf16[16,576,128]{2,1,0:T(8,128)(2,1)} %pad_maximum_fusion.2), calls=%async_computation.1 | async-start | bytes 4718592 | tf_op jit(solution)/shard_map/all_to_all | solution.py:107
  134.5 31.1 %all-to-all-done.1 = bf16[16,576,128]{2,1,0:T(8,128)(2,1)S(1)} async-done(((bf16[16,576,128]{2,1,0:T(8,128)(2,1)}), bf16[16,576,128]{2,1,0:T(8,128)(2,1)S(1)}, u32[]{:S(2)}, u32[]{:S(2)}) %all-to-all-start.1) | async-done | bytes 2359328 | tf_op jit(solution)/shard_map/all_to_all | solution.py:107
  165.8 0.7 fusion.67
  166.6 1.3 gather_fusion.3
  167.9 13.3 %all_to_all.19 = f32[16,1,8]{2,1,0:T(1,128)S(1)} all-to-all(f32[16,1,8]{2,1,0:T(1,128)S(1)} %bitcast.192), channel_id=1, replica_groups=mesh['tsink'=8,'mom'=16] {'mom'}, dimensions={0} | all-to-all | bytes 1024 | tf_op jit(solution)/shard_map/all_to_all | solution.py:115
  (58 shorter events, 4.5 us)
Async XLA Ops:
  0.6 36.9 %all-to-all-start = ((bf16[8,128,1024]{2,1,0:T(8,128)(2,1)}), bf16[8,128,1024]{2,1,0:T(8,128)(2,1)}, u32[]{:S(2)}, u32[]{:S(2)}) async-start(bf16[8,128,1024]{2,1,0:T(8,128)(2,1)} %bitcast.189), calls=%async_computation | async-start | bytes 4194304 | tf_op jit(solution)/shard_map/all_to_all | solution.py:26
  6.8 5.8 %copy-start.8 = (s32[4]{0:T(128)S(1)}, s32[4]{0:T(128)}, u32[]{:S(2)}) copy-start(s32[4]{0:T(128)} %param.12) | copy-start | bytes 52
  12.6 9.1 %copy-start.1 = (bf16[1,1,1024,1024]{3,2,1,0:T(8,128)(2,1)S(1)}, bf16[1,1,1024,1024]{3,2,1,0:T(8,128)(2,1)}, u32[]{:S(2)}) copy-start(bf16[1,1,1024,1024]{3,2,1,0:T(8,128)(2,1)} %get-tuple-element.4) | copy-start | bytes 6291460
  12.6 10.1 %copy-start = (bf16[1,1,1024,1024]{3,2,1,0:T(8,128)(2,1)S(1)}, bf16[1,1,1024,1024]{3,2,1,0:T(8,128)(2,1)}, u32[]{:S(2)}) copy-start(bf16[1,1,1024,1024]{3,2,1,0:T(8,128)(2,1)} %get-tuple-element.3) | copy-start | bytes 6291460
  12.7 12.0 %copy-start.2 = (bf16[1,1,1024,1024]{3,2,1,0:T(8,128)(2,1)S(1)}, bf16[1,1,1024,1024]{3,2,1,0:T(8,128)(2,1)}, u32[]{:S(2)}) copy-start(bf16[1,1,1024,1024]{3,2,1,0:T(8,128)(2,1)} %get-tuple-element.5) | copy-start | bytes 6291460
  25.7 17.5 %copy-start.4 = (s32[36]{0:T(128)S(1)}, s32[36]{0:T(128)}, u32[]{:S(2)}) copy-start(s32[36]{0:T(128)} %constant.128) | copy-start | bytes 436
  25.7 17.5 %copy-start.5 = (s32[36]{0:T(128)S(1)}, s32[36]{0:T(128)}, u32[]{:S(2)}) copy-start(s32[36]{0:T(128)} %constant.130) | copy-start | bytes 436
  39.8 23.2 %collective-permute-start.2 = (bf16[4,128,1024]{2,1,0:T(8,128)(2,1)S(1)}, bf16[4,128,1024]{2,1,0:T(8,128)(2,1)S(1)}, u32[]{:S(2)}, u32[]{:S(2)}) collective-permute-start(bf16[4,128,1024]{2,1,0:T(8,128)(2,1)S(1)} %gather_fusion), channel_id=1, source_target_pairs={{0,96},{16,112},{32,0},{48,16},{64,32},{80,48},{96,64},{112,80},{1... | collective-permute-start | bytes 3145736 | tf_op jit(solution)/shard_map/ppermute | solution.py:12
  41.8 24.4 %collective-permute-start.1 = (bf16[4,128,1024]{2,1,0:T(8,128)(2,1)S(1)}, bf16[4,128,1024]{2,1,0:T(8,128)(2,1)S(1)}, u32[]{:S(2)}, u32[]{:S(2)}) collective-permute-start(bf16[4,128,1024]{2,1,0:T(8,128)(2,1)S(1)} %gather_fusion), channel_id=1, source_target_pairs={{0,32},{16,48},{32,64},{48,80},{64,96},{80,112},{96,0},{112,16},{1... | collective-permute-start | bytes 3145736 | tf_op jit(solution)/shard_map/ppermute | solution.py:12
  43.3 26.8 %slice-start = ((s8[8388608]{0:T(1024)(128)(4,1)}), s8[4194304]{0:T(1024)(128)(4,1)S(1)}, s32[]{:S(2)}) async-start(s8[8388608]{0:T(1024)(128)(4,1)} %bitcast.179), calls=%async_computation.3 | async-start | bytes 8388608
  44.3 25.8 %slice-start.1 = ((s8[8388608]{0:T(1024)(128)(4,1)}), s8[4194304]{0:T(1024)(128)(4,1)S(1)}, s32[]{:S(2)}) async-start(s8[8388608]{0:T(1024)(128)(4,1)} %bitcast.179), calls=%async_computation.4 | async-start | bytes 8388608
  44.3 22.6 %collective-permute-start = (bf16[4,128,1024]{2,1,0:T(8,128)(2,1)S(1)}, bf16[4,128,1024]{2,1,0:T(8,128)(2,1)S(1)}, u32[]{:S(2)}, u32[]{:S(2)}) collective-permute-start(bf16[4,128,1024]{2,1,0:T(8,128)(2,1)S(1)} %gather_fusion), channel_id=1, source_target_pairs={{0,16},{16,0},{32,48},{48,32},{64,80},{80,64},{96,112},{112,96},{1... | collective-permute-start | bytes 3145736 | tf_op jit(solution)/shard_map/ppermute | solution.py:16
  67.2 23.0 %collective-permute-start.3 = (bf16[2,4,64,1024]{3,2,1,0:T(8,128)(2,1)S(1)}, bf16[2,4,64,1024]{3,2,1,0:T(8,128)(2,1)S(1)}, u32[]{:S(2)}, u32[]{:S(2)}) collective-permute-start(bf16[2,4,64,1024]{3,2,1,0:T(8,128)(2,1)S(1)} %get-tuple-element.50), channel_id=1, source_target_pairs={{0,32},{16,48},{32,64},{48,80},{64,96},{80,112},{96,0},{112,16},{1... | collective-permute-start | bytes 3145736 | tf_op jit(solution)/shard_map/ppermute | solution.py:12
  67.5 22.8 %collective-permute-start.4 = (bf16[2,4,64,1024]{3,2,1,0:T(8,128)(2,1)S(1)}, bf16[2,4,64,1024]{3,2,1,0:T(8,128)(2,1)S(1)}, u32[]{:S(2)}, u32[]{:S(2)}) collective-permute-start(bf16[2,4,64,1024]{3,2,1,0:T(8,128)(2,1)S(1)} %get-tuple-element.49), channel_id=1, source_target_pairs={{0,96},{16,112},{32,0},{48,16},{64,32},{80,48},{96,64},{112,80},{1... | collective-permute-start | bytes 3145736 | tf_op jit(solution)/shard_map/ppermute | solution.py:12
  69.9 23.6 %collective-permute-start.5 = (bf16[2,4,64,1024]{3,2,1,0:T(8,128)(2,1)S(1)}, bf16[2,4,64,1024]{3,2,1,0:T(8,128)(2,1)S(1)}, u32[]{:S(2)}, u32[]{:S(2)}) collective-permute-start(bf16[2,4,64,1024]{3,2,1,0:T(8,128)(2,1)S(1)} %get-tuple-element.48), channel_id=1, source_target_pairs={{0,16},{16,0},{32,48},{48,32},{64,80},{80,64},{96,112},{112,96},{1... | collective-permute-start | bytes 3145736 | tf_op jit(solution)/shard_map/ppermute | solution.py:16
  90.3 12.1 %collective-permute-start.6 = (bf16[4,32,1024]{2,1,0:T(8,128)(2,1)S(1)}, bf16[4,32,1024]{2,1,0:T(8,128)(2,1)S(1)}, u32[]{:S(2)}, u32[]{:S(2)}) collective-permute-start(bf16[4,32,1024]{2,1,0:T(8,128)(2,1)S(1)} %slice.132), channel_id=1, source_target_pairs={{0,32},{16,48},{32,64},{48,80},{64,96},{80,112},{96,0},{112,16},{1... | collective-permute-start | bytes 786440 | tf_op jit(solution)/shard_map/ppermute | solution.py:12
  90.5 11.9 %collective-permute-start.7 = (bf16[4,32,1024]{2,1,0:T(8,128)(2,1)S(1)}, bf16[4,32,1024]{2,1,0:T(8,128)(2,1)S(1)}, u32[]{:S(2)}, u32[]{:S(2)}) collective-permute-start(bf16[4,32,1024]{2,1,0:T(8,128)(2,1)S(1)} %slice.133), channel_id=1, source_target_pairs={{0,96},{16,112},{32,0},{48,16},{64,32},{80,48},{96,64},{112,80},{1... | collective-permute-start | bytes 786440 | tf_op jit(solution)/shard_map/ppermute | solution.py:12
  93.2 9.2 %collective-permute-start.8 = (bf16[4,64,1024]{2,1,0:T(8,128)(2,1)S(1)}, bf16[4,64,1024]{2,1,0:T(8,128)(2,1)S(1)}, u32[]{:S(2)}, u32[]{:S(2)}) collective-permute-start(bf16[4,64,1024]{2,1,0:T(8,128)(2,1)S(1)} %get-tuple-element.47), channel_id=1, source_target_pairs={{0,16},{16,0},{32,48},{48,32},{64,80},{80,64},{96,112},{112,96},{1... | collective-permute-start | bytes 1572872 | tf_op jit(solution)/shard_map/ppermute | solution.py:16
  113.1 1.4 copy-start.3
  114.5 4.4 %copy-start.6 = (s32[8]{0:T(128)S(1)}, s32[8]{0:T(128)}, u32[]{:S(2)}) copy-start(s32[8]{0:T(128)} %constant.129) | copy-start | bytes 100
  120.1 14.4 %copy-start.7 = (s32[128,2]{0,1:T(2,128)S(1)}, s32[128,2]{0,1:T(2,128)}, u32[]{:S(2)}) copy-start(s32[128,2]{0,1:T(2,128)} %param.13) | copy-start | bytes 3076
  121.8 43.8 %all-to-all-start.1 = ((bf16[16,576,128]{2,1,0:T(8,128)(2,1)}), bf16[16,576,128]{2,1,0:T(8,128)(2,1)S(1)}, u32[]{:S(2)}, u32[]{:S(2)}) async-start(bf16[16,576,128]{2,1,0:T(8,128)(2,1)} %pad_maximum_fusion.2), calls=%async_computation.1 | async-start | bytes 4718592 | tf_op jit(solution)/shard_map/all_to_all | solution.py:107

commit v9 on v3

--- a/solution.py
+++ b/solution.py
@@ -30,12 +30,12 @@
     partner = swapped(own, n_t)
     from_left = shifted(own, step, n_t)
     from_right = shifted(own, -step, n_t)
-    to_right = shifted(jnp.stack([from_left[:, :half], partner[:, :half]]), step, n_t)
-    to_left = shifted(jnp.stack([from_right[:, half:], partner[:, :half]]), -step, n_t)
-    far = jnp.concatenate([to_right[0], to_left[0]], axis=1)
+    far = jnp.concatenate(
+        [shifted(from_left[:, :half], step, n_t), shifted(from_right[:, half:], -step, n_t)], axis=1
+    )
     partner_b = swapped(jnp.stack([from_left[:, half:], from_right[:, half:]]), n_t)
-    partner_left_a = to_right[1]
-    partner_right_a = to_left[1]
+    partner_left_a = shifted(partner[:, :half], step, n_t)
+    partner_right_a = shifted(partner[:, :half], -step, n_t)
     partner_far_a = jnp.concatenate(
         [
             shifted(partner_left_a[:, :quarter], step, n_t),

time: 182 us -> 183 us (level)
  starting transfers between devices: 26.4 us -> 28.3 us
    ppermute x6 -> x8, waiting for transfers between devices: 19.4 us -> 2.43 us  [shifted(): return lax.ppermute(block, 'tsink', pairs)]
    ppermute x3, waiting for transfers between devices: 0.58 us -> 17.5 us  [swapped(): return lax.ppermute(block, 'tsink', [(t, t ^ 1) for t in range(n_t)])]
    ppermute x3, starting transfers between devices: 0.45 us -> 2.76 us  [swapped(): return lax.ppermute(block, 'tsink', [(t, t ^ 1) for t in range(n_t)])]
    ppermute x6 -> x8, starting transfers between devices: 7.06 us -> 7.38 us  [shifted(): return lax.ppermute(block, 'tsink', pairs)]
  transfers between devices with their start and end apart: 11 -> 13, of which waited for: 6 -> 6; matrix products, arithmetic and copies ran while one was open for 32% -> 30% of each run, Pallas kernels for 0% -> 0%
where the time goes in v9:
time: 183 us
  waiting for transfers between devices  57.7 us (32%)
  matrix products  41.3 us (23%)
  local copies, waits for them, and re-layouts  36.7 us (20%)
  starting transfers between devices  28.3 us (15%)
  blocking collectives  13.3 us (7%)
  other arithmetic  4.65 us (3%)
    all_to_all x1, waiting for transfers between devices, body(): received = lax.all_to_all(slices, 'mom', 0, 0)  31.1 us
    dot_general x8, matrix products, stacked(): jnp.einsum('sik,sjk->sij', piece, propagators, preferred_element_type=jnp...  27.2 us
    unnamed x42, local copies, waits for them, and re-layouts  20.8 us
    ppermute x3, waiting for transfers between devices, swapped(): return lax.ppermute(block, 'tsink', [(t, t ^ 1) for t in range(n_t)])  17.5 us
    dot_general x2, matrix products, stacked(): jnp.dot(columns, blocks.reshape(-1, block_order), preferred_element_type=...  13.4 us
    all_to_all x1, blocking collectives, body(): spread = lax.all_to_all(per_diagram.reshape(n_m, -1), 'mom', 0, 0)  13.3 us
    all_to_all x1, starting transfers between devices, body(): received = lax.all_to_all(slices, 'mom', 0, 0)  11.9 us
    ppermute x8, starting transfers between devices, shifted(): return lax.ppermute(block, 'tsink', pairs)  7.38 us
  transfers between devices with their start and end apart: 13, of which 6 were waited for; matrix products, arithmetic and copies ran while one was open for 30% of the time, Pallas kernels for 0%

profile of v9, /device:TPU:1, one launch (start us, length us, event | category | flops | bytes accessed | tf_op | source)
XLA Modules:
  0.0 183.0 jit_solution(8593718322587733337)
XLA Ops:
  0.6 6.2 %all-to-all-start = ((bf16[8,128,1024]{2,1,0:T(8,128)(2,1)}), bf16[8,128,1024]{2,1,0:T(8,128)(2,1)}, u32[]{:S(2)}, u32[]{:S(2)}) async-start(bf16[8,128,1024]{2,1,0:T(8,128)(2,1)} %bitcast.179), calls=%async_computation | async-start | bytes 4194304 | tf_op jit(solution)/shard_map/all_to_all | solution.py:26
  6.9 5.8 %fusion.97 = (bf16[1,1,1024,1024]{3,2,1,0:T(8,128)(2,1)S(1)}, bf16[1,1,1024,1024]{3,2,1,0:T(8,128)(2,1)}, bf16[1,1,1024,1024]{3,2,1,0:T(8,128)(2,1)}, bf16[1,1,1024,1024]{3,2,1,0:T(8,128)(2,1)}) fusion(bf16[1,4,1024,1024]{3,2,1,0:T(8,128)(2,1)} %param.9), kind=kLoop, calls=%fused_computation.118 | loop fusion | bytes 16777216 | tf_op jit(solution)/shard_map/slice | solution.py:68
  12.9 2.1 %bitcast_dynamic-update-slice_fusion.15 = (bf16[1024,2048]{1,0:T(8,128)(2,1)}, bf16[1024,2048]{1,0:T(8,128)(2,1)}) fusion(bf16[1,1,1024,1024]{3,2,1,0:T(8,128)(2,1)} %get-tuple-element.5, s32[]{:T(128)S(6)} %select_n.115, s32[]{:T(128)S(6)} %select_n.107), kind=kLoop, calls=%fused_computation.79 | loop fusion | bytes 1048584
  15.0 2.0 %bitcast_dynamic-update-slice_fusion.14 = (bf16[1024,2048]{1,0:T(8,128)(2,1)}, bf16[1024,2048]{1,0:T(8,128)(2,1)}) fusion(bf16[1024,2048]{1,0:T(8,128)(2,1)} %get-tuple-element.38, bf16[1,1,1024,1024]{3,2,1,0:T(8,128)(2,1)} %get-tuple-element.4, s32[]{:T(128)S(6)} %select_n.115, bf16[1024,2048]{1,0:T(8,128)(2,1)} %get-tuple-element.39, s32[]{:T(128)S(6)} %select_n.107), kind=kLoop, calls=%fused_computation.78 | loop fusion | bytes 1048584
  17.0 2.0 %bitcast_dynamic-update-slice_fusion.13 = (bf16[1024,2048]{1,0:T(8,128)(2,1)}, bf16[1024,2048]{1,0:T(8,128)(2,1)}) fusion(bf16[1024,2048]{1,0:T(8,128)(2,1)} %get-tuple-element.36, bf16[1,1,1024,1024]{3,2,1,0:T(8,128)(2,1)} %get-tuple-element.3, s32[]{:T(128)S(6)} %select_n.115, bf16[1024,2048]{1,0:T(8,128)(2,1)} %get-tuple-element.37, s32[]{:T(128)S(6)} %select_n.107), kind=kLoop, calls=%fused_computation.77 | loop fusion | bytes 1048584
  19.0 1.0 bitcast_dynamic-update-slice_fusion.12
  19.9 1.9 %bitcast_dynamic-update-slice_fusion.11 = (bf16[1024,2048]{1,0:T(8,128)(2,1)}, bf16[1024,2048]{1,0:T(8,128)(2,1)}) fusion(bf16[1024,2048]{1,0:T(8,128)(2,1)} %get-tuple-element.32, bf16[1,1,1024,1024]{3,2,1,0:T(8,128)(2,1)} %get-tuple-element.5, s32[]{:T(128)S(6)} %select_n.116, bf16[1024,2048]{1,0:T(8,128)(2,1)} %get-tuple-element.33, s32[]{:T(128)S(6)} %select_n.108), kind=kLoop, calls=%fused_computation.75 | loop fusion | bytes 1048584
  21.8 1.0 bitcast_dynamic-update-slice_fusion.10
  22.8 1.0 bitcast_dynamic-update-slice_fusion.9
  23.8 1.0 bitcast_dynamic-update-slice_fusion.8
  24.8 1.0 bitcast_dynamic-update-slice_fusion.7
  25.8 1.0 bitcast_dynamic-update-slice_fusion.6
  26.8 1.0 bitcast_dynamic-update-slice_fusion.5
  27.8 1.0 bitcast_dynamic-update-slice_fusion.4
  28.9 1.0 bitcast_dynamic-update-slice_fusion.3
  29.9 1.0 bitcast_dynamic-update-slice_fusion.2
  30.9 6.7 %all-to-all-done = bf16[8,128,1024]{2,1,0:T(8,128)(2,1)} async-done(((bf16[8,128,1024]{2,1,0:T(8,128)(2,1)}), bf16[8,128,1024]{2,1,0:T(8,128)(2,1)}, u32[]{:S(2)}, u32[]{:S(2)}) %all-to-all-start) | async-done | bytes 2097184 | tf_op jit(solution)/shard_map/all_to_all | solution.py:26
  37.6 2.2 %gather_fusion = bf16[4,128,1024]{2,1,0:T(8,128)(2,1)S(1)} fusion(bf16[8,128,1024]{2,1,0:T(8,128)(2,1)} %all-to-all-done, s32[1024]{0:T(1024)S(1)} %pad_clamp_fusion.2), kind=kCustom, calls=%fused_computation | custom fusion | bytes 2097168 | tf_op jit(solution)/shard_map/gather | solution.py:27
  40.0 1.9 %bitcast_dynamic-update-slice_fusion.1 = (bf16[1024,2048]{1,0:T(8,128)(2,1)}, bf16[1024,2048]{1,0:T(8,128)(2,1)}) fusion(bf16[1024,2048]{1,0:T(8,128)(2,1)} %get-tuple-element.12, bf16[1,1,1024,1024]{3,2,1,0:T(8,128)(2,1)} %get-tuple-element.3, s32[]{:T(128)S(6)} %select_n.118, bf16[1024,2048]{1,0:T(8,128)(2,1)} %get-tuple-element.13, s32[]{:T(128)S(6)} %select_n.112), kind=kLoop, calls=%fused_computation.65 | loop fusion | bytes 1048584
  41.9 1.4 collective-permute-start.1
  43.3 1.0 bitcast_dynamic-update-slice_fusion
  44.3 6.8 %fusion.61 = bf16[1,4,128,1024]{3,2,1,0:T(8,128)(2,1)S(1)} fusion(bf16[4,128,1024]{2,1,0:T(8,128)(2,1)S(1)} %gather_fusion, bf16[1,4,1024,1024]{3,2,1,0:T(8,128)(2,1)} %param.9), kind=kOutput, calls=%fused_computation.40 | convolution fusion | flops 1074266112 | bytes 10485760 | tf_op jit(solution)/shard_map/sik,sjk->sij/dot_general | solution.py:76
  51.0 12.1 %collective-permute-done = bf16[4,128,1024]{2,1,0:T(8,128)(2,1)S(1)} collective-permute-done((bf16[4,128,1024]{2,1,0:T(8,128)(2,1)S(1)}, bf16[4,128,1024]{2,1,0:T(8,128)(2,1)S(1)}, u32[]{:S(2)}, u32[]{:S(2)}) %collective-permute-start) | collective-permute-done | bytes 1048608 | tf_op jit(solution)/shard_map/ppermute | solution.py:16
  63.1 1.2 collective-permute-start.5
  64.3 1.6 collective-permute-start.7
  66.2 1.5 collective-permute-start.6
  68.0 2.9 %fusion.52 = bf16[1,4,128,1024]{3,2,1,0:T(8,128)(2,1)S(1)} fusion(bf16[4,128,1024]{2,1,0:T(8,128)(2,1)S(1)} %collective-permute-done.2, bf16[1,4,1024,1024]{3,2,1,0:T(8,128)(2,1)S(1)} %bitcast.169), kind=kOutput, calls=%fused_computation.37 | convolution fusion | flops 1074266112 | bytes 10485760 | tf_op jit(solution)/shard_map/sik,sjk->sij/dot_general | solution.py:76
  71.0 3.0 %fusion.55 = bf16[1,4,128,1024]{3,2,1,0:T(8,128)(2,1)S(1)} fusion(bf16[4,128,1024]{2,1,0:T(8,128)(2,1)S(1)} %collective-permute-done.1, bf16[1,4,1024,1024]{3,2,1,0:T(8,128)(2,1)S(1)} %bitcast.169), kind=kOutput, calls=%fused_computation.38 | convolution fusion | flops 1074266112 | bytes 10485760 | tf_op jit(solution)/shard_map/sik,sjk->sij/dot_general | solution.py:76
  74.0 2.9 %fusion.58 = bf16[1,4,128,1024]{3,2,1,0:T(8,128)(2,1)S(1)} fusion(bf16[4,128,1024]{2,1,0:T(8,128)(2,1)S(1)} %collective-permute-done, bf16[1,4,1024,1024]{3,2,1,0:T(8,128)(2,1)S(1)} %bitcast.169), kind=kOutput, calls=%fused_computation.39 | convolution fusion | flops 1074266112 | bytes 10485760 | tf_op jit(solution)/shard_map/sik,sjk->sij/dot_general | solution.py:76
  77.5 6.4 %fusion.100 = f32[1024,1024]{1,0:T(8,128)S(1)} fusion(bf16[1024,2048]{1,0:T(8,128)(2,1)} %get-tuple-element.9, bf16[2048,1024]{1,0:T(8,128)(2,1)S(1)} %bitcast.178), kind=kOutput, calls=%fused_computation.121 | convolution fusion | flops 4294967296 | bytes 12582912 | tf_op jit(solution)/shard_map/dot_general | solution.py:82
  84.0 2.7 %collective-permute-start.9 = (bf16[4,32,1024]{2,1,0:T(8,128)(2,1)S(1)}, bf16[4,32,1024]{2,1,0:T(8,128)(2,1)S(1)}, u32[]{:S(2)}, u32[]{:S(2)}) collective-permute-start(bf16[4,32,1024]{2,1,0:T(8,128)(2,1)S(1)} %slice.113), channel_id=1, source_target_pairs={{0,96},{16,112},{32,0},{48,16},{64,32},{80,48},{96,64},{112,80},{1... | collective-permute-start | bytes 786440 | tf_op jit(solution)/shard_map/ppermute | solution.py:12
  86.7 1.2 collective-permute-start.10
  87.9 1.1 collective-permute-done.3
  89.1 2.9 %fusion.49 = bf16[1,4,128,1024]{3,2,1,0:T(8,128)(2,1)S(1)} fusion(bf16[1,4,1024,1024]{3,2,1,0:T(8,128)(2,1)S(1)} %bitcast.169, bf16[4,64,1024]{2,1,0:T(8,128)(2,1)S(1)} %collective-permute-done.4, bf16[4,64,1024]{2,1,0:T(8,128)(2,1)S(1)} %collective-permute-done.3), kind=kOutput, calls=%fused_computation.36 | convolution fusion | flops 1076363264 | bytes 10485760 | tf_op jit(solution)/shard_map/sik,sjk->sij/dot_general | solution.py:76
  92.0 1.3 collective-permute-done.8
  93.3 5.4 %collective-permute-done.10 = bf16[4,64,1024]{2,1,0:T(8,128)(2,1)S(1)} collective-permute-done((bf16[4,64,1024]{2,1,0:T(8,128)(2,1)S(1)}, bf16[4,64,1024]{2,1,0:T(8,128)(2,1)S(1)}, u32[]{:S(2)}, u32[]{:S(2)}) %collective-permute-start.10) | collective-permute-done | bytes 524320 | tf_op jit(solution)/shard_map/ppermute | solution.py:16
  98.7 2.9 %fusion.40 = bf16[1,4,128,1024]{3,2,1,0:T(8,128)(2,1)S(1)} fusion(bf16[1,4,1024,1024]{3,2,1,0:T(8,128)(2,1)S(1)} %bitcast.169, bf16[4,64,1024]{2,1,0:T(8,128)(2,1)S(1)} %collective-permute-done.10, bf16[4,32,1024]{2,1,0:T(8,128)(2,1)S(1)} %collective-permute-done.9, bf16[4,32,1024]{2,1,0:T(8,128)(2,1)S(1)} %collective-permute-done.8), kind=kOutput, calls=%fused_computation.33 | convolution fusion | flops 1077411840 | bytes 10485760 | tf_op jit(solution)/shard_map/sik,sjk->sij/dot_general | solution.py:76
  101.7 2.9 %fusion.43 = bf16[1,4,128,1024]{3,2,1,0:T(8,128)(2,1)S(1)} fusion(bf16[1,4,1024,1024]{3,2,1,0:T(8,128)(2,1)S(1)} %bitcast.169, bf16[4,64,1024]{2,1,0:T(8,128)(2,1)S(1)} %get-tuple-element.43, bf16[4,64,1024]{2,1,0:T(8,128)(2,1)S(1)} %collective-permute-done.7), kind=kOutput, calls=%fused_computation.34 | convolution fusion | flops 1076363264 | bytes 10485760 | tf_op jit(solution)/shard_map/sik,sjk->sij/dot_general | solution.py:76
  104.6 2.9 %fusion.46 = bf16[1,4,128,1024]{3,2,1,0:T(8,128)(2,1)S(1)} fusion(bf16[1,4,1024,1024]{3,2,1,0:T(8,128)(2,1)S(1)} %bitcast.169, bf16[4,64,1024]{2,1,0:T(8,128)(2,1)S(1)} %get-tuple-element.42, bf16[4,64,1024]{2,1,0:T(8,128)(2,1)S(1)} %collective-permute-done.5), kind=kOutput, calls=%fused_computation.35 | convolution fusion | flops 1076363264 | bytes 10485760 | tf_op jit(solution)/shard_map/sik,sjk->sij/dot_general | solution.py:76
  108.4 7.0 %add_convert_fusion = bf16[1024,1024]{1,0:T(8,128)(2,1)S(1)} fusion(f32[1024,1024]{1,0:T(8,128)S(1)} %fusion.100, bf16[1024,2048]{1,0:T(8,128)(2,1)} %get-tuple-element.8, bf16[2048,1024]{1,0:T(8,128)(2,1)S(1)} %bitcast.177), kind=kOutput, calls=%fused_computation.22 | convolution fusion | flops 4297064448 | bytes 14680064 | tf_op jit(solution)/shard_map/dot_general | solution.py:82
  116.7 1.8 gather_fusion.1
  119.3 1.4 copy.20
  121.0 0.9 fusion.64
  122.0 1.7 pad_maximum_fusion.2
  123.7 11.9 %all-to-all-start.1 = ((bf16[16,576,128]{2,1,0:T(8,128)(2,1)}), bf16[16,576,128]{2,1,0:T(8,128)(2,1)S(1)}, u32[]{:S(2)}, u32[]{:S(2)}) async-start(bf16[16,576,128]{2,1,0:T(8,128)(2,1)} %pad_maximum_fusion.2), calls=%async_computation.1 | async-start | bytes 4718592 | tf_op jit(solution)/shard_map/all_to_all | solution.py:107
  135.7 31.1 %all-to-all-done.1 = bf16[16,576,128]{2,1,0:T(8,128)(2,1)S(1)} async-done(((bf16[16,576,128]{2,1,0:T(8,128)(2,1)}), bf16[16,576,128]{2,1,0:T(8,128)(2,1)S(1)}, u32[]{:S(2)}, u32[]{:S(2)}) %all-to-all-start.1) | async-done | bytes 2359328 | tf_op jit(solution)/shard_map/all_to_all | solution.py:107
  167.7 1.3 gather_fusion.3
  169.1 13.3 %all_to_all.19 = f32[16,1,8]{2,1,0:T(1,128)S(1)} all-to-all(f32[16,1,8]{2,1,0:T(1,128)S(1)} %bitcast.182), channel_id=1, replica_groups=mesh['tsink'=8,'mom'=16] {'mom'}, dimensions={0} | all-to-all | bytes 1024 | tf_op jit(solution)/shard_map/all_to_all | solution.py:115
  (66 shorter events, 6.8 us)
Async XLA Ops:
  0.6 36.9 %all-to-all-start = ((bf16[8,128,1024]{2,1,0:T(8,128)(2,1)}), bf16[8,128,1024]{2,1,0:T(8,128)(2,1)}, u32[]{:S(2)}, u32[]{:S(2)}) async-start(bf16[8,128,1024]{2,1,0:T(8,128)(2,1)} %bitcast.179), calls=%async_computation | async-start | bytes 4194304 | tf_op jit(solution)/shard_map/all_to_all | solution.py:26
  6.8 5.8 %copy-start.10 = (s32[4]{0:T(128)S(1)}, s32[4]{0:T(128)}, u32[]{:S(2)}) copy-start(s32[4]{0:T(128)} %param.11) | copy-start | bytes 52
  6.8 5.8 %copy-start.8 = (pred[36]{0:T(512)(128)(4,1)S(1)}, pred[36]{0:T(512)(128)(4,1)}, u32[]{:S(2)}) copy-start(pred[36]{0:T(512)(128)(4,1)} %constant.109) | copy-start | bytes 112
  12.8 9.0 %copy-start.1 = (bf16[1,1,1024,1024]{3,2,1,0:T(8,128)(2,1)S(1)}, bf16[1,1,1024,1024]{3,2,1,0:T(8,128)(2,1)}, u32[]{:S(2)}) copy-start(bf16[1,1,1024,1024]{3,2,1,0:T(8,128)(2,1)} %get-tuple-element.4) | copy-start | bytes 6291460
  12.8 10.0 %copy-start = (bf16[1,1,1024,1024]{3,2,1,0:T(8,128)(2,1)S(1)}, bf16[1,1,1024,1024]{3,2,1,0:T(8,128)(2,1)}, u32[]{:S(2)}) copy-start(bf16[1,1,1024,1024]{3,2,1,0:T(8,128)(2,1)} %get-tuple-element.3) | copy-start | bytes 6291460
  12.9 12.0 %copy-start.2 = (bf16[1,1,1024,1024]{3,2,1,0:T(8,128)(2,1)S(1)}, bf16[1,1,1024,1024]{3,2,1,0:T(8,128)(2,1)}, u32[]{:S(2)}) copy-start(bf16[1,1,1024,1024]{3,2,1,0:T(8,128)(2,1)} %get-tuple-element.5) | copy-start | bytes 6291460
  25.8 17.4 %copy-start.6 = (s32[36]{0:T(128)S(1)}, s32[36]{0:T(128)}, u32[]{:S(2)}) copy-start(s32[36]{0:T(128)} %constant.124) | copy-start | bytes 436
  25.8 17.4 %copy-start.7 = (s32[36]{0:T(128)S(1)}, s32[36]{0:T(128)}, u32[]{:S(2)}) copy-start(s32[36]{0:T(128)} %constant.125) | copy-start | bytes 436
  39.8 26.1 %collective-permute-start.2 = (bf16[4,128,1024]{2,1,0:T(8,128)(2,1)S(1)}, bf16[4,128,1024]{2,1,0:T(8,128)(2,1)S(1)}, u32[]{:S(2)}, u32[]{:S(2)}) collective-permute-start(bf16[4,128,1024]{2,1,0:T(8,128)(2,1)S(1)} %gather_fusion), channel_id=1, source_target_pairs={{0,96},{16,112},{32,0},{48,16},{64,32},{80,48},{96,64},{112,80},{1... | collective-permute-start | bytes 3145736 | tf_op jit(solution)/shard_map/ppermute | solution.py:12
  39.8 23.2 %collective-permute-start = (bf16[4,128,1024]{2,1,0:T(8,128)(2,1)S(1)}, bf16[4,128,1024]{2,1,0:T(8,128)(2,1)S(1)}, u32[]{:S(2)}, u32[]{:S(2)}) collective-permute-start(bf16[4,128,1024]{2,1,0:T(8,128)(2,1)S(1)} %gather_fusion), channel_id=1, source_target_pairs={{0,16},{16,0},{32,48},{48,32},{64,80},{80,64},{96,112},{112,96},{1... | collective-permute-start | bytes 3145736 | tf_op jit(solution)/shard_map/ppermute | solution.py:16
  41.9 24.1 %collective-permute-start.1 = (bf16[4,128,1024]{2,1,0:T(8,128)(2,1)S(1)}, bf16[4,128,1024]{2,1,0:T(8,128)(2,1)S(1)}, u32[]{:S(2)}, u32[]{:S(2)}) collective-permute-start(bf16[4,128,1024]{2,1,0:T(8,128)(2,1)S(1)} %gather_fusion), channel_id=1, source_target_pairs={{0,32},{16,48},{32,64},{48,80},{64,96},{80,112},{96,0},{112,16},{1... | collective-permute-start | bytes 3145736 | tf_op jit(solution)/shard_map/ppermute | solution.py:12
  43.3 24.8 %slice-start = ((s8[8388608]{0:T(1024)(128)(4,1)}), s8[4194304]{0:T(1024)(128)(4,1)S(1)}, s32[]{:S(2)}) async-start(s8[8388608]{0:T(1024)(128)(4,1)} %bitcast.168), calls=%async_computation.3 | async-start | bytes 8388608
  44.3 23.8 %slice-start.1 = ((s8[8388608]{0:T(1024)(128)(4,1)}), s8[4194304]{0:T(1024)(128)(4,1)S(1)}, s32[]{:S(2)}) async-start(s8[8388608]{0:T(1024)(128)(4,1)} %bitcast.168), calls=%async_computation.4 | async-start | bytes 8388608
  63.1 20.7 %collective-permute-start.5 = (bf16[4,64,1024]{2,1,0:T(8,128)(2,1)S(1)}, bf16[4,64,1024]{2,1,0:T(8,128)(2,1)S(1)}, u32[]{:S(2)}, u32[]{:S(2)}) collective-permute-start(bf16[4,64,1024]{2,1,0:T(8,128)(2,1)S(1)} %slice.108), channel_id=1, source_target_pairs={{0,32},{16,48},{32,64},{48,80},{64,96},{80,112},{96,0},{112,16},{1... | collective-permute-start | bytes 1572872 | tf_op jit(solution)/shard_map/ppermute | solution.py:12
  64.3 19.7 %collective-permute-start.7 = (bf16[4,64,1024]{2,1,0:T(8,128)(2,1)S(1)}, bf16[4,64,1024]{2,1,0:T(8,128)(2,1)S(1)}, u32[]{:S(2)}, u32[]{:S(2)}) collective-permute-start(bf16[4,64,1024]{2,1,0:T(8,128)(2,1)S(1)} %slice.108), channel_id=1, source_target_pairs={{0,96},{16,112},{32,0},{48,16},{64,32},{80,48},{96,64},{112,80},{1... | collective-permute-start | bytes 1572872 | tf_op jit(solution)/shard_map/ppermute | solution.py:12
  65.9 20.8 %collective-permute-start.4 = (bf16[4,64,1024]{2,1,0:T(8,128)(2,1)S(1)}, bf16[4,64,1024]{2,1,0:T(8,128)(2,1)S(1)}, u32[]{:S(2)}, u32[]{:S(2)}) collective-permute-start(bf16[4,64,1024]{2,1,0:T(8,128)(2,1)S(1)} %get-tuple-element.45), channel_id=1, source_target_pairs={{0,96},{16,112},{32,0},{48,16},{64,32},{80,48},{96,64},{112,80},{1... | collective-permute-start | bytes 1572872 | tf_op jit(solution)/shard_map/ppermute | solution.py:12
  66.2 35.4 %collective-permute-start.6 = (bf16[2,4,64,1024]{3,2,1,0:T(8,128)(2,1)S(1)}, bf16[2,4,64,1024]{3,2,1,0:T(8,128)(2,1)S(1)}, u32[]{:S(2)}, u32[]{:S(2)}) collective-permute-start(bf16[2,4,64,1024]{3,2,1,0:T(8,128)(2,1)S(1)} %pad_maximum_fusion.3), channel_id=1, source_target_pairs={{0,16},{16,0},{32,48},{48,32},{64,80},{80,64},{96,112},{112,96},{1... | collective-permute-start | bytes 3145736 | tf_op jit(solution)/shard_map/ppermute | solution.py:16
  67.7 21.3 %collective-permute-start.3 = (bf16[4,64,1024]{2,1,0:T(8,128)(2,1)S(1)}, bf16[4,64,1024]{2,1,0:T(8,128)(2,1)S(1)}, u32[]{:S(2)}, u32[]{:S(2)}) collective-permute-start(bf16[4,64,1024]{2,1,0:T(8,128)(2,1)S(1)} %get-tuple-element.40), channel_id=1, source_target_pairs={{0,32},{16,48},{32,64},{48,80},{64,96},{80,112},{96,0},{112,16},{1... | collective-permute-start | bytes 1572872 | tf_op jit(solution)/shard_map/ppermute | solution.py:12
  83.9 9.4 %collective-permute-start.8 = (bf16[4,32,1024]{2,1,0:T(8,128)(2,1)S(1)}, bf16[4,32,1024]{2,1,0:T(8,128)(2,1)S(1)}, u32[]{:S(2)}, u32[]{:S(2)}) collective-permute-start(bf16[4,32,1024]{2,1,0:T(8,128)(2,1)S(1)} %slice.112), channel_id=1, source_target_pairs={{0,32},{16,48},{32,64},{48,80},{64,96},{80,112},{96,0},{112,16},{1... | collective-permute-start | bytes 786440 | tf_op jit(solution)/shard_map/ppermute | solution.py:12
  84.0 9.3 %collective-permute-start.9 = (bf16[4,32,1024]{2,1,0:T(8,128)(2,1)S(1)}, bf16[4,32,1024]{2,1,0:T(8,128)(2,1)S(1)}, u32[]{:S(2)}, u32[]{:S(2)}) collective-permute-start(bf16[4,32,1024]{2,1,0:T(8,128)(2,1)S(1)} %slice.113), channel_id=1, source_target_pairs={{0,96},{16,112},{32,0},{48,16},{64,32},{80,48},{96,64},{112,80},{1... | collective-permute-start | bytes 786440 | tf_op jit(solution)/shard_map/ppermute | solution.py:12
  86.7 12.0 %collective-permute-start.10 = (bf16[4,64,1024]{2,1,0:T(8,128)(2,1)S(1)}, bf16[4,64,1024]{2,1,0:T(8,128)(2,1)S(1)}, u32[]{:S(2)}, u32[]{:S(2)}) collective-permute-start(bf16[4,64,1024]{2,1,0:T(8,128)(2,1)S(1)} %collective-permute-done.4), channel_id=1, source_target_pairs={{0,16},{16,0},{32,48},{48,32},{64,80},{80,64},{96,112},{112,96},{1... | collective-permute-start | bytes 1572872 | tf_op jit(solution)/shard_map/ppermute | solution.py:16
  115.4 1.4 copy-start.5
  119.3 1.7 copy-start.3
  120.8 1.3 copy-start.4
  122.0 13.6 %copy-start.9 = (s32[128,2]{0,1:T(2,128)S(1)}, s32[128,2]{0,1:T(2,128)}, u32[]{:S(2)}) copy-start(s32[128,2]{0,1:T(2,128)} %param.12) | copy-start | bytes 3076
  123.7 43.1 %all-to-all-start.1 = ((bf16[16,576,128]{2,1,0:T(8,128)(2,1)}), bf16[16,576,128]{2,1,0:T(8,128)(2,1)S(1)}, u32[]{:S(2)}, u32[]{:S(2)}) async-start(bf16[16,576,128]{2,1,0:T(8,128)(2,1)} %pad_maximum_fusion.2), calls=%async_computation.1 | async-start | bytes 4718592 | tf_op jit(solution)/shard_map/all_to_all | solution.py:107
